TPU v7x, 256 devices: a whole 4x4x8 slice. The times are simulated.
256 devices in a mesh: gx: 16 (over z_lo, x, core), gy: 16 (over z_hi, y).
Axes of the slice: x: 4, y: 4, z: 8 (z_hi: 4, z_lo: 2; z = z_hi * 2 + z_lo), core: 2. Of those that a mesh axis runs over, the one named last changes fastest.
Arguments:
- species_field: float32 [4, 1024, 256, 256], P(None, 'gx', 'gy'), may hold values from -400 to 400
- initial: float32 [1024, 128], replicated, may hold values from -6 to 6
Outputs:
- factor: float32 [1024, 128], replicated
- gram_two: float32 [256, 256], replicated
All inputs are finite; a program needn't handle non-finite values.
Results may differ from a plain program's by a relative error of at most 0.0002.
Values sent between devices are 32-bit elements; how exact they have to be, the bound alone decides.
No kernel may reach another device: no remote copies, remote signals or barrier semaphores. Data moves between devices by JAX's collectives and lax.ppermute only.
A program may use at most 128 MiB of HBM per device.

v0:
```python
import math

import jax
import jax.numpy as jnp
from jax import lax
from jax.sharding import PartitionSpec as P

S = 4
NY = 256
NZ = 256
R = 128
SWEEPS = 3


def body(species_field, initial):
    highest = lax.Precision.HIGHEST
    regrouped = lax.all_to_all(species_field, "gx", split_axis=3, concat_axis=1, tiled=True)
    species, rows_x, cols_y, slab_z = regrouped.shape
    fibers = regrouped.reshape(species, rows_x, cols_y * slab_z)
    scale_one = 1.0 / (S * NY * NZ)
    basis = initial
    gram_one = lax.psum(
        jnp.einsum("sxc,swc->xw", fibers, fibers, precision=highest) * scale_one, ("gx", "gy")
    )
    for sweep_index in range(SWEEPS):
        wide = jnp.dot(gram_one, basis, precision=highest, preferred_element_type=jnp.float32)
        square = jnp.dot(wide.T, wide, precision=highest, preferred_element_type=jnp.float32)
        factor_low = jnp.linalg.cholesky(square)
        basis = jax.scipy.linalg.solve_triangular(factor_low, wide.T, lower=True).T
    core_tensor = jnp.einsum("xr,sxc->src", basis, fibers, precision=highest)
    core_blocks = core_tensor.reshape(species, R, cols_y, slab_z)
    blocks = lax.all_to_all(core_blocks, "gy", split_axis=1, concat_axis=2, tiled=True)
    second_part = jnp.einsum("sryz,srwz->yw", blocks, blocks, precision=highest) / (S * R * NZ)
    gram_two = lax.psum(second_part, ("gx", "gy"))
    return (basis * math.sqrt(rows_x), gram_two)


def solution(mesh):
    placed = (P(None, "gx", "gy", None), P())
    return jax.shard_map(body, mesh=mesh, in_specs=placed, out_specs=(P(), P()), check_vma=False)
```

profile of v0, /device:TPU:6, one launch (start us, length us, event | category | flops | bytes accessed | tf_op | source)
XLA Modules:
  0.0 817.2 jit_solution(10671262008300448773)
XLA Ops:
  7.2 0.0 copy-start
  7.2 0.0 all-reduce.3.cloned.1.call-start
  7.2 9.2 %copy.33 = f32[4,64,16,256]{1,2,0,3:T(8,128)} copy(f32[4,64,16,256]{3,2,1,0:T(8,128)} %param.5) | data formatting | bytes 8388608 | tf_op args[0]
  16.4 13.3 %reshape.24 = f32[16,1,65536]{2,1,0:T(1,128)} reshape(f32[256,4,16,64]{3,2,1,0:T(8,128)} %bitcast.87) | data formatting | bytes 8388608
  29.7 54.5 %all_to_all.33 = f32[16,1,65536]{2,1,0:T(1,128)} all-to-all(f32[16,1,65536]{2,1,0:T(1,128)} %reshape.24), channel_id=1, replica_groups=mesh['gx'=16,'gy'=16] {'gx'}, dimensions={0} | all-to-all | bytes 8388608 | tf_op jit(solution)/shard_map/all_to_all | solution.py:17
  84.2 0.5 broadcast.39
  84.7 13.7 %reduce.4 = f32[16,65536]{1,0:T(8,128)} reduce(f32[16,1,65536]{2,1,0:T(1,128)} %all_to_all.33, f32[]{:T(128)} %broadcast.39), dimensions={1}, to_apply=%all_to_all.24.reduce_sub_computation | reduce | bytes 8388612 | tf_op jit(solution)/shard_map/all_to_all | solution.py:17
  98.4 6.9 reshape.25
  105.3 11.4 %copy.35 = f32[4,16,64,16,16]{2,1,4,3,0:T(8,128)} copy(f32[4,16,64,16,16]{2,3,0,4,1:T(8,128)} %bitcast.88) | data formatting | bytes 8388608 | tf_op jit(solution)/shard_map/all_to_all | solution.py:17
  116.8 7.6 reshape.19
  124.4 17.8 %bitcast_multiply_fusion = f32[1024,1024]{1,0:T(8,128)} fusion(f32[4,1024,256]{1,2,0:T(8,128)} %reshape.19), kind=kOutput, calls=%fused_computation | convolution fusion | flops 12885950464 | bytes 8388608 | tf_op jit(solution)/shard_map/sxc,swc->xw/dot_general | solution.py:23
  142.2 0.0 all-reduce.3.cloned.1.call-update
  142.2 0.0 all-reduce.5.cloned.1.call-start
  142.2 271.7 %all-reduce.3.cloned.1.call-done = f32[1024,1024]{1,0:T(8,128)} async-done(((f32[1024,1024]{1,0:T(8,128)}), f32[1024,1024]{1,0:T(8,128)}) %all-reduce.3.cloned.1.call-update) | async-done | bytes 4194320 | tf_op jit(solution)/shard_map/psum | solution.py:22
  414.0 0.0 copy-done
  414.0 5.6 fusion.21
  419.6 1.0 fusion.22
  420.6 0.1 copy.38
  420.7 11.7 %cholesky.59 = f32[128,128]{1,0:T(8,128)S(1)} custom-call(f32[128,128]{1,0:T(8,128)S(1)} %fusion.16), custom_call_target="Cholesky" | custom-call | tf_op jit(solution)/shard_map/jit(cholesky)/cholesky | solution.py:28
  432.4 0.6 compare_reduce_fusion.2
  433.1 0.7 fusion.8
  433.7 9.8 %custom-call.7 = f32[1,128,128]{1,2,0:T(8,128)S(1)} custom-call(f32[1,128,128]{2,1,0:T(8,128)S(1)} %fusion.8), custom_call_target="InvertDiagBlocksLowerTriangular" | custom-call | tf_op jit(solution)/shard_map/jit(_solve_triangular)/triangular_solve | solution.py:29
  443.6 0.6 fusion.6
  444.2 5.4 fusion.23
  449.6 1.0 fusion.24
  450.6 0.1 copy.39
  450.7 11.7 %cholesky.70 = f32[128,128]{1,0:T(8,128)S(1)} custom-call(f32[128,128]{1,0:T(8,128)S(1)} %fusion.14), custom_call_target="Cholesky" | custom-call | tf_op jit(solution)/shard_map/jit(cholesky)/cholesky | solution.py:28
  462.5 0.6 compare_reduce_fusion.1
  463.1 0.7 fusion.9
  463.8 9.8 %custom-call.8 = f32[1,128,128]{1,2,0:T(8,128)S(1)} custom-call(f32[1,128,128]{2,1,0:T(8,128)S(1)} %fusion.9), custom_call_target="InvertDiagBlocksLowerTriangular" | custom-call | tf_op jit(solution)/shard_map/jit(_solve_triangular)/triangular_solve | solution.py:29
  473.6 0.6 fusion.4
  474.2 5.4 fusion.25
  479.7 1.0 fusion.26
  480.7 0.1 copy.40
  480.8 11.7 %cholesky.81 = f32[128,128]{1,0:T(8,128)S(1)} custom-call(f32[128,128]{1,0:T(8,128)S(1)} %fusion.12), custom_call_target="Cholesky" | custom-call | tf_op jit(solution)/shard_map/jit(cholesky)/cholesky | solution.py:28
  492.6 0.6 compare_reduce_fusion
  493.2 0.7 fusion.10
  493.9 9.8 %custom-call.9 = f32[1,128,128]{1,2,0:T(8,128)S(1)} custom-call(f32[1,128,128]{2,1,0:T(8,128)S(1)} %fusion.10), custom_call_target="InvertDiagBlocksLowerTriangular" | custom-call | tf_op jit(solution)/shard_map/jit(_solve_triangular)/triangular_solve | solution.py:29
  503.7 0.6 fusion.2
  504.3 6.5 convolution_bitcast_fusion
  510.9 0.2 copy.42
  511.1 4.6 copy.43
  515.7 3.5 reshape.26
  519.2 20.9 %all_to_all.34 = f32[16,1,8192]{2,1,0:T(1,128)S(1)} all-to-all(f32[16,1,8192]{2,1,0:T(1,128)S(1)} %reshape.26), channel_id=1, replica_groups=mesh['gx'=16,'gy'=16] {'gy'}, dimensions={0} | all-to-all | bytes 1048576 | tf_op jit(solution)/shard_map/all_to_all | solution.py:32
  540.2 1.9 reduce.5
  542.1 2.8 reshape.27
  544.8 5.6 copy.45
  550.4 3.5 all_to_all.30
  553.9 1.7 fusion
  555.6 0.0 all-reduce.5.cloned.1.call-update
  555.7 1.0 copy.46
  556.7 251.6 %all-reduce.5.cloned.1.call-done = f32[256,256]{1,0:T(8,128)} async-done(((f32[256,256]{1,0:T(8,128)}), f32[256,256]{1,0:T(8,128)}) %all-reduce.5.cloned.1.call-update) | async-done | bytes 262160 | tf_op jit(solution)/shard_map/psum | solution.py:34
  808.2 1.7 copy.55
  (7 shorter events, 0.2 us)
Async XLA Ops:
  7.2 406.8 %copy-start = (f32[1024,128]{1,0:T(8,128)S(1)}, f32[1024,128]{1,0:T(8,128)}, u32[]{:S(2)}) copy-start(f32[1024,128]{1,0:T(8,128)} %param.6) | copy-start | bytes 1572868
  7.2 406.8 %all-reduce.3.cloned.1.call-start = ((), (), s32[]{:S(2)}) async-start(), calls=%async_computation.2 | async-start | bytes 8388608 | tf_op jit(solution)/shard_map/psum | solution.py:22
  142.2 666.0 %all-reduce.5.cloned.1.call-start = ((), (), s32[]{:S(2)}) async-start(), calls=%async_computation.3 | async-start | bytes 524288 | tf_op jit(solution)/shard_map/psum | solution.py:34
Sparse Core Ops, SparseCore 0:
  142.3 271.5 all-reduce.2
  555.7 252.4 all-reduce.4
where the time goes:
time: 826 us; the launch traced here: 817 us
  waiting for transfers between devices  523 us (63%)
  other arithmetic  84.2 us (10%)
  blocking collectives  75.4 us (9%)
  local copies, waits for them, and re-layouts  72 us (9%)
  matrix products  47.4 us (6%)
  between operations  14.7 us (2%)
    psum x1, waiting for transfers between devices, body(): lax.psum(jnp.einsum('sxc,swc->xw', fibers, fibers, precision=highest) * s...  272 us
    psum x1, waiting for transfers between devices, body(): gram_two = lax.psum(second_part, ('gx', 'gy'))  252 us
    all_to_all x1, blocking collectives, body(): lax.all_to_all(species_field, 'gx', split_axis=3, concat_axis=1, tiled=True)  54.5 us
    unnamed x9, local copies, waits for them, and re-layouts  38.3 us
    another operation x9, other arithmetic, body(): factor_low = jnp.linalg.cholesky(square)  37.2 us
    another operation x6, other arithmetic, body(): basis = jax.scipy.linalg.solve_triangular(factor_low, wide.T, lower=True).T  31.4 us
    all_to_all x1, blocking collectives, body(): lax.all_to_all(core_blocks, 'gy', split_axis=1, concat_axis=2, tiled=True)  20.9 us
    dot_general x1, matrix products, body(): jnp.einsum('sxc,swc->xw', fibers, fibers, precision=highest) * scale_one  17.8 us
  transfers between devices with their start and end apart: 2, of which 2 were waited for; matrix products, arithmetic and copies ran while one was open for 0% of the time, Pallas kernels for 0%

commit v1 on v0

--- a/solution.py
+++ b/solution.py
@@ -10,6 +10,14 @@
 NZ = 256
 R = 128
 SWEEPS = 3
+
+
+def butterfly_sum(value, axis, size):
+    stride = 1
+    while stride < size:
+        value = value + lax.ppermute(value, axis, [(i, i ^ stride) for i in range(size)])
+        stride *= 2
+    return value
 
 
 def body(species_field, initial):
@@ -31,7 +39,8 @@
     core_blocks = core_tensor.reshape(species, R, cols_y, slab_z)
     blocks = lax.all_to_all(core_blocks, "gy", split_axis=1, concat_axis=2, tiled=True)
     second_part = jnp.einsum("sryz,srwz->yw", blocks, blocks, precision=highest) / (S * R * NZ)
-    gram_two = lax.psum(second_part, ("gx", "gy"))
+    gram_two = butterfly_sum(second_part, "gx", lax.axis_size("gx"))
+    gram_two = butterfly_sum(gram_two, "gy", lax.axis_size("gy"))
     return (basis * math.sqrt(rows_x), gram_two)
 
 

time: 826 us -> 644 us (0.78)
  waiting for transfers between devices: 523 us -> 330 us
  starting transfers between devices: 0.08 us -> 13.2 us
    psum x1 -> x0, waiting for transfers between devices: 252 us -> none  [body(): gram_two = lax.psum(second_part, ('gx', 'gy'))]
    ppermute x0 -> x8, waiting for transfers between devices: none -> 57.8 us  [butterfly_sum(): lax.ppermute(value, axis, [(i, i ^ stride) for i in range(size)])]
    ppermute x0 -> x8, starting transfers between devices: none -> 13.1 us  [butterfly_sum(): lax.ppermute(value, axis, [(i, i ^ stride) for i in range(size)])]
    unnamed x9 -> x8, local copies, waits for them, and re-layouts: 38.3 us -> 36.6 us
  transfers between devices with their start and end apart: 2 -> 9, of which waited for: 2 -> 9; matrix products, arithmetic and copies ran while one was open for 0% -> 0% of each run, Pallas kernels for 0% -> 0%
where the time goes in v1:
time: 644 us; the launch traced here: 635 us
  waiting for transfers between devices  330 us (51%)
  other arithmetic  85.2 us (13%)
  blocking collectives  75.4 us (12%)
  local copies, waits for them, and re-layouts  70.3 us (11%)
  matrix products  46.7 us (7%)
  between operations  14.7 us (2%)
  starting transfers between devices  13.2 us (2%)
    psum x1, waiting for transfers between devices, body(): lax.psum(jnp.einsum('sxc,swc->xw', fibers, fibers, precision=highest) * s...  272 us
    ppermute x8, waiting for transfers between devices, butterfly_sum(): lax.ppermute(value, axis, [(i, i ^ stride) for i in range(size)])  57.8 us
    all_to_all x1, blocking collectives, body(): lax.all_to_all(species_field, 'gx', split_axis=3, concat_axis=1, tiled=True)  54.5 us
    another operation x9, other arithmetic, body(): factor_low = jnp.linalg.cholesky(square)  37.2 us
    unnamed x8, local copies, waits for them, and re-layouts  36.6 us
    another operation x6, other arithmetic, body(): basis = jax.scipy.linalg.solve_triangular(factor_low, wide.T, lower=True).T  31.4 us
    all_to_all x1, blocking collectives, body(): lax.all_to_all(core_blocks, 'gy', split_axis=1, concat_axis=2, tiled=True)  20.9 us
    dot_general x1, matrix products, body(): jnp.einsum('sxc,swc->xw', fibers, fibers, precision=highest) * scale_one  17.8 us
  transfers between devices with their start and end apart: 9, of which 9 were waited for; matrix products, arithmetic and copies ran while one was open for 0% of the time, Pallas kernels for 0%

profile of v1, /device:TPU:6, one launch (start us, length us, event | category | flops | bytes accessed | tf_op | source)
XLA Modules:
  0.0 635.2 jit_solution(13289644270254414132)
XLA Ops:
  7.2 0.0 all-reduce.2.cloned.1.call-start
  7.2 9.2 %copy.33 = f32[4,64,16,256]{1,2,0,3:T(8,128)} copy(f32[4,64,16,256]{3,2,1,0:T(8,128)} %param.5) | data formatting | bytes 8388608 | tf_op args[0]
  16.4 13.3 %reshape.24 = f32[16,1,65536]{2,1,0:T(1,128)} reshape(f32[256,4,16,64]{3,2,1,0:T(8,128)} %bitcast.87) | data formatting | bytes 8388608
  29.7 54.5 %all_to_all.33 = f32[16,1,65536]{2,1,0:T(1,128)} all-to-all(f32[16,1,65536]{2,1,0:T(1,128)} %reshape.24), channel_id=1, replica_groups=mesh['gx'=16,'gy'=16] {'gx'}, dimensions={0} | all-to-all | bytes 8388608 | tf_op jit(solution)/shard_map/all_to_all | solution.py:25
  84.2 0.5 broadcast.39
  84.7 13.7 %reduce.4 = f32[16,65536]{1,0:T(8,128)} reduce(f32[16,1,65536]{2,1,0:T(1,128)} %all_to_all.33, f32[]{:T(128)} %broadcast.39), dimensions={1}, to_apply=%all_to_all.24.reduce_sub_computation | reduce | bytes 8388612 | tf_op jit(solution)/shard_map/all_to_all | solution.py:25
  98.4 6.9 %reshape.25 = f32[256,4,16,64]{3,2,1,0:T(8,128)} reshape(f32[16,65536]{1,0:T(8,128)} %reduce.4) | data formatting | bytes 8388608
  105.3 11.4 %copy.35 = f32[4,16,64,16,16]{2,1,4,3,0:T(8,128)} copy(f32[4,16,64,16,16]{2,3,0,4,1:T(8,128)} %bitcast.88) | data formatting | bytes 8388608 | tf_op jit(solution)/shard_map/all_to_all | solution.py:25
  116.8 7.6 %reshape.19 = f32[4,1024,256]{1,2,0:T(8,128)} reshape(f32[4,16,64,16,16]{2,1,4,3,0:T(8,128)} %copy.35) | data formatting | bytes 8388608 | tf_op jit(solution)/shard_map/reshape | solution.py:27
  124.4 17.8 %bitcast_multiply_fusion = f32[1024,1024]{1,0:T(8,128)} fusion(f32[4,1024,256]{1,2,0:T(8,128)} %reshape.19), kind=kOutput, calls=%fused_computation | convolution fusion | flops 12885950464 | bytes 8388608 | tf_op jit(solution)/shard_map/sxc,swc->xw/dot_general | solution.py:31
  142.2 0.0 all-reduce.2.cloned.1.call-update
  142.2 271.8 %all-reduce.2.cloned.1.call-done = f32[1024,1024]{1,0:T(8,128)} async-done(((f32[1024,1024]{1,0:T(8,128)}), f32[1024,1024]{1,0:T(8,128)}) %all-reduce.2.cloned.1.call-update) | async-done | bytes 4194320 | tf_op jit(solution)/shard_map/psum | solution.py:30
  414.0 5.6 fusion.21
  419.6 1.0 fusion.22
  420.6 0.1 copy.38
  420.7 11.7 %cholesky.59 = f32[128,128]{1,0:T(8,128)S(1)} custom-call(f32[128,128]{1,0:T(8,128)S(1)} %fusion.16), custom_call_target="Cholesky" | custom-call | tf_op jit(solution)/shard_map/jit(cholesky)/cholesky | solution.py:36
  432.5 0.6 compare_reduce_fusion.2
  433.1 0.7 fusion.8
  433.8 9.8 %custom-call.7 = f32[1,128,128]{1,2,0:T(8,128)S(1)} custom-call(f32[1,128,128]{2,1,0:T(8,128)S(1)} %fusion.8), custom_call_target="InvertDiagBlocksLowerTriangular" | custom-call | tf_op jit(solution)/shard_map/jit(_solve_triangular)/triangular_solve | solution.py:37
  443.6 0.6 fusion.6
  444.2 5.4 fusion.23
  449.6 1.0 fusion.24
  450.6 0.1 copy.39
  450.8 11.7 %cholesky.70 = f32[128,128]{1,0:T(8,128)S(1)} custom-call(f32[128,128]{1,0:T(8,128)S(1)} %fusion.14), custom_call_target="Cholesky" | custom-call | tf_op jit(solution)/shard_map/jit(cholesky)/cholesky | solution.py:36
  462.5 0.6 compare_reduce_fusion.1
  463.1 0.7 fusion.9
  463.8 9.8 %custom-call.8 = f32[1,128,128]{1,2,0:T(8,128)S(1)} custom-call(f32[1,128,128]{2,1,0:T(8,128)S(1)} %fusion.9), custom_call_target="InvertDiagBlocksLowerTriangular" | custom-call | tf_op jit(solution)/shard_map/jit(_solve_triangular)/triangular_solve | solution.py:37
  473.6 0.6 fusion.4
  474.3 5.4 fusion.25
  479.7 1.0 fusion.26
  480.7 0.1 copy.40
  480.8 11.7 %cholesky.81 = f32[128,128]{1,0:T(8,128)S(1)} custom-call(f32[128,128]{1,0:T(8,128)S(1)} %fusion.12), custom_call_target="Cholesky" | custom-call | tf_op jit(solution)/shard_map/jit(cholesky)/cholesky | solution.py:36
  492.6 0.6 compare_reduce_fusion
  493.2 0.7 fusion.10
  493.9 9.8 %custom-call.9 = f32[1,128,128]{1,2,0:T(8,128)S(1)} custom-call(f32[1,128,128]{2,1,0:T(8,128)S(1)} %fusion.10), custom_call_target="InvertDiagBlocksLowerTriangular" | custom-call | tf_op jit(solution)/shard_map/jit(_solve_triangular)/triangular_solve | solution.py:37
  503.7 0.6 fusion.2
  504.4 6.5 %convolution_bitcast_fusion = f32[4,128,256]{2,1,0:T(8,128)S(1)} fusion(f32[4,1024,256]{1,2,0:T(8,128)} %reshape.19, f32[128,1024]{1,0:T(8,128)S(1)} %fusion.2), kind=kOutput, calls=%fused_computation.1 | convolution fusion | flops 1610612736 | bytes 5242880 | tf_op jit(solution)/shard_map/xr,sxc->src/dot_general | solution.py:38
  510.9 0.2 copy.42
  511.1 4.6 copy.43
  515.8 3.5 reshape.26
  519.3 20.9 %all_to_all.34 = f32[16,1,8192]{2,1,0:T(1,128)S(1)} all-to-all(f32[16,1,8192]{2,1,0:T(1,128)S(1)} %reshape.26), channel_id=1, replica_groups=mesh['gx'=16,'gy'=16] {'gy'}, dimensions={0} | all-to-all | bytes 1048576 | tf_op jit(solution)/shard_map/all_to_all | solution.py:40
  540.2 1.9 reduce.5
  542.1 2.8 reshape.27
  544.8 5.6 copy.45
  550.4 3.5 all_to_all.30
  553.9 1.0 fusion
  554.9 0.1 collective-permute-start
  555.0 1.5 collective-permute-done
  556.6 1.0 collective-permute-start.1
  557.5 7.5 %collective-permute-done.1 = f32[256,256]{1,0:T(8,128)S(1)} collective-permute-done((f32[256,256]{1,0:T(8,128)S(1)}, f32[256,256]{1,0:T(8,128)S(1)}, u32[]{:S(2)}, u32[]{:S(2)}) %collective-permute-start.1) | collective-permute-done | bytes 262176 | tf_op jit(solution)/shard_map/ppermute | solution.py:18
  565.0 4.4 collective-permute-start.2
  569.4 6.0 collective-permute-done.2
  575.5 3.1 collective-permute-start.3
  578.6 4.9 collective-permute-done.3
  583.5 0.7 collective-permute-start.4
  584.1 6.8 %collective-permute-done.4 = f32[256,256]{1,0:T(8,128)S(1)} collective-permute-done((f32[256,256]{1,0:T(8,128)S(1)}, f32[256,256]{1,0:T(8,128)S(1)}, u32[]{:S(2)}, u32[]{:S(2)}) %collective-permute-start.4) | collective-permute-done | bytes 262176 | tf_op jit(solution)/shard_map/ppermute | solution.py:18
  591.0 0.6 collective-permute-start.5
  591.6 7.4 %collective-permute-done.5 = f32[256,256]{1,0:T(8,128)S(1)} collective-permute-done((f32[256,256]{1,0:T(8,128)S(1)}, f32[256,256]{1,0:T(8,128)S(1)}, u32[]{:S(2)}, u32[]{:S(2)}) %collective-permute-start.5) | collective-permute-done | bytes 262176 | tf_op jit(solution)/shard_map/ppermute | solution.py:18
  599.0 0.7 collective-permute-start.6
  599.7 15.1 %collective-permute-done.6 = f32[256,256]{1,0:T(8,128)S(1)} collective-permute-done((f32[256,256]{1,0:T(8,128)S(1)}, f32[256,256]{1,0:T(8,128)S(1)}, u32[]{:S(2)}, u32[]{:S(2)}) %collective-permute-start.6) | collective-permute-done | bytes 262176 | tf_op jit(solution)/shard_map/ppermute | solution.py:18
  614.8 2.7 collective-permute-start.7
  617.6 1.0 copy.46
  618.6 8.7 %collective-permute-done.7 = f32[256,256]{1,0:T(8,128)S(1)} collective-permute-done((f32[256,256]{1,0:T(8,128)S(1)}, f32[256,256]{1,0:T(8,128)S(1)}, u32[]{:S(2)}, u32[]{:S(2)}) %collective-permute-start.7) | collective-permute-done | bytes 262176 | tf_op jit(solution)/shard_map/ppermute | solution.py:18
  627.2 0.7 add.42
  (16 shorter events, 0.4 us)
Async XLA Ops:
  7.2 406.8 %copy-start = (f32[1024,128]{1,0:T(8,128)S(1)}, f32[1024,128]{1,0:T(8,128)}, u32[]{:S(2)}) copy-start(f32[1024,128]{1,0:T(8,128)} %param.6) | copy-start | bytes 1572868
  7.2 406.8 %all-reduce.2.cloned.1.call-start = ((), (), s32[]{:S(2)}) async-start(), calls=%async_computation.2 | async-start | bytes 8388608 | tf_op jit(solution)/shard_map/psum | solution.py:30
  554.9 1.6 collective-permute-start
  556.6 8.4 %collective-permute-start.1 = (f32[256,256]{1,0:T(8,128)S(1)}, f32[256,256]{1,0:T(8,128)S(1)}, u32[]{:S(2)}, u32[]{:S(2)}) collective-permute-start(f32[256,256]{1,0:T(8,128)S(1)} %add.35), channel_id=1, source_target_pairs={{0,32},{16,48},{32,0},{48,16},{64,96},{80,112},{96,64},{112,80},{1... | collective-permute-start | bytes 786440 | tf_op jit(solution)/shard_map/ppermute | solution.py:18
  565.0 10.4 %collective-permute-start.2 = (f32[256,256]{1,0:T(8,128)S(1)}, f32[256,256]{1,0:T(8,128)S(1)}, u32[]{:S(2)}, u32[]{:S(2)}) collective-permute-start(f32[256,256]{1,0:T(8,128)S(1)} %add.36), channel_id=1, source_target_pairs={{0,64},{16,80},{32,96},{48,112},{64,0},{80,16},{96,32},{112,48},{1... | collective-permute-start | bytes 786440 | tf_op jit(solution)/shard_map/ppermute | solution.py:18
  575.5 8.0 %collective-permute-start.3 = (f32[256,256]{1,0:T(8,128)S(1)}, f32[256,256]{1,0:T(8,128)S(1)}, u32[]{:S(2)}, u32[]{:S(2)}) collective-permute-start(f32[256,256]{1,0:T(8,128)S(1)} %add.37), channel_id=1, source_target_pairs={{0,128},{16,144},{32,160},{48,176},{64,192},{80,208},{96,224},{112... | collective-permute-start | bytes 786440 | tf_op jit(solution)/shard_map/ppermute | solution.py:18
  583.5 7.5 %collective-permute-start.4 = (f32[256,256]{1,0:T(8,128)S(1)}, f32[256,256]{1,0:T(8,128)S(1)}, u32[]{:S(2)}, u32[]{:S(2)}) collective-permute-start(f32[256,256]{1,0:T(8,128)S(1)} %add.38), channel_id=1, source_target_pairs={{0,1},{1,0},{2,3},{3,2},{4,5},{5,4},{6,7},{7,6},{8,9},{9,8},{10,11... | collective-permute-start | bytes 786440 | tf_op jit(solution)/shard_map/ppermute | solution.py:18
  591.0 8.0 %collective-permute-start.5 = (f32[256,256]{1,0:T(8,128)S(1)}, f32[256,256]{1,0:T(8,128)S(1)}, u32[]{:S(2)}, u32[]{:S(2)}) collective-permute-start(f32[256,256]{1,0:T(8,128)S(1)} %add.39), channel_id=1, source_target_pairs={{0,2},{1,3},{2,0},{3,1},{4,6},{5,7},{6,4},{7,5},{8,10},{9,11},{10,... | collective-permute-start | bytes 786440 | tf_op jit(solution)/shard_map/ppermute | solution.py:18
  599.0 15.8 %collective-permute-start.6 = (f32[256,256]{1,0:T(8,128)S(1)}, f32[256,256]{1,0:T(8,128)S(1)}, u32[]{:S(2)}, u32[]{:S(2)}) collective-permute-start(f32[256,256]{1,0:T(8,128)S(1)} %add.40), channel_id=1, source_target_pairs={{0,4},{1,5},{2,6},{3,7},{4,0},{5,1},{6,2},{7,3},{8,12},{9,13},{10,... | collective-permute-start | bytes 786440 | tf_op jit(solution)/shard_map/ppermute | solution.py:18
  614.8 12.4 %collective-permute-start.7 = (f32[256,256]{1,0:T(8,128)S(1)}, f32[256,256]{1,0:T(8,128)S(1)}, u32[]{:S(2)}, u32[]{:S(2)}) collective-permute-start(f32[256,256]{1,0:T(8,128)S(1)} %add.41), channel_id=1, source_target_pairs={{0,8},{1,9},{2,10},{3,11},{4,12},{5,13},{6,14},{7,15},{8,0},{9,1},... | collective-permute-start | bytes 786440 | tf_op jit(solution)/shard_map/ppermute | solution.py:18
Sparse Core Ops, SparseCore 0:
  142.3 271.5 all-reduce.1

commit v2 on v1

--- a/solution.py
+++ b/solution.py
@@ -10,6 +10,7 @@
 NZ = 256
 R = 128
 SWEEPS = 3
+BLOCK = 128
 
 
 def butterfly_sum(value, axis, size):
@@ -20,16 +21,64 @@
     return value
 
 
+def halving_steps(sizes):
+    steps = []
+    for axis, size in sizes:
+        stride = size // 2
+        while stride >= 1:
+            steps.append((axis, size, stride))
+            stride //= 2
+    return steps
+
+
+def halving_doubling_sum(value, sizes):
+    steps = halving_steps(sizes)
+    for axis, size, stride in steps:
+        upper = (lax.axis_index(axis) // stride) % 2 == 1
+        half = value.shape[0] // 2
+        low, high = value[:half], value[half:]
+        keep = jnp.where(upper, high, low)
+        send = jnp.where(upper, low, high)
+        value = keep + lax.ppermute(send, axis, [(i, i ^ stride) for i in range(size)])
+    for axis, size, stride in reversed(steps):
+        upper = (lax.axis_index(axis) // stride) % 2 == 1
+        other = lax.ppermute(value, axis, [(i, i ^ stride) for i in range(size)])
+        value = jnp.where(upper, jnp.concatenate([other, value]), jnp.concatenate([value, other]))
+    return value
+
+
 def body(species_field, initial):
     highest = lax.Precision.HIGHEST
     regrouped = lax.all_to_all(species_field, "gx", split_axis=3, concat_axis=1, tiled=True)
     species, rows_x, cols_y, slab_z = regrouped.shape
     fibers = regrouped.reshape(species, rows_x, cols_y * slab_z)
     scale_one = 1.0 / (S * NY * NZ)
+    n_blocks = rows_x // BLOCK
+    lower = []
+    for row in range(n_blocks):
+        strip = jnp.einsum(
+            "sxc,swc->xw",
+            fibers[:, row * BLOCK:(row + 1) * BLOCK],
+            fibers[:, :(row + 1) * BLOCK],
+            precision=highest,
+        ) * scale_one
+        lower.extend(strip[:, col * BLOCK:(col + 1) * BLOCK] for col in range(row + 1))
+    packed = jnp.concatenate(lower, axis=0)
+    sizes = (("gx", lax.axis_size("gx")), ("gy", lax.axis_size("gy")))
+    packed = halving_doubling_sum(packed, sizes)
+    blocks = packed.reshape(-1, BLOCK, BLOCK)
+    index = {}
+    for row in range(n_blocks):
+        for col in range(row + 1):
+            index[(row, col)] = len(index)
+    gram_one = jnp.concatenate([
+        jnp.concatenate([
+            blocks[index[(row, col)]] if col <= row else blocks[index[(col, row)]].T
+            for col in range(n_blocks)
+        ], axis=1)
+        for row in range(n_blocks)
+    ], axis=0)
     basis = initial
-    gram_one = lax.psum(
-        jnp.einsum("sxc,swc->xw", fibers, fibers, precision=highest) * scale_one, ("gx", "gy")
-    )
     for sweep_index in range(SWEEPS):
         wide = jnp.dot(gram_one, basis, precision=highest, preferred_element_type=jnp.float32)
         square = jnp.dot(wide.T, wide, precision=highest, preferred_element_type=jnp.float32)

time: 644 us -> 603 us (0.936)
  waiting for transfers between devices: 330 us -> 245 us
  local copies, waits for them, and re-layouts: 70.3 us -> 141 us
  blocking collectives: 75.4 us -> 22.9 us
  starting transfers between devices: 13.2 us -> 46.2 us
  between operations: 14.7 us -> 1.86 us
    psum x1 -> x0, waiting for transfers between devices: 272 us -> none  [body(): lax.psum(jnp.einsum('sxc,swc->xw', fibers, fibers, precision=highest) * s...]
    ppermute x0 -> x16, waiting for transfers between devices: none -> 124 us  [the longest x8 63.8 us: halving_doubling_sum(): other = lax.ppermute(value, axis, [(i, i ^ stride) for i in range(size)])]
    unnamed x8 -> x124, local copies, waits for them, and re-layouts: 36.6 us -> 97.8 us
    all_to_all x0 -> x1, waiting for transfers between devices: none -> 61.1 us  [body(): lax.all_to_all(species_field, 'gx', split_axis=3, concat_axis=1, tiled=True)]
    all_to_all x1 -> x0, blocking collectives: 54.5 us -> none  [body(): lax.all_to_all(species_field, 'gx', split_axis=3, concat_axis=1, tiled=True)]
    ppermute x0 -> x16, starting transfers between devices: none -> 31.7 us  [the longest x8 18.1 us: halving_doubling_sum(): lax.ppermute(send, axis, [(i, i ^ stride) for i in range(size)])]
    all_to_all x0 -> x1, starting transfers between devices: none -> 6.49 us  [body(): lax.all_to_all(species_field, 'gx', split_axis=3, concat_axis=1, tiled=True)]
    dot_general x1 -> x8, matrix products: 17.8 us -> 18.1 us  [body(): jnp.einsum('sxc,swc->xw', fibers[:, row * BLOCK:(row + 1) * BLOCK], fiber...]
  transfers between devices with their start and end apart: 9 -> 25, of which waited for: 9 -> 25; matrix products, arithmetic and copies ran while one was open for 0% -> 0% of each run, Pallas kernels for 0% -> 0%
where the time goes in v2:
time: 603 us; the launch traced here: 592 us
  waiting for transfers between devices  245 us (41%)
  local copies, waits for them, and re-layouts  141 us (23%)
  other arithmetic  87.5 us (15%)
  matrix products  47.1 us (8%)
  starting transfers between devices  46.2 us (8%)
  blocking collectives  22.9 us (4%)
    unnamed x124, local copies, waits for them, and re-layouts  97.8 us
    ppermute x8, waiting for transfers between devices, halving_doubling_sum(): other = lax.ppermute(value, axis, [(i, i ^ stride) for i in range(size)])  63.8 us
    all_to_all x1, waiting for transfers between devices, body(): lax.all_to_all(species_field, 'gx', split_axis=3, concat_axis=1, tiled=True)  61.1 us
    ppermute x8, waiting for transfers between devices, halving_doubling_sum(): lax.ppermute(send, axis, [(i, i ^ stride) for i in range(size)])  60.7 us
    ppermute x8, waiting for transfers between devices, butterfly_sum(): lax.ppermute(value, axis, [(i, i ^ stride) for i in range(size)])  59.8 us
    another operation x9, other arithmetic, body(): factor_low = jnp.linalg.cholesky(square)  37.2 us
    another operation x6, other arithmetic, body(): basis = jax.scipy.linalg.solve_triangular(factor_low, wide.T, lower=True).T  31.4 us
    all_to_all x1, blocking collectives, body(): lax.all_to_all(core_blocks, 'gy', split_axis=1, concat_axis=2, tiled=True)  22.9 us
  transfers between devices with their start and end apart: 25, of which 25 were waited for; matrix products, arithmetic and copies ran while one was open for 0% of the time, Pallas kernels for 0%

profile of v2, /device:TPU:6, one launch (start us, length us, event | category | flops | bytes accessed | tf_op | source)
XLA Modules:
  0.0 591.7 jit_solution(4743115421449389787)
XLA Ops:
  0.6 9.2 %copy.164 = f32[4,64,16,256]{1,2,0,3:T(8,128)} copy(f32[4,64,16,256]{3,2,1,0:T(8,128)} %param.5) | data formatting | bytes 8388608 | tf_op args[0]
  9.9 13.2 %reshape.104 = f32[16,1,65536]{2,1,0:T(1,128)} reshape(f32[256,4,16,64]{3,2,1,0:T(8,128)} %bitcast.174) | data formatting | bytes 8388608
  23.1 6.5 %all-to-all-start = ((f32[16,1,65536]{2,1,0:T(1,128)}), f32[16,1,65536]{2,1,0:T(1,128)}, u32[]{:S(2)}, u32[]{:S(2)}) async-start(f32[16,1,65536]{2,1,0:T(1,128)} %reshape.104), calls=%async_computation | async-start | bytes 8388608 | tf_op jit(solution)/shard_map/all_to_all | solution.py:52
  29.6 61.1 %all-to-all-done = f32[16,1,65536]{2,1,0:T(1,128)} async-done(((f32[16,1,65536]{2,1,0:T(1,128)}), f32[16,1,65536]{2,1,0:T(1,128)}, u32[]{:S(2)}, u32[]{:S(2)}) %all-to-all-start) | async-done | bytes 4194336 | tf_op jit(solution)/shard_map/all_to_all | solution.py:52
  91.2 13.7 %reduce.4 = f32[16,65536]{1,0:T(8,128)} reduce(f32[16,1,65536]{2,1,0:T(1,128)} %all-to-all-done, f32[]{:T(128)} %broadcast.55), dimensions={1}, to_apply=%all_to_all.24.reduce_sub_computation | reduce | bytes 8388612 | tf_op jit(solution)/shard_map/all_to_all | solution.py:52
  104.9 6.9 %reshape.105 = f32[256,4,16,64]{3,2,1,0:T(8,128)} reshape(f32[16,65536]{1,0:T(8,128)} %reduce.4) | data formatting | bytes 8388608
  111.8 11.5 %copy.166 = f32[4,16,64,16,16]{2,1,4,3,0:T(8,128)} copy(f32[4,16,64,16,16]{2,3,0,4,1:T(8,128)} %bitcast.175) | data formatting | bytes 8388608 | tf_op jit(solution)/shard_map/all_to_all | solution.py:52
  123.2 8.0 %reshape.92 = f32[4,1024,256]{1,2,0:T(8,128)} reshape(f32[4,16,64,16,16]{2,1,4,3,0:T(8,128)} %copy.166) | data formatting | bytes 8388608 | tf_op jit(solution)/shard_map/reshape | solution.py:54
  131.3 2.6 fusion.42
  133.9 2.4 fusion.44
  136.3 2.8 fusion.39
  140.6 1.9 fusion.30
  142.4 2.0 fusion.23
  144.5 2.4 fusion.17
  146.9 2.6 fusion.10
  151.2 1.7 collective-permute-start
  152.9 26.8 %collective-permute-done = f32[2304,128]{1,0:T(8,128)} collective-permute-done((f32[2304,128]{1,0:T(8,128)S(1)}, f32[2304,128]{1,0:T(8,128)}, u32[]{:S(2)}, u32[]{:S(2)}) %collective-permute-start) | collective-permute-done | bytes 1179680 | tf_op jit(solution)/shard_map/ppermute | solution.py:42
  181.3 16.2 %collective-permute-done.1 = f32[1152,128]{1,0:T(8,128)S(1)} collective-permute-done((f32[1152,128]{1,0:T(8,128)S(1)}, f32[1152,128]{1,0:T(8,128)S(1)}, u32[]{:S(2)}, u32[]{:S(2)}) %collective-permute-start.1) | collective-permute-done | bytes 589856 | tf_op jit(solution)/shard_map/ppermute | solution.py:42
  197.8 7.6 %collective-permute-done.2 = f32[576,128]{1,0:T(8,128)S(1)} collective-permute-done((f32[576,128]{1,0:T(8,128)S(1)}, f32[576,128]{1,0:T(8,128)S(1)}, u32[]{:S(2)}, u32[]{:S(2)}) %collective-permute-start.2) | collective-permute-done | bytes 294944 | tf_op jit(solution)/shard_map/ppermute | solution.py:42
  206.9 7.1 %collective-permute-start.4 = (f32[144,128]{1,0:T(8,128)S(1)}, f32[144,128]{1,0:T(8,128)S(1)}, u32[]{:S(2)}, u32[]{:S(2)}) collective-permute-start(f32[144,128]{1,0:T(8,128)S(1)} %slice_select_fusion.3), channel_id=1, source_target_pairs={{0,8},{1,9},{2,10},{3,11},{4,12},{5,13},{6,14},{7,15},{8,0},{9,1},... | collective-permute-start | bytes 221192 | tf_op jit(solution)/shard_map/ppermute | solution.py:42
  214.1 2.7 collective-permute-done.4
  216.8 4.0 collective-permute-start.5
  220.8 1.9 collective-permute-done.5
  222.8 3.3 collective-permute-start.6
  226.1 2.1 collective-permute-done.6
  228.2 1.7 collective-permute-start.7
  229.9 2.1 collective-permute-done.7
  233.6 2.1 collective-permute-done.8
  235.7 3.3 collective-permute-start.9
  239.0 2.1 collective-permute-done.9
  241.1 3.0 collective-permute-start.10
  244.1 3.8 collective-permute-done.10
  247.9 4.3 collective-permute-start.11
  252.2 4.1 collective-permute-done.11
  258.2 8.8 %collective-permute-done.13 = f32[576,128]{1,0:T(8,128)S(1)} collective-permute-done((f32[576,128]{1,0:T(8,128)S(1)}, f32[576,128]{1,0:T(8,128)S(1)}, u32[]{:S(2)}, u32[]{:S(2)}) %collective-permute-start.13) | collective-permute-done | bytes 294944 | tf_op jit(solution)/shard_map/ppermute | solution.py:45
  267.6 15.5 %collective-permute-done.14 = f32[1152,128]{1,0:T(8,128)S(1)} collective-permute-done((f32[1152,128]{1,0:T(8,128)S(1)}, f32[1152,128]{1,0:T(8,128)S(1)}, u32[]{:S(2)}, u32[]{:S(2)}) %collective-permute-start.14) | collective-permute-done | bytes 589856 | tf_op jit(solution)/shard_map/ppermute | solution.py:45
  283.5 26.1 %collective-permute-done.15 = f32[2304,128]{1,0:T(8,128)S(1)} collective-permute-done((f32[2304,128]{1,0:T(8,128)S(1)}, f32[2304,128]{1,0:T(8,128)S(1)}, u32[]{:S(2)}, u32[]{:S(2)}) %collective-permute-start.15) | collective-permute-done | bytes 1179680 | tf_op jit(solution)/shard_map/ppermute | solution.py:45
  350.6 1.6 copy.256
  378.5 5.4 fusion.76
  385.1 11.7 %cholesky.59 = f32[128,128]{1,0:T(8,128)S(1)} custom-call(f32[128,128]{1,0:T(8,128)S(1)} %fusion.69), custom_call_target="Cholesky" | custom-call | tf_op jit(solution)/shard_map/jit(cholesky)/cholesky | solution.py:85
  398.1 9.8 %custom-call.7 = f32[1,128,128]{1,2,0:T(8,128)S(1)} custom-call(f32[1,128,128]{2,1,0:T(8,128)S(1)} %fusion.61), custom_call_target="InvertDiagBlocksLowerTriangular" | custom-call | tf_op jit(solution)/shard_map/jit(_solve_triangular)/triangular_solve | solution.py:86
  408.6 5.6 fusion.78
  415.3 11.7 %cholesky.70 = f32[128,128]{1,0:T(8,128)S(1)} custom-call(f32[128,128]{1,0:T(8,128)S(1)} %fusion.67), custom_call_target="Cholesky" | custom-call | tf_op jit(solution)/shard_map/jit(cholesky)/cholesky | solution.py:85
  428.4 9.8 %custom-call.8 = f32[1,128,128]{1,2,0:T(8,128)S(1)} custom-call(f32[1,128,128]{2,1,0:T(8,128)S(1)} %fusion.62), custom_call_target="InvertDiagBlocksLowerTriangular" | custom-call | tf_op jit(solution)/shard_map/jit(_solve_triangular)/triangular_solve | solution.py:86
  438.9 5.4 fusion.80
  445.4 11.7 %cholesky.81 = f32[128,128]{1,0:T(8,128)S(1)} custom-call(f32[128,128]{1,0:T(8,128)S(1)} %fusion.65), custom_call_target="Cholesky" | custom-call | tf_op jit(solution)/shard_map/jit(cholesky)/cholesky | solution.py:85
  458.5 9.8 %custom-call.9 = f32[1,128,128]{1,2,0:T(8,128)S(1)} custom-call(f32[1,128,128]{2,1,0:T(8,128)S(1)} %fusion.63), custom_call_target="InvertDiagBlocksLowerTriangular" | custom-call | tf_op jit(solution)/shard_map/jit(_solve_triangular)/triangular_solve | solution.py:86
  468.9 6.5 %convolution_bitcast_fusion = f32[4,128,256]{2,1,0:T(8,128)S(1)} fusion(f32[4,1024,256]{1,2,0:T(8,128)} %reshape.92, f32[128,1024]{1,0:T(8,128)S(1)} %fusion.55), kind=kOutput, calls=%fused_computation.11 | convolution fusion | flops 1610612736 | bytes 5242880 | tf_op jit(solution)/shard_map/xr,sxc->src/dot_general | solution.py:87
  475.7 4.6 copy.222
  480.3 3.5 reshape.106
  483.8 22.9 %all_to_all.33 = f32[16,1,8192]{2,1,0:T(1,128)S(1)} all-to-all(f32[16,1,8192]{2,1,0:T(1,128)S(1)} %reshape.106), channel_id=1, replica_groups=mesh['gx'=16,'gy'=16] {'gy'}, dimensions={0} | all-to-all | bytes 1048576 | tf_op jit(solution)/shard_map/all_to_all | solution.py:89
  506.7 1.9 reduce.5
  508.6 2.8 reshape.107
  511.4 5.6 copy.224
  517.0 3.5 all_to_all.30
  523.5 8.1 %collective-permute-done.17 = f32[256,256]{1,0:T(8,128)S(1)} collective-permute-done((f32[256,256]{1,0:T(8,128)S(1)}, f32[256,256]{1,0:T(8,128)S(1)}, u32[]{:S(2)}, u32[]{:S(2)}) %collective-permute-start.17) | collective-permute-done | bytes 262176 | tf_op jit(solution)/shard_map/ppermute | solution.py:19
  532.3 8.4 %collective-permute-done.18 = f32[256,256]{1,0:T(8,128)S(1)} collective-permute-done((f32[256,256]{1,0:T(8,128)S(1)}, f32[256,256]{1,0:T(8,128)S(1)}, u32[]{:S(2)}, u32[]{:S(2)}) %collective-permute-start.18) | collective-permute-done | bytes 262176 | tf_op jit(solution)/shard_map/ppermute | solution.py:19
  540.8 3.3 collective-permute-start.19
  544.1 4.9 collective-permute-done.19
  549.7 5.8 collective-permute-done.20
  555.5 2.0 collective-permute-start.21
  557.6 5.9 collective-permute-done.21
  564.3 16.0 %collective-permute-done.22 = f32[256,256]{1,0:T(8,128)S(1)} collective-permute-done((f32[256,256]{1,0:T(8,128)S(1)}, f32[256,256]{1,0:T(8,128)S(1)}, u32[]{:S(2)}, u32[]{:S(2)}) %collective-permute-start.22) | collective-permute-done | bytes 262176 | tf_op jit(solution)/shard_map/ppermute | solution.py:19
  581.4 9.3 %collective-permute-done.23 = f32[256,256]{1,0:T(8,128)S(1)} collective-permute-done((f32[256,256]{1,0:T(8,128)S(1)}, f32[256,256]{1,0:T(8,128)S(1)}, u32[]{:S(2)}, u32[]{:S(2)}) %collective-permute-start.23) | collective-permute-done | bytes 262176 | tf_op jit(solution)/shard_map/ppermute | solution.py:19
  (206 shorter events, 95.1 us)
Async XLA Ops:
  0.6 377.9 %copy-start = (f32[1024,128]{1,0:T(8,128)S(1)}, f32[1024,128]{1,0:T(8,128)}, u32[]{:S(2)}) copy-start(f32[1024,128]{1,0:T(8,128)} %param.6) | copy-start | bytes 1572868
  23.1 67.5 %all-to-all-start = ((f32[16,1,65536]{2,1,0:T(1,128)}), f32[16,1,65536]{2,1,0:T(1,128)}, u32[]{:S(2)}, u32[]{:S(2)}) async-start(f32[16,1,65536]{2,1,0:T(1,128)} %reshape.104), calls=%async_computation | async-start | bytes 8388608 | tf_op jit(solution)/shard_map/all_to_all | solution.py:52
  131.3 7.8 %copy-start.1 = (f32[4,1024,256]{1,2,0:T(8,128)S(1)}, f32[4,1024,256]{1,2,0:T(8,128)}, u32[]{:S(2)}) copy-start(f32[4,1024,256]{1,2,0:T(8,128)} %reshape.92) | copy-start | bytes 12582916
  150.1 1.0 copy-start.2
  151.2 28.5 %collective-permute-start = (f32[2304,128]{1,0:T(8,128)S(1)}, f32[2304,128]{1,0:T(8,128)}, u32[]{:S(2)}, u32[]{:S(2)}) collective-permute-start(f32[2304,128]{1,0:T(8,128)S(1)} %broadcast_select_fusion), channel_id=1, source_target_pairs={{0,128},{16,144},{32,160},{48,176},{64,192},{80,208},{96,224},{112... | collective-permute-start | bytes 3538952 | tf_op jit(solution)/shard_map/ppermute | solution.py:42
  181.2 16.4 %collective-permute-start.1 = (f32[1152,128]{1,0:T(8,128)S(1)}, f32[1152,128]{1,0:T(8,128)S(1)}, u32[]{:S(2)}, u32[]{:S(2)}) collective-permute-start(f32[1152,128]{1,0:T(8,128)S(1)} %slice_select_fusion), channel_id=1, source_target_pairs={{0,64},{16,80},{32,96},{48,112},{64,0},{80,16},{96,32},{112,48},{1... | collective-permute-start | bytes 1769480 | tf_op jit(solution)/shard_map/ppermute | solution.py:42
  197.7 7.7 %collective-permute-start.2 = (f32[576,128]{1,0:T(8,128)S(1)}, f32[576,128]{1,0:T(8,128)S(1)}, u32[]{:S(2)}, u32[]{:S(2)}) collective-permute-start(f32[576,128]{1,0:T(8,128)S(1)} %slice_select_fusion.1), channel_id=1, source_target_pairs={{0,32},{16,48},{32,0},{48,16},{64,96},{80,112},{96,64},{112,80},{1... | collective-permute-start | bytes 884744 | tf_op jit(solution)/shard_map/ppermute | solution.py:42
  205.4 1.5 collective-permute-start.3
  206.9 9.8 %collective-permute-start.4 = (f32[144,128]{1,0:T(8,128)S(1)}, f32[144,128]{1,0:T(8,128)S(1)}, u32[]{:S(2)}, u32[]{:S(2)}) collective-permute-start(f32[144,128]{1,0:T(8,128)S(1)} %slice_select_fusion.3), channel_id=1, source_target_pairs={{0,8},{1,9},{2,10},{3,11},{4,12},{5,13},{6,14},{7,15},{8,0},{9,1},... | collective-permute-start | bytes 221192 | tf_op jit(solution)/shard_map/ppermute | solution.py:42
  216.8 6.0 %collective-permute-start.5 = (f32[72,128]{1,0:T(8,128)S(1)}, f32[72,128]{1,0:T(8,128)S(1)}, u32[]{:S(2)}, u32[]{:S(2)}) collective-permute-start(f32[72,128]{1,0:T(8,128)S(1)} %slice_select_fusion.4), channel_id=1, source_target_pairs={{0,4},{1,5},{2,6},{3,7},{4,0},{5,1},{6,2},{7,3},{8,12},{9,13},{10,... | collective-permute-start | bytes 110600 | tf_op jit(solution)/shard_map/ppermute | solution.py:42
  222.8 5.4 collective-permute-start.6
  228.2 3.8 collective-permute-start.7
  232.0 3.7 collective-permute-start.8
  235.7 5.4 collective-permute-start.9
  241.1 6.9 %collective-permute-start.10 = (f32[72,128]{1,0:T(8,128)S(1)}, f32[72,128]{1,0:T(8,128)S(1)}, u32[]{:S(2)}, u32[]{:S(2)}) collective-permute-start(f32[72,128]{1,0:T(8,128)S(1)} %maximum_select_fusion.6), channel_id=1, source_target_pairs={{0,4},{1,5},{2,6},{3,7},{4,0},{5,1},{6,2},{7,3},{8,12},{9,13},{10,... | collective-permute-start | bytes 110600 | tf_op jit(solution)/shard_map/ppermute | solution.py:45
  247.9 8.3 %collective-permute-start.11 = (f32[144,128]{1,0:T(8,128)S(1)}, f32[144,128]{1,0:T(8,128)S(1)}, u32[]{:S(2)}, u32[]{:S(2)}) collective-permute-start(f32[144,128]{1,0:T(8,128)S(1)} %maximum_select_fusion.5), channel_id=1, source_target_pairs={{0,8},{1,9},{2,10},{3,11},{4,12},{5,13},{6,14},{7,15},{8,0},{9,1},... | collective-permute-start | bytes 221192 | tf_op jit(solution)/shard_map/ppermute | solution.py:45
  256.3 1.5 collective-permute-start.12
  257.8 9.1 %collective-permute-start.13 = (f32[576,128]{1,0:T(8,128)S(1)}, f32[576,128]{1,0:T(8,128)S(1)}, u32[]{:S(2)}, u32[]{:S(2)}) collective-permute-start(f32[576,128]{1,0:T(8,128)S(1)} %maximum_select_fusion.3), channel_id=1, source_target_pairs={{0,32},{16,48},{32,0},{48,16},{64,96},{80,112},{96,64},{112,80},{1... | collective-permute-start | bytes 884744 | tf_op jit(solution)/shard_map/ppermute | solution.py:45
  267.0 16.1 %collective-permute-start.14 = (f32[1152,128]{1,0:T(8,128)S(1)}, f32[1152,128]{1,0:T(8,128)S(1)}, u32[]{:S(2)}, u32[]{:S(2)}) collective-permute-start(f32[1152,128]{1,0:T(8,128)S(1)} %maximum_select_fusion.2), channel_id=1, source_target_pairs={{0,64},{16,80},{32,96},{48,112},{64,0},{80,16},{96,32},{112,48},{1... | collective-permute-start | bytes 1769480 | tf_op jit(solution)/shard_map/ppermute | solution.py:45
  283.2 26.4 %collective-permute-start.15 = (f32[2304,128]{1,0:T(8,128)S(1)}, f32[2304,128]{1,0:T(8,128)S(1)}, u32[]{:S(2)}, u32[]{:S(2)}) collective-permute-start(f32[2304,128]{1,0:T(8,128)S(1)} %maximum_select_fusion.1), channel_id=1, source_target_pairs={{0,128},{16,144},{32,160},{48,176},{64,192},{80,208},{96,224},{112... | collective-permute-start | bytes 3538952 | tf_op jit(solution)/shard_map/ppermute | solution.py:45
  334.9 7.4 %copy-start.3 = (f32[128,128]{0,1:T(8,128)}, f32[128,128]{0,1:T(8,128)S(1)}, u32[]{:S(2)}) copy-start(f32[128,128]{0,1:T(8,128)S(1)} %copy.253) | copy-start | bytes 196612
  350.6 22.1 %copy-start.4 = (f32[128,128]{1,0:T(8,128)S(1)}, f32[128,128]{1,0:T(8,128)}, u32[]{:S(2)}) copy-start(f32[128,128]{1,0:T(8,128)} %get-tuple-element.12) | copy-start | bytes 196612
  521.5 1.6 collective-permute-start.16
  523.2 8.4 %collective-permute-start.17 = (f32[256,256]{1,0:T(8,128)S(1)}, f32[256,256]{1,0:T(8,128)S(1)}, u32[]{:S(2)}, u32[]{:S(2)}) collective-permute-start(f32[256,256]{1,0:T(8,128)S(1)} %add.114), channel_id=1, source_target_pairs={{0,32},{16,48},{32,0},{48,16},{64,96},{80,112},{96,64},{112,80},{1... | collective-permute-start | bytes 786440 | tf_op jit(solution)/shard_map/ppermute | solution.py:19
  531.6 9.1 %collective-permute-start.18 = (f32[256,256]{1,0:T(8,128)S(1)}, f32[256,256]{1,0:T(8,128)S(1)}, u32[]{:S(2)}, u32[]{:S(2)}) collective-permute-start(f32[256,256]{1,0:T(8,128)S(1)} %add.115), channel_id=1, source_target_pairs={{0,64},{16,80},{32,96},{48,112},{64,0},{80,16},{96,32},{112,48},{1... | collective-permute-start | bytes 786440 | tf_op jit(solution)/shard_map/ppermute | solution.py:19
  540.8 8.2 %collective-permute-start.19 = (f32[256,256]{1,0:T(8,128)S(1)}, f32[256,256]{1,0:T(8,128)S(1)}, u32[]{:S(2)}, u32[]{:S(2)}) collective-permute-start(f32[256,256]{1,0:T(8,128)S(1)} %add.116), channel_id=1, source_target_pairs={{0,128},{16,144},{32,160},{48,176},{64,192},{80,208},{96,224},{112... | collective-permute-start | bytes 786440 | tf_op jit(solution)/shard_map/ppermute | solution.py:19
  549.0 6.5 %collective-permute-start.20 = (f32[256,256]{1,0:T(8,128)S(1)}, f32[256,256]{1,0:T(8,128)S(1)}, u32[]{:S(2)}, u32[]{:S(2)}) collective-permute-start(f32[256,256]{1,0:T(8,128)S(1)} %add.117), channel_id=1, source_target_pairs={{0,1},{1,0},{2,3},{3,2},{4,5},{5,4},{6,7},{7,6},{8,9},{9,8},{10,11... | collective-permute-start | bytes 786440 | tf_op jit(solution)/shard_map/ppermute | solution.py:19
  555.5 8.0 %collective-permute-start.21 = (f32[256,256]{1,0:T(8,128)S(1)}, f32[256,256]{1,0:T(8,128)S(1)}, u32[]{:S(2)}, u32[]{:S(2)}) collective-permute-start(f32[256,256]{1,0:T(8,128)S(1)} %add.118), channel_id=1, source_target_pairs={{0,2},{1,3},{2,0},{3,1},{4,6},{5,7},{6,4},{7,5},{8,10},{9,11},{10,... | collective-permute-start | bytes 786440 | tf_op jit(solution)/shard_map/ppermute | solution.py:19
  563.5 16.7 %collective-permute-start.22 = (f32[256,256]{1,0:T(8,128)S(1)}, f32[256,256]{1,0:T(8,128)S(1)}, u32[]{:S(2)}, u32[]{:S(2)}) collective-permute-start(f32[256,256]{1,0:T(8,128)S(1)} %add.119), channel_id=1, source_target_pairs={{0,4},{1,5},{2,6},{3,7},{4,0},{5,1},{6,2},{7,3},{8,12},{9,13},{10,... | collective-permute-start | bytes 786440 | tf_op jit(solution)/shard_map/ppermute | solution.py:19
  580.3 10.4 %collective-permute-start.23 = (f32[256,256]{1,0:T(8,128)S(1)}, f32[256,256]{1,0:T(8,128)S(1)}, u32[]{:S(2)}, u32[]{:S(2)}) collective-permute-start(f32[256,256]{1,0:T(8,128)S(1)} %add.120), channel_id=1, source_target_pairs={{0,8},{1,9},{2,10},{3,11},{4,12},{5,13},{6,14},{7,15},{8,0},{9,1},... | collective-permute-start | bytes 786440 | tf_op jit(solution)/shard_map/ppermute | solution.py:19

commit v3 on v2

--- a/solution.py
+++ b/solution.py
@@ -67,17 +67,15 @@
     sizes = (("gx", lax.axis_size("gx")), ("gy", lax.axis_size("gy")))
     packed = halving_doubling_sum(packed, sizes)
     blocks = packed.reshape(-1, BLOCK, BLOCK)
+    both = jnp.concatenate([blocks, jnp.swapaxes(blocks, 1, 2)], axis=0)
     index = {}
     for row in range(n_blocks):
         for col in range(row + 1):
             index[(row, col)] = len(index)
-    gram_one = jnp.concatenate([
-        jnp.concatenate([
-            blocks[index[(row, col)]] if col <= row else blocks[index[(col, row)]].T
-            for col in range(n_blocks)
-        ], axis=1)
-        for row in range(n_blocks)
-    ], axis=0)
+    picks = [[index[(row, col)] if col <= row else len(index) + index[(col, row)]
+              for col in range(n_blocks)] for row in range(n_blocks)]
+    tiles = jnp.take(both, jnp.asarray(picks, jnp.int32), axis=0)
+    gram_one = jnp.swapaxes(tiles, 1, 2).reshape(rows_x, rows_x)
     basis = initial
     for sweep_index in range(SWEEPS):
         wide = jnp.dot(gram_one, basis, precision=highest, preferred_element_type=jnp.float32)

time: 603 us -> 548 us (0.909)
  local copies, waits for them, and re-layouts: 141 us -> 84.1 us
    unnamed x124 -> x47, local copies, waits for them, and re-layouts: 97.8 us -> 37.9 us
    select_n x0 -> x2, local copies, waits for them, and re-layouts: none -> 6.94 us  [the longest x1 4.56 us: body(): tiles = jnp.take(both, jnp.asarray(picks, jnp.int32), axis=0)]
    concatenate x7 -> x0, local copies, waits for them, and re-layouts: 6.27 us -> none  [the longest x6 5.63 us: body(): jnp.concatenate([blocks[index[row, col]] if col <= row else blocks[index[...]
where the time goes in v3:
time: 548 us; the launch traced here: 540 us
  waiting for transfers between devices  245 us (45%)
  other arithmetic  92.1 us (17%)
  local copies, waits for them, and re-layouts  84.1 us (15%)
  starting transfers between devices  48.4 us (9%)
  matrix products  45.8 us (8%)
  blocking collectives  22.9 us (4%)
    ppermute x8, waiting for transfers between devices, halving_doubling_sum(): other = lax.ppermute(value, axis, [(i, i ^ stride) for i in range(size)])  63.8 us
    all_to_all x1, waiting for transfers between devices, body(): lax.all_to_all(species_field, 'gx', split_axis=3, concat_axis=1, tiled=True)  61.1 us
    ppermute x8, waiting for transfers between devices, halving_doubling_sum(): lax.ppermute(send, axis, [(i, i ^ stride) for i in range(size)])  60.7 us
    ppermute x8, waiting for transfers between devices, butterfly_sum(): lax.ppermute(value, axis, [(i, i ^ stride) for i in range(size)])  59.3 us
    unnamed x47, local copies, waits for them, and re-layouts  37.9 us
    another operation x9, other arithmetic, body(): factor_low = jnp.linalg.cholesky(square)  37.2 us
    another operation x6, other arithmetic, body(): basis = jax.scipy.linalg.solve_triangular(factor_low, wide.T, lower=True).T  31.5 us
    all_to_all x1, blocking collectives, body(): lax.all_to_all(core_blocks, 'gy', split_axis=1, concat_axis=2, tiled=True)  22.9 us
  transfers between devices with their start and end apart: 25, of which 25 were waited for; matrix products, arithmetic and copies ran while one was open for 0% of the time, Pallas kernels for 0%

profile of v3, /device:TPU:6, one launch (start us, length us, event | category | flops | bytes accessed | tf_op | source)
XLA Modules:
  0.0 539.9 jit_solution(7904885238582510879)
XLA Ops:
  0.6 9.2 %copy.64 = f32[4,64,16,256]{1,2,0,3:T(8,128)} copy(f32[4,64,16,256]{3,2,1,0:T(8,128)} %param.6) | data formatting | bytes 8388608 | tf_op args[0]
  9.9 13.3 %reshape.54 = f32[16,1,65536]{2,1,0:T(1,128)} reshape(f32[256,4,16,64]{3,2,1,0:T(8,128)} %bitcast.132) | data formatting | bytes 8388608
  23.1 6.5 %all-to-all-start = ((f32[16,1,65536]{2,1,0:T(1,128)}), f32[16,1,65536]{2,1,0:T(1,128)}, u32[]{:S(2)}, u32[]{:S(2)}) async-start(f32[16,1,65536]{2,1,0:T(1,128)} %reshape.54), calls=%async_computation | async-start | bytes 8388608 | tf_op jit(solution)/shard_map/all_to_all | solution.py:52
  29.6 61.1 %all-to-all-done = f32[16,1,65536]{2,1,0:T(1,128)} async-done(((f32[16,1,65536]{2,1,0:T(1,128)}), f32[16,1,65536]{2,1,0:T(1,128)}, u32[]{:S(2)}, u32[]{:S(2)}) %all-to-all-start) | async-done | bytes 4194336 | tf_op jit(solution)/shard_map/all_to_all | solution.py:52
  91.2 13.7 %reduce.4 = f32[16,65536]{1,0:T(8,128)} reduce(f32[16,1,65536]{2,1,0:T(1,128)} %all-to-all-done, f32[]{:T(128)} %broadcast.72), dimensions={1}, to_apply=%all_to_all.24.reduce_sub_computation | reduce | bytes 8388612 | tf_op jit(solution)/shard_map/all_to_all | solution.py:52
  104.9 6.9 %reshape.55 = f32[256,4,16,64]{3,2,1,0:T(8,128)} reshape(f32[16,65536]{1,0:T(8,128)} %reduce.4) | data formatting | bytes 8388608
  111.8 11.5 %copy.66 = f32[4,16,64,16,16]{2,1,4,3,0:T(8,128)} copy(f32[4,16,64,16,16]{2,3,0,4,1:T(8,128)} %bitcast.133) | data formatting | bytes 8388608 | tf_op jit(solution)/shard_map/all_to_all | solution.py:52
  123.3 8.0 %reshape.32 = f32[4,1024,256]{1,2,0:T(8,128)} reshape(f32[4,16,64,16,16]{2,1,4,3,0:T(8,128)} %copy.66) | data formatting | bytes 8388608 | tf_op jit(solution)/shard_map/reshape | solution.py:54
  131.3 2.6 fusion.51
  133.9 2.2 fusion.53
  136.1 2.8 fusion.48
  142.3 2.0 fusion.32
  144.3 2.4 fusion.26
  146.7 2.7 fusion.19
  152.6 26.8 %collective-permute-done = f32[2304,128]{1,0:T(8,128)} collective-permute-done((f32[2304,128]{1,0:T(8,128)S(1)}, f32[2304,128]{1,0:T(8,128)}, u32[]{:S(2)}, u32[]{:S(2)}) %collective-permute-start) | collective-permute-done | bytes 1179680 | tf_op jit(solution)/shard_map/ppermute | solution.py:42
  181.0 16.2 %collective-permute-done.1 = f32[1152,128]{1,0:T(8,128)S(1)} collective-permute-done((f32[1152,128]{1,0:T(8,128)S(1)}, f32[1152,128]{1,0:T(8,128)S(1)}, u32[]{:S(2)}, u32[]{:S(2)}) %collective-permute-start.1) | collective-permute-done | bytes 589856 | tf_op jit(solution)/shard_map/ppermute | solution.py:42
  197.5 7.6 %collective-permute-done.2 = f32[576,128]{1,0:T(8,128)S(1)} collective-permute-done((f32[576,128]{1,0:T(8,128)S(1)}, f32[576,128]{1,0:T(8,128)S(1)}, u32[]{:S(2)}, u32[]{:S(2)}) %collective-permute-start.2) | collective-permute-done | bytes 294944 | tf_op jit(solution)/shard_map/ppermute | solution.py:42
  206.6 7.1 %collective-permute-start.4 = (f32[144,128]{1,0:T(8,128)S(1)}, f32[144,128]{1,0:T(8,128)S(1)}, u32[]{:S(2)}, u32[]{:S(2)}) collective-permute-start(f32[144,128]{1,0:T(8,128)S(1)} %slice_select_fusion.3), channel_id=1, source_target_pairs={{0,8},{1,9},{2,10},{3,11},{4,12},{5,13},{6,14},{7,15},{8,0},{9,1},... | collective-permute-start | bytes 221192 | tf_op jit(solution)/shard_map/ppermute | solution.py:42
  213.7 2.7 collective-permute-done.4
  216.4 4.0 collective-permute-start.5
  220.5 1.9 collective-permute-done.5
  222.4 3.3 collective-permute-start.6
  225.7 2.1 collective-permute-done.6
  229.5 2.1 collective-permute-done.7
  233.2 2.1 collective-permute-done.8
  235.3 3.3 collective-permute-start.9
  238.6 2.1 collective-permute-done.9
  240.7 3.0 collective-permute-start.10
  243.7 3.8 collective-permute-done.10
  247.6 4.3 collective-permute-start.11
  251.8 4.1 collective-permute-done.11
  257.8 8.8 %collective-permute-done.13 = f32[576,128]{1,0:T(8,128)S(1)} collective-permute-done((f32[576,128]{1,0:T(8,128)S(1)}, f32[576,128]{1,0:T(8,128)S(1)}, u32[]{:S(2)}, u32[]{:S(2)}) %collective-permute-start.13) | collective-permute-done | bytes 294944 | tf_op jit(solution)/shard_map/ppermute | solution.py:45
  267.3 15.5 %collective-permute-done.14 = f32[1152,128]{1,0:T(8,128)S(1)} collective-permute-done((f32[1152,128]{1,0:T(8,128)S(1)}, f32[1152,128]{1,0:T(8,128)S(1)}, u32[]{:S(2)}, u32[]{:S(2)}) %collective-permute-start.14) | collective-permute-done | bytes 589856 | tf_op jit(solution)/shard_map/ppermute | solution.py:45
  283.1 26.1 %collective-permute-done.15 = f32[2304,128]{1,0:T(8,128)S(1)} collective-permute-done((f32[2304,128]{1,0:T(8,128)S(1)}, f32[2304,128]{1,0:T(8,128)S(1)}, u32[]{:S(2)}, u32[]{:S(2)}) %collective-permute-start.15) | collective-permute-done | bytes 1179680 | tf_op jit(solution)/shard_map/ppermute | solution.py:45
  309.5 2.4 copy.82
  311.9 4.3 pad_maximum_fusion
  316.2 5.2 gather_fusion
  321.4 4.6 copy.83
  326.0 3.5 fusion.4
  330.6 11.7 %cholesky.59 = f32[128,128]{1,0:T(8,128)S(1)} custom-call(f32[128,128]{1,0:T(8,128)S(1)} %fusion.78), custom_call_target="Cholesky" | custom-call | tf_op jit(solution)/shard_map/jit(cholesky)/cholesky | solution.py:83
  343.6 9.9 %custom-call.7 = f32[1,128,128]{1,2,0:T(8,128)S(1)} custom-call(f32[1,128,128]{2,1,0:T(8,128)S(1)} %fusion.70), custom_call_target="InvertDiagBlocksLowerTriangular" | custom-call | tf_op jit(solution)/shard_map/jit(_solve_triangular)/triangular_solve | solution.py:84
  354.2 5.7 %fusion.2 = f32[1024,128]{1,0:T(8,128)S(1)} fusion(f32[128,1024]{1,0:T(8,128)S(1)} %fusion.68, f32[128,8,8,128]{3,2,1,0:T(8,128)} %bitcast.130), kind=kOutput, calls=%fused_computation.4 | convolution fusion | flops 1610612736 | bytes 5242880 | tf_op jit(solution)/shard_map/dot_general | solution.py:81
  361.1 11.7 %cholesky.70 = f32[128,128]{1,0:T(8,128)S(1)} custom-call(f32[128,128]{1,0:T(8,128)S(1)} %fusion.76), custom_call_target="Cholesky" | custom-call | tf_op jit(solution)/shard_map/jit(cholesky)/cholesky | solution.py:83
  374.2 9.8 %custom-call.8 = f32[1,128,128]{1,2,0:T(8,128)S(1)} custom-call(f32[1,128,128]{2,1,0:T(8,128)S(1)} %fusion.71), custom_call_target="InvertDiagBlocksLowerTriangular" | custom-call | tf_op jit(solution)/shard_map/jit(_solve_triangular)/triangular_solve | solution.py:84
  384.6 6.1 %fusion = f32[1024,128]{1,0:T(8,128)S(1)} fusion(f32[128,1024]{1,0:T(8,128)S(1)} %fusion.66, f32[128,8,8,128]{3,2,1,0:T(8,128)} %bitcast.131), kind=kOutput, calls=%fused_computation.2 | convolution fusion | flops 1610612736 | bytes 5242880 | tf_op jit(solution)/shard_map/dot_general | solution.py:81
  391.9 11.7 %cholesky.81 = f32[128,128]{1,0:T(8,128)S(1)} custom-call(f32[128,128]{1,0:T(8,128)S(1)} %fusion.74), custom_call_target="Cholesky" | custom-call | tf_op jit(solution)/shard_map/jit(cholesky)/cholesky | solution.py:83
  405.0 9.8 %custom-call.9 = f32[1,128,128]{1,2,0:T(8,128)S(1)} custom-call(f32[1,128,128]{2,1,0:T(8,128)S(1)} %fusion.72), custom_call_target="InvertDiagBlocksLowerTriangular" | custom-call | tf_op jit(solution)/shard_map/jit(_solve_triangular)/triangular_solve | solution.py:84
  415.4 6.5 %convolution_bitcast_fusion = f32[4,128,256]{2,1,0:T(8,128)S(1)} fusion(f32[4,1024,256]{1,2,0:T(8,128)} %reshape.32, f32[128,1024]{1,0:T(8,128)S(1)} %fusion.64), kind=kOutput, calls=%fused_computation.22 | convolution fusion | flops 1610612736 | bytes 5242880 | tf_op jit(solution)/shard_map/xr,sxc->src/dot_general | solution.py:85
  422.2 4.6 copy.89
  426.7 3.5 reshape.56
  430.2 22.9 %all_to_all.33 = f32[16,1,8192]{2,1,0:T(1,128)S(1)} all-to-all(f32[16,1,8192]{2,1,0:T(1,128)S(1)} %reshape.56), channel_id=1, replica_groups=mesh['gx'=16,'gy'=16] {'gy'}, dimensions={0} | all-to-all | bytes 1048576 | tf_op jit(solution)/shard_map/all_to_all | solution.py:87
  455.0 2.8 reshape.57
  457.8 5.6 %copy.91 = f32[4,8,16,16,16]{3,2,4,0,1:T(8,128)} copy(f32[4,8,16,16,16]{4,3,0,1,2:T(8,128)} %bitcast.137) | data formatting | bytes 1048576 | tf_op jit(solution)/shard_map/all_to_all | solution.py:87
  463.4 3.5 all_to_all.30
  470.0 8.1 %collective-permute-done.17 = f32[256,256]{1,0:T(8,128)S(1)} collective-permute-done((f32[256,256]{1,0:T(8,128)S(1)}, f32[256,256]{1,0:T(8,128)S(1)}, u32[]{:S(2)}, u32[]{:S(2)}) %collective-permute-start.17) | collective-permute-done | bytes 262176 | tf_op jit(solution)/shard_map/ppermute | solution.py:19
  478.7 8.5 %collective-permute-done.18 = f32[256,256]{1,0:T(8,128)S(1)} collective-permute-done((f32[256,256]{1,0:T(8,128)S(1)}, f32[256,256]{1,0:T(8,128)S(1)}, u32[]{:S(2)}, u32[]{:S(2)}) %collective-permute-start.18) | collective-permute-done | bytes 262176 | tf_op jit(solution)/shard_map/ppermute | solution.py:19
  487.2 3.3 collective-permute-start.19
  490.5 4.9 collective-permute-done.19
  496.1 5.8 %collective-permute-done.20 = f32[256,256]{1,0:T(8,128)S(1)} collective-permute-done((f32[256,256]{1,0:T(8,128)S(1)}, f32[256,256]{1,0:T(8,128)S(1)}, u32[]{:S(2)}, u32[]{:S(2)}) %collective-permute-start.20) | collective-permute-done | bytes 262176 | tf_op jit(solution)/shard_map/ppermute | solution.py:19
  502.0 2.0 collective-permute-start.21
  503.9 6.0 %collective-permute-done.21 = f32[256,256]{1,0:T(8,128)S(1)} collective-permute-done((f32[256,256]{1,0:T(8,128)S(1)}, f32[256,256]{1,0:T(8,128)S(1)}, u32[]{:S(2)}, u32[]{:S(2)}) %collective-permute-start.21) | collective-permute-done | bytes 262176 | tf_op jit(solution)/shard_map/ppermute | solution.py:19
  510.8 15.9 %collective-permute-done.22 = f32[256,256]{1,0:T(8,128)S(1)} collective-permute-done((f32[256,256]{1,0:T(8,128)S(1)}, f32[256,256]{1,0:T(8,128)S(1)}, u32[]{:S(2)}, u32[]{:S(2)}) %collective-permute-start.22) | collective-permute-done | bytes 262176 | tf_op jit(solution)/shard_map/ppermute | solution.py:19
  526.7 2.6 collective-permute-start.23
  530.3 8.7 %collective-permute-done.23 = f32[256,256]{1,0:T(8,128)S(1)} collective-permute-done((f32[256,256]{1,0:T(8,128)S(1)}, f32[256,256]{1,0:T(8,128)S(1)}, u32[]{:S(2)}, u32[]{:S(2)}) %collective-permute-start.23) | collective-permute-done | bytes 262176 | tf_op jit(solution)/shard_map/ppermute | solution.py:19
  (122 shorter events, 35.1 us)
Async XLA Ops:
  0.6 325.3 %copy-start = (f32[1024,128]{1,0:T(8,128)S(1)}, f32[1024,128]{1,0:T(8,128)}, u32[]{:S(2)}) copy-start(f32[1024,128]{1,0:T(8,128)} %param.7) | copy-start | bytes 1572868
  23.1 67.6 %all-to-all-start = ((f32[16,1,65536]{2,1,0:T(1,128)}), f32[16,1,65536]{2,1,0:T(1,128)}, u32[]{:S(2)}, u32[]{:S(2)}) async-start(f32[16,1,65536]{2,1,0:T(1,128)} %reshape.54), calls=%async_computation | async-start | bytes 8388608 | tf_op jit(solution)/shard_map/all_to_all | solution.py:52
  131.3 7.6 %copy-start.1 = (f32[4,1024,256]{1,2,0:T(8,128)S(1)}, f32[4,1024,256]{1,2,0:T(8,128)}, u32[]{:S(2)}) copy-start(f32[4,1024,256]{1,2,0:T(8,128)} %reshape.32) | copy-start | bytes 12582916
  149.9 1.0 copy-start.3
  151.0 28.4 %collective-permute-start = (f32[2304,128]{1,0:T(8,128)S(1)}, f32[2304,128]{1,0:T(8,128)}, u32[]{:S(2)}, u32[]{:S(2)}) collective-permute-start(f32[2304,128]{1,0:T(8,128)S(1)} %broadcast_select_fusion), channel_id=1, source_target_pairs={{0,128},{16,144},{32,160},{48,176},{64,192},{80,208},{96,224},{112... | collective-permute-start | bytes 3538952 | tf_op jit(solution)/shard_map/ppermute | solution.py:42
  180.9 16.4 %collective-permute-start.1 = (f32[1152,128]{1,0:T(8,128)S(1)}, f32[1152,128]{1,0:T(8,128)S(1)}, u32[]{:S(2)}, u32[]{:S(2)}) collective-permute-start(f32[1152,128]{1,0:T(8,128)S(1)} %slice_select_fusion), channel_id=1, source_target_pairs={{0,64},{16,80},{32,96},{48,112},{64,0},{80,16},{96,32},{112,48},{1... | collective-permute-start | bytes 1769480 | tf_op jit(solution)/shard_map/ppermute | solution.py:42
  197.4 7.7 %collective-permute-start.2 = (f32[576,128]{1,0:T(8,128)S(1)}, f32[576,128]{1,0:T(8,128)S(1)}, u32[]{:S(2)}, u32[]{:S(2)}) collective-permute-start(f32[576,128]{1,0:T(8,128)S(1)} %slice_select_fusion.1), channel_id=1, source_target_pairs={{0,32},{16,48},{32,0},{48,16},{64,96},{80,112},{96,64},{112,80},{1... | collective-permute-start | bytes 884744 | tf_op jit(solution)/shard_map/ppermute | solution.py:42
  205.1 1.5 collective-permute-start.3
  206.6 9.8 %collective-permute-start.4 = (f32[144,128]{1,0:T(8,128)S(1)}, f32[144,128]{1,0:T(8,128)S(1)}, u32[]{:S(2)}, u32[]{:S(2)}) collective-permute-start(f32[144,128]{1,0:T(8,128)S(1)} %slice_select_fusion.3), channel_id=1, source_target_pairs={{0,8},{1,9},{2,10},{3,11},{4,12},{5,13},{6,14},{7,15},{8,0},{9,1},... | collective-permute-start | bytes 221192 | tf_op jit(solution)/shard_map/ppermute | solution.py:42
  216.4 6.0 %collective-permute-start.5 = (f32[72,128]{1,0:T(8,128)S(1)}, f32[72,128]{1,0:T(8,128)S(1)}, u32[]{:S(2)}, u32[]{:S(2)}) collective-permute-start(f32[72,128]{1,0:T(8,128)S(1)} %slice_select_fusion.4), channel_id=1, source_target_pairs={{0,4},{1,5},{2,6},{3,7},{4,0},{5,1},{6,2},{7,3},{8,12},{9,13},{10,... | collective-permute-start | bytes 110600 | tf_op jit(solution)/shard_map/ppermute | solution.py:42
  222.4 5.4 collective-permute-start.6
  227.8 3.8 collective-permute-start.7
  231.6 3.7 collective-permute-start.8
  235.3 5.4 collective-permute-start.9
  240.7 6.9 %collective-permute-start.10 = (f32[72,128]{1,0:T(8,128)S(1)}, f32[72,128]{1,0:T(8,128)S(1)}, u32[]{:S(2)}, u32[]{:S(2)}) collective-permute-start(f32[72,128]{1,0:T(8,128)S(1)} %maximum_select_fusion.6), channel_id=1, source_target_pairs={{0,4},{1,5},{2,6},{3,7},{4,0},{5,1},{6,2},{7,3},{8,12},{9,13},{10,... | collective-permute-start | bytes 110600 | tf_op jit(solution)/shard_map/ppermute | solution.py:45
  247.6 8.3 %collective-permute-start.11 = (f32[144,128]{1,0:T(8,128)S(1)}, f32[144,128]{1,0:T(8,128)S(1)}, u32[]{:S(2)}, u32[]{:S(2)}) collective-permute-start(f32[144,128]{1,0:T(8,128)S(1)} %maximum_select_fusion.5), channel_id=1, source_target_pairs={{0,8},{1,9},{2,10},{3,11},{4,12},{5,13},{6,14},{7,15},{8,0},{9,1},... | collective-permute-start | bytes 221192 | tf_op jit(solution)/shard_map/ppermute | solution.py:45
  255.9 1.5 collective-permute-start.12
  257.4 9.1 %collective-permute-start.13 = (f32[576,128]{1,0:T(8,128)S(1)}, f32[576,128]{1,0:T(8,128)S(1)}, u32[]{:S(2)}, u32[]{:S(2)}) collective-permute-start(f32[576,128]{1,0:T(8,128)S(1)} %maximum_select_fusion.3), channel_id=1, source_target_pairs={{0,32},{16,48},{32,0},{48,16},{64,96},{80,112},{96,64},{112,80},{1... | collective-permute-start | bytes 884744 | tf_op jit(solution)/shard_map/ppermute | solution.py:45
  266.6 16.5 %copy-start.4 = (s32[64]{0:T(128)S(1)}, s32[64]{0:T(128)}, u32[]{:S(2)}) copy-start(s32[64]{0:T(128)} %constant.219) | copy-start | bytes 772
  266.6 16.1 %collective-permute-start.14 = (f32[1152,128]{1,0:T(8,128)S(1)}, f32[1152,128]{1,0:T(8,128)S(1)}, u32[]{:S(2)}, u32[]{:S(2)}) collective-permute-start(f32[1152,128]{1,0:T(8,128)S(1)} %maximum_select_fusion.2), channel_id=1, source_target_pairs={{0,64},{16,80},{32,96},{48,112},{64,0},{80,16},{96,32},{112,48},{1... | collective-permute-start | bytes 1769480 | tf_op jit(solution)/shard_map/ppermute | solution.py:45
  282.8 26.4 %collective-permute-start.15 = (f32[2304,128]{1,0:T(8,128)S(1)}, f32[2304,128]{1,0:T(8,128)S(1)}, u32[]{:S(2)}, u32[]{:S(2)}) collective-permute-start(f32[2304,128]{1,0:T(8,128)S(1)} %maximum_select_fusion.1), channel_id=1, source_target_pairs={{0,128},{16,144},{32,160},{48,176},{64,192},{80,208},{96,224},{112... | collective-permute-start | bytes 3538952 | tf_op jit(solution)/shard_map/ppermute | solution.py:45
  325.9 3.5 copy-start.2
  468.0 1.6 collective-permute-start.16
  469.6 8.4 %collective-permute-start.17 = (f32[256,256]{1,0:T(8,128)S(1)}, f32[256,256]{1,0:T(8,128)S(1)}, u32[]{:S(2)}, u32[]{:S(2)}) collective-permute-start(f32[256,256]{1,0:T(8,128)S(1)} %add.124), channel_id=1, source_target_pairs={{0,32},{16,48},{32,0},{48,16},{64,96},{80,112},{96,64},{112,80},{1... | collective-permute-start | bytes 786440 | tf_op jit(solution)/shard_map/ppermute | solution.py:19
  478.1 9.1 %collective-permute-start.18 = (f32[256,256]{1,0:T(8,128)S(1)}, f32[256,256]{1,0:T(8,128)S(1)}, u32[]{:S(2)}, u32[]{:S(2)}) collective-permute-start(f32[256,256]{1,0:T(8,128)S(1)} %add.125), channel_id=1, source_target_pairs={{0,64},{16,80},{32,96},{48,112},{64,0},{80,16},{96,32},{112,48},{1... | collective-permute-start | bytes 786440 | tf_op jit(solution)/shard_map/ppermute | solution.py:19
  487.2 8.2 %collective-permute-start.19 = (f32[256,256]{1,0:T(8,128)S(1)}, f32[256,256]{1,0:T(8,128)S(1)}, u32[]{:S(2)}, u32[]{:S(2)}) collective-permute-start(f32[256,256]{1,0:T(8,128)S(1)} %add.126), channel_id=1, source_target_pairs={{0,128},{16,144},{32,160},{48,176},{64,192},{80,208},{96,224},{112... | collective-permute-start | bytes 786440 | tf_op jit(solution)/shard_map/ppermute | solution.py:19
  495.5 6.5 %collective-permute-start.20 = (f32[256,256]{1,0:T(8,128)S(1)}, f32[256,256]{1,0:T(8,128)S(1)}, u32[]{:S(2)}, u32[]{:S(2)}) collective-permute-start(f32[256,256]{1,0:T(8,128)S(1)} %add.127), channel_id=1, source_target_pairs={{0,1},{1,0},{2,3},{3,2},{4,5},{5,4},{6,7},{7,6},{8,9},{9,8},{10,11... | collective-permute-start | bytes 786440 | tf_op jit(solution)/shard_map/ppermute | solution.py:19
  502.0 8.0 %collective-permute-start.21 = (f32[256,256]{1,0:T(8,128)S(1)}, f32[256,256]{1,0:T(8,128)S(1)}, u32[]{:S(2)}, u32[]{:S(2)}) collective-permute-start(f32[256,256]{1,0:T(8,128)S(1)} %add.128), channel_id=1, source_target_pairs={{0,2},{1,3},{2,0},{3,1},{4,6},{5,7},{6,4},{7,5},{8,10},{9,11},{10,... | collective-permute-start | bytes 786440 | tf_op jit(solution)/shard_map/ppermute | solution.py:19
  510.0 16.7 %collective-permute-start.22 = (f32[256,256]{1,0:T(8,128)S(1)}, f32[256,256]{1,0:T(8,128)S(1)}, u32[]{:S(2)}, u32[]{:S(2)}) collective-permute-start(f32[256,256]{1,0:T(8,128)S(1)} %add.129), channel_id=1, source_target_pairs={{0,4},{1,5},{2,6},{3,7},{4,0},{5,1},{6,2},{7,3},{8,12},{9,13},{10,... | collective-permute-start | bytes 786440 | tf_op jit(solution)/shard_map/ppermute | solution.py:19
  526.7 12.3 %collective-permute-start.23 = (f32[256,256]{1,0:T(8,128)S(1)}, f32[256,256]{1,0:T(8,128)S(1)}, u32[]{:S(2)}, u32[]{:S(2)}) collective-permute-start(f32[256,256]{1,0:T(8,128)S(1)} %add.130), channel_id=1, source_target_pairs={{0,8},{1,9},{2,10},{3,11},{4,12},{5,13},{6,14},{7,15},{8,0},{9,1},... | collective-permute-start | bytes 786440 | tf_op jit(solution)/shard_map/ppermute | solution.py:19

commit v4 on v3

--- a/solution.py
+++ b/solution.py
@@ -76,12 +76,13 @@
               for col in range(n_blocks)] for row in range(n_blocks)]
     tiles = jnp.take(both, jnp.asarray(picks, jnp.int32), axis=0)
     gram_one = jnp.swapaxes(tiles, 1, 2).reshape(rows_x, rows_x)
-    basis = initial
-    for sweep_index in range(SWEEPS):
+    def sweep(sweep_index, basis):
         wide = jnp.dot(gram_one, basis, precision=highest, preferred_element_type=jnp.float32)
         square = jnp.dot(wide.T, wide, precision=highest, preferred_element_type=jnp.float32)
         factor_low = jnp.linalg.cholesky(square)
-        basis = jax.scipy.linalg.solve_triangular(factor_low, wide.T, lower=True).T
+        return jax.scipy.linalg.solve_triangular(factor_low, wide.T, lower=True).T
+
+    basis = lax.fori_loop(0, SWEEPS, sweep, initial)
     core_tensor = jnp.einsum("xr,sxc->src", basis, fibers, precision=highest)
     core_blocks = core_tensor.reshape(species, R, cols_y, slab_z)
     blocks = lax.all_to_all(core_blocks, "gy", split_axis=1, concat_axis=2, tiled=True)

time: 548 us -> 552 us (level)
    unnamed x47 -> x43, local copies, waits for them, and re-layouts: 37.9 us -> 38.9 us
where the time goes in v4:
time: 552 us; the launch traced here: 543 us
  waiting for transfers between devices  243 us (44%)
  other arithmetic  93 us (17%)
  local copies, waits for them, and re-layouts  84.5 us (15%)
  starting transfers between devices  50.6 us (9%)
  matrix products  46.4 us (8%)
  blocking collectives  23.4 us (4%)
    ppermute x8, waiting for transfers between devices, halving_doubling_sum(): other = lax.ppermute(value, axis, [(i, i ^ stride) for i in range(size)])  62.9 us
    all_to_all x1, waiting for transfers between devices, body(): lax.all_to_all(species_field, 'gx', split_axis=3, concat_axis=1, tiled=True)  61.1 us
    ppermute x8, waiting for transfers between devices, halving_doubling_sum(): lax.ppermute(send, axis, [(i, i ^ stride) for i in range(size)])  60.6 us
    ppermute x8, waiting for transfers between devices, butterfly_sum(): lax.ppermute(value, axis, [(i, i ^ stride) for i in range(size)])  58.5 us
    unnamed x43, local copies, waits for them, and re-layouts  38.9 us
    another operation x9, other arithmetic, sweep(): factor_low = jnp.linalg.cholesky(square)  37.4 us
    another operation x6, other arithmetic, sweep(): return jax.scipy.linalg.solve_triangular(factor_low, wide.T, lower=True).T  31.5 us
    all_to_all x1, blocking collectives, body(): lax.all_to_all(core_blocks, 'gy', split_axis=1, concat_axis=2, tiled=True)  23.4 us
  transfers between devices with their start and end apart: 25, of which 25 were waited for; matrix products, arithmetic and copies ran while one was open for 0% of the time, Pallas kernels for 0%

profile of v4, /device:TPU:6, one launch (start us, length us, event | category | flops | bytes accessed | tf_op | source)
XLA Modules:
  0.0 543.3 jit_solution(18318209025834888931)
XLA Ops:
  0.6 9.1 %copy.61 = f32[4,64,16,256]{1,2,0,3:T(8,128)} copy(f32[4,64,16,256]{3,2,1,0:T(8,128)} %param.5) | data formatting | bytes 8388608 | tf_op args[0]
  9.7 13.3 %reshape.56 = f32[16,1,65536]{2,1,0:T(1,128)} reshape(f32[256,4,16,64]{3,2,1,0:T(8,128)} %bitcast.108) | data formatting | bytes 8388608
  23.0 6.5 %all-to-all-start = ((f32[16,1,65536]{2,1,0:T(1,128)}), f32[16,1,65536]{2,1,0:T(1,128)}, u32[]{:S(2)}, u32[]{:S(2)}) async-start(f32[16,1,65536]{2,1,0:T(1,128)} %reshape.56), calls=%async_computation | async-start | bytes 8388608 | tf_op jit(solution)/shard_map/all_to_all | solution.py:52
  29.5 61.1 %all-to-all-done = f32[16,1,65536]{2,1,0:T(1,128)} async-done(((f32[16,1,65536]{2,1,0:T(1,128)}), f32[16,1,65536]{2,1,0:T(1,128)}, u32[]{:S(2)}, u32[]{:S(2)}) %all-to-all-start) | async-done | bytes 4194336 | tf_op jit(solution)/shard_map/all_to_all | solution.py:52
  91.1 13.7 %reduce.6 = f32[16,65536]{1,0:T(8,128)} reduce(f32[16,1,65536]{2,1,0:T(1,128)} %all-to-all-done, f32[]{:T(128)} %broadcast.87), dimensions={1}, to_apply=%all_to_all.24.reduce_sub_computation | reduce | bytes 8388612 | tf_op jit(solution)/shard_map/all_to_all | solution.py:52
  104.8 6.9 %reshape.57 = f32[256,4,16,64]{3,2,1,0:T(8,128)} reshape(f32[16,65536]{1,0:T(8,128)} %reduce.6) | data formatting | bytes 8388608
  111.7 11.5 %copy.63 = f32[4,16,64,16,16]{2,1,4,3,0:T(8,128)} copy(f32[4,16,64,16,16]{2,3,0,4,1:T(8,128)} %bitcast.109) | data formatting | bytes 8388608 | tf_op jit(solution)/shard_map/all_to_all | solution.py:52
  123.1 7.8 %reshape.34 = f32[4,1024,256]{1,2,0:T(8,128)} reshape(f32[4,16,64,16,16]{2,1,4,3,0:T(8,128)} %copy.63) | data formatting | bytes 8388608 | tf_op jit(solution)/shard_map/reshape | solution.py:54
  130.9 2.6 fusion.46
  133.5 2.4 fusion.48
  135.9 2.8 fusion.43
  144.1 2.4 fusion.21
  146.5 2.9 fusion.14
  151.8 26.8 %collective-permute-done = f32[2304,128]{1,0:T(8,128)} collective-permute-done((f32[2304,128]{1,0:T(8,128)S(1)}, f32[2304,128]{1,0:T(8,128)}, u32[]{:S(2)}, u32[]{:S(2)}) %collective-permute-start) | collective-permute-done | bytes 1179680 | tf_op jit(solution)/shard_map/ppermute | solution.py:42
  180.2 16.2 %collective-permute-done.1 = f32[1152,128]{1,0:T(8,128)S(1)} collective-permute-done((f32[1152,128]{1,0:T(8,128)S(1)}, f32[1152,128]{1,0:T(8,128)S(1)}, u32[]{:S(2)}, u32[]{:S(2)}) %collective-permute-start.1) | collective-permute-done | bytes 589856 | tf_op jit(solution)/shard_map/ppermute | solution.py:42
  196.7 7.6 %collective-permute-done.2 = f32[576,128]{1,0:T(8,128)S(1)} collective-permute-done((f32[576,128]{1,0:T(8,128)S(1)}, f32[576,128]{1,0:T(8,128)S(1)}, u32[]{:S(2)}, u32[]{:S(2)}) %collective-permute-start.2) | collective-permute-done | bytes 294944 | tf_op jit(solution)/shard_map/ppermute | solution.py:42
  205.8 7.1 %collective-permute-start.4 = (f32[144,128]{1,0:T(8,128)S(1)}, f32[144,128]{1,0:T(8,128)S(1)}, u32[]{:S(2)}, u32[]{:S(2)}) collective-permute-start(f32[144,128]{1,0:T(8,128)S(1)} %slice_select_fusion.3), channel_id=1, source_target_pairs={{0,8},{1,9},{2,10},{3,11},{4,12},{5,13},{6,14},{7,15},{8,0},{9,1},... | collective-permute-start | bytes 221192 | tf_op jit(solution)/shard_map/ppermute | solution.py:42
  212.9 2.7 collective-permute-done.4
  215.6 4.0 collective-permute-start.5
  221.6 3.3 collective-permute-start.6
  225.0 2.1 collective-permute-done.6
  228.7 2.1 collective-permute-done.7
  232.4 2.1 collective-permute-done.8
  234.5 3.3 collective-permute-start.9
  237.8 2.1 collective-permute-done.9
  239.9 3.1 collective-permute-start.10
  243.0 3.4 collective-permute-done.10
  246.4 4.6 collective-permute-start.11
  251.1 3.7 collective-permute-done.11
  256.6 8.8 %collective-permute-done.13 = f32[576,128]{1,0:T(8,128)S(1)} collective-permute-done((f32[576,128]{1,0:T(8,128)S(1)}, f32[576,128]{1,0:T(8,128)S(1)}, u32[]{:S(2)}, u32[]{:S(2)}) %collective-permute-start.13) | collective-permute-done | bytes 294944 | tf_op jit(solution)/shard_map/ppermute | solution.py:45
  266.1 15.5 %collective-permute-done.14 = f32[1152,128]{1,0:T(8,128)S(1)} collective-permute-done((f32[1152,128]{1,0:T(8,128)S(1)}, f32[1152,128]{1,0:T(8,128)S(1)}, u32[]{:S(2)}, u32[]{:S(2)}) %collective-permute-start.14) | collective-permute-done | bytes 589856 | tf_op jit(solution)/shard_map/ppermute | solution.py:45
  282.0 26.1 %collective-permute-done.15 = f32[2304,128]{1,0:T(8,128)S(1)} collective-permute-done((f32[2304,128]{1,0:T(8,128)S(1)}, f32[2304,128]{1,0:T(8,128)S(1)}, u32[]{:S(2)}, u32[]{:S(2)}) %collective-permute-start.15) | collective-permute-done | bytes 1179680 | tf_op jit(solution)/shard_map/ppermute | solution.py:45
  308.3 2.1 copy.79
  310.5 4.3 pad_maximum_fusion
  314.8 5.2 gather_fusion
  320.0 4.6 copy.80
  324.6 3.0 copy.110
  327.6 89.9 %while.10 = (s32[]{:T(128)}, f32[1024,128]{1,0:T(8,128)S(1)}, f32[1024,1024]{1,0:T(8,128)}, s32[]{:T(128)}) while((s32[]{:T(128)}, f32[1024,128]{1,0:T(8,128)S(1)}, f32[1024,1024]{1,0:T(8,128)}, s32[]{:T(128)}) %tuple.29), condition=%wide.region_3.4_spmd, body=%wide.region_0.3_spmd.sunk | while | flops 2013413504 | bytes 7472183 | solution.py:85
  327.6 5.2 fusion.87
  333.9 11.7 %cholesky.58 = f32[128,128]{1,0:T(8,128)S(1)} custom-call(f32[128,128]{1,0:T(8,128)S(1)} %fusion.89), custom_call_target="Cholesky" | custom-call | tf_op jit(solution)/shard_map/while/body/eval_jaxpr/jit(cholesky)/cholesky | solution.py:82
  347.1 9.8 %custom-call.14 = f32[1,128,128]{1,2,0:T(8,128)S(1)} custom-call(f32[1,128,128]{2,1,0:T(8,128)S(1)} %fusion.90), custom_call_target="InvertDiagBlocksLowerTriangular" | custom-call | tf_op jit(solution)/shard_map/while/body/eval_jaxpr/jit(_solve_triangular)/triangular_solve | solution.py:83
  357.5 5.2 fusion.87
  363.8 11.7 %cholesky.58 = f32[128,128]{1,0:T(8,128)S(1)} custom-call(f32[128,128]{1,0:T(8,128)S(1)} %fusion.89), custom_call_target="Cholesky" | custom-call | tf_op jit(solution)/shard_map/while/body/eval_jaxpr/jit(cholesky)/cholesky | solution.py:82
  377.0 9.8 %custom-call.14 = f32[1,128,128]{1,2,0:T(8,128)S(1)} custom-call(f32[1,128,128]{2,1,0:T(8,128)S(1)} %fusion.90), custom_call_target="InvertDiagBlocksLowerTriangular" | custom-call | tf_op jit(solution)/shard_map/while/body/eval_jaxpr/jit(_solve_triangular)/triangular_solve | solution.py:83
  387.4 5.2 fusion.87
  393.7 11.7 %cholesky.58 = f32[128,128]{1,0:T(8,128)S(1)} custom-call(f32[128,128]{1,0:T(8,128)S(1)} %fusion.89), custom_call_target="Cholesky" | custom-call | tf_op jit(solution)/shard_map/while/body/eval_jaxpr/jit(cholesky)/cholesky | solution.py:82
  406.9 9.8 %custom-call.14 = f32[1,128,128]{1,2,0:T(8,128)S(1)} custom-call(f32[1,128,128]{2,1,0:T(8,128)S(1)} %fusion.90), custom_call_target="InvertDiagBlocksLowerTriangular" | custom-call | tf_op jit(solution)/shard_map/while/body/eval_jaxpr/jit(_solve_triangular)/triangular_solve | solution.py:83
  417.5 6.7 %convolution_bitcast_fusion = f32[4,128,256]{2,1,0:T(8,128)S(1)} fusion(f32[4,1024,256]{1,2,0:T(8,128)} %reshape.34, f32[1024,128]{1,0:T(8,128)S(1)} %get-tuple-element.19), kind=kOutput, calls=%fused_computation.24 | convolution fusion | flops 1610612736 | bytes 5242880 | tf_op jit(solution)/shard_map/xr,sxc->src/dot_general | solution.py:86
  424.3 4.4 copy.84
  428.8 3.5 reshape.58
  432.3 23.4 %all_to_all.33 = f32[16,1,8192]{2,1,0:T(1,128)S(1)} all-to-all(f32[16,1,8192]{2,1,0:T(1,128)S(1)} %reshape.58), channel_id=1, replica_groups=mesh['gx'=16,'gy'=16] {'gy'}, dimensions={0} | all-to-all | bytes 1048576 | tf_op jit(solution)/shard_map/all_to_all | solution.py:88
  457.6 2.8 reshape.59
  460.4 5.6 %copy.86 = f32[4,8,16,16,16]{3,2,4,0,1:T(8,128)} copy(f32[4,8,16,16,16]{4,3,0,1,2:T(8,128)} %bitcast.114) | data formatting | bytes 1048576 | tf_op jit(solution)/shard_map/all_to_all | solution.py:88
  466.0 3.5 all_to_all.30
  472.6 8.1 %collective-permute-done.17 = f32[256,256]{1,0:T(8,128)S(1)} collective-permute-done((f32[256,256]{1,0:T(8,128)S(1)}, f32[256,256]{1,0:T(8,128)S(1)}, u32[]{:S(2)}, u32[]{:S(2)}) %collective-permute-start.17) | collective-permute-done | bytes 262176 | tf_op jit(solution)/shard_map/ppermute | solution.py:19
  481.6 8.4 %collective-permute-done.18 = f32[256,256]{1,0:T(8,128)S(1)} collective-permute-done((f32[256,256]{1,0:T(8,128)S(1)}, f32[256,256]{1,0:T(8,128)S(1)}, u32[]{:S(2)}, u32[]{:S(2)}) %collective-permute-start.18) | collective-permute-done | bytes 262176 | tf_op jit(solution)/shard_map/ppermute | solution.py:19
  490.0 2.9 collective-permute-start.19
  493.0 4.9 collective-permute-done.19
  498.5 5.8 %collective-permute-done.20 = f32[256,256]{1,0:T(8,128)S(1)} collective-permute-done((f32[256,256]{1,0:T(8,128)S(1)}, f32[256,256]{1,0:T(8,128)S(1)}, u32[]{:S(2)}, u32[]{:S(2)}) %collective-permute-start.20) | collective-permute-done | bytes 262176 | tf_op jit(solution)/shard_map/ppermute | solution.py:19
  504.4 2.3 collective-permute-start.21
  506.7 5.6 %collective-permute-done.21 = f32[256,256]{1,0:T(8,128)S(1)} collective-permute-done((f32[256,256]{1,0:T(8,128)S(1)}, f32[256,256]{1,0:T(8,128)S(1)}, u32[]{:S(2)}, u32[]{:S(2)}) %collective-permute-start.21) | collective-permute-done | bytes 262176 | tf_op jit(solution)/shard_map/ppermute | solution.py:19
  514.0 15.3 %collective-permute-done.22 = f32[256,256]{1,0:T(8,128)S(1)} collective-permute-done((f32[256,256]{1,0:T(8,128)S(1)}, f32[256,256]{1,0:T(8,128)S(1)}, u32[]{:S(2)}, u32[]{:S(2)}) %collective-permute-start.22) | collective-permute-done | bytes 262176 | tf_op jit(solution)/shard_map/ppermute | solution.py:19
  529.3 3.1 collective-permute-start.23
  533.3 8.9 %collective-permute-done.23 = f32[256,256]{1,0:T(8,128)S(1)} collective-permute-done((f32[256,256]{1,0:T(8,128)S(1)}, f32[256,256]{1,0:T(8,128)S(1)}, u32[]{:S(2)}, u32[]{:S(2)}) %collective-permute-start.23) | collective-permute-done | bytes 262176 | tf_op jit(solution)/shard_map/ppermute | solution.py:19
  (119 shorter events, 39.2 us)
Async XLA Ops:
  23.0 67.5 %all-to-all-start = ((f32[16,1,65536]{2,1,0:T(1,128)}), f32[16,1,65536]{2,1,0:T(1,128)}, u32[]{:S(2)}, u32[]{:S(2)}) async-start(f32[16,1,65536]{2,1,0:T(1,128)} %reshape.56), calls=%async_computation | async-start | bytes 8388608 | tf_op jit(solution)/shard_map/all_to_all | solution.py:52
  130.9 7.8 %copy-start = (f32[4,1024,256]{1,2,0:T(8,128)S(1)}, f32[4,1024,256]{1,2,0:T(8,128)}, u32[]{:S(2)}) copy-start(f32[4,1024,256]{1,2,0:T(8,128)} %reshape.34) | copy-start | bytes 12582916
  150.1 28.5 %collective-permute-start = (f32[2304,128]{1,0:T(8,128)S(1)}, f32[2304,128]{1,0:T(8,128)}, u32[]{:S(2)}, u32[]{:S(2)}) collective-permute-start(f32[2304,128]{1,0:T(8,128)S(1)} %broadcast_select_fusion), channel_id=1, source_target_pairs={{0,128},{16,144},{32,160},{48,176},{64,192},{80,208},{96,224},{112... | collective-permute-start | bytes 3538952 | tf_op jit(solution)/shard_map/ppermute | solution.py:42
  180.1 16.4 %collective-permute-start.1 = (f32[1152,128]{1,0:T(8,128)S(1)}, f32[1152,128]{1,0:T(8,128)S(1)}, u32[]{:S(2)}, u32[]{:S(2)}) collective-permute-start(f32[1152,128]{1,0:T(8,128)S(1)} %slice_select_fusion), channel_id=1, source_target_pairs={{0,64},{16,80},{32,96},{48,112},{64,0},{80,16},{96,32},{112,48},{1... | collective-permute-start | bytes 1769480 | tf_op jit(solution)/shard_map/ppermute | solution.py:42
  196.6 7.7 %collective-permute-start.2 = (f32[576,128]{1,0:T(8,128)S(1)}, f32[576,128]{1,0:T(8,128)S(1)}, u32[]{:S(2)}, u32[]{:S(2)}) collective-permute-start(f32[576,128]{1,0:T(8,128)S(1)} %slice_select_fusion.1), channel_id=1, source_target_pairs={{0,32},{16,48},{32,0},{48,16},{64,96},{80,112},{96,64},{112,80},{1... | collective-permute-start | bytes 884744 | tf_op jit(solution)/shard_map/ppermute | solution.py:42
  204.3 1.5 collective-permute-start.3
  205.8 9.8 %collective-permute-start.4 = (f32[144,128]{1,0:T(8,128)S(1)}, f32[144,128]{1,0:T(8,128)S(1)}, u32[]{:S(2)}, u32[]{:S(2)}) collective-permute-start(f32[144,128]{1,0:T(8,128)S(1)} %slice_select_fusion.3), channel_id=1, source_target_pairs={{0,8},{1,9},{2,10},{3,11},{4,12},{5,13},{6,14},{7,15},{8,0},{9,1},... | collective-permute-start | bytes 221192 | tf_op jit(solution)/shard_map/ppermute | solution.py:42
  215.6 6.0 %collective-permute-start.5 = (f32[72,128]{1,0:T(8,128)S(1)}, f32[72,128]{1,0:T(8,128)S(1)}, u32[]{:S(2)}, u32[]{:S(2)}) collective-permute-start(f32[72,128]{1,0:T(8,128)S(1)} %slice_select_fusion.4), channel_id=1, source_target_pairs={{0,4},{1,5},{2,6},{3,7},{4,0},{5,1},{6,2},{7,3},{8,12},{9,13},{10,... | collective-permute-start | bytes 110600 | tf_op jit(solution)/shard_map/ppermute | solution.py:42
  221.6 5.4 collective-permute-start.6
  227.0 3.8 collective-permute-start.7
  230.8 3.7 collective-permute-start.8
  234.5 5.4 collective-permute-start.9
  239.9 6.5 %collective-permute-start.10 = (f32[72,128]{1,0:T(8,128)S(1)}, f32[72,128]{1,0:T(8,128)S(1)}, u32[]{:S(2)}, u32[]{:S(2)}) collective-permute-start(f32[72,128]{1,0:T(8,128)S(1)} %maximum_select_fusion.6), channel_id=1, source_target_pairs={{0,4},{1,5},{2,6},{3,7},{4,0},{5,1},{6,2},{7,3},{8,12},{9,13},{10,... | collective-permute-start | bytes 110600 | tf_op jit(solution)/shard_map/ppermute | solution.py:45
  246.4 8.3 %collective-permute-start.11 = (f32[144,128]{1,0:T(8,128)S(1)}, f32[144,128]{1,0:T(8,128)S(1)}, u32[]{:S(2)}, u32[]{:S(2)}) collective-permute-start(f32[144,128]{1,0:T(8,128)S(1)} %maximum_select_fusion.5), channel_id=1, source_target_pairs={{0,8},{1,9},{2,10},{3,11},{4,12},{5,13},{6,14},{7,15},{8,0},{9,1},... | collective-permute-start | bytes 221192 | tf_op jit(solution)/shard_map/ppermute | solution.py:45
  254.8 1.5 collective-permute-start.12
  256.3 9.1 %collective-permute-start.13 = (f32[576,128]{1,0:T(8,128)S(1)}, f32[576,128]{1,0:T(8,128)S(1)}, u32[]{:S(2)}, u32[]{:S(2)}) collective-permute-start(f32[576,128]{1,0:T(8,128)S(1)} %maximum_select_fusion.3), channel_id=1, source_target_pairs={{0,32},{16,48},{32,0},{48,16},{64,96},{80,112},{96,64},{112,80},{1... | collective-permute-start | bytes 884744 | tf_op jit(solution)/shard_map/ppermute | solution.py:45
  265.5 16.5 %copy-start.2 = (s32[64]{0:T(128)S(1)}, s32[64]{0:T(128)}, u32[]{:S(2)}) copy-start(s32[64]{0:T(128)} %constant.236) | copy-start | bytes 772
  265.5 16.1 %collective-permute-start.14 = (f32[1152,128]{1,0:T(8,128)S(1)}, f32[1152,128]{1,0:T(8,128)S(1)}, u32[]{:S(2)}, u32[]{:S(2)}) collective-permute-start(f32[1152,128]{1,0:T(8,128)S(1)} %maximum_select_fusion.2), channel_id=1, source_target_pairs={{0,64},{16,80},{32,96},{48,112},{64,0},{80,16},{96,32},{112,48},{1... | collective-permute-start | bytes 1769480 | tf_op jit(solution)/shard_map/ppermute | solution.py:45
  281.7 26.4 %collective-permute-start.15 = (f32[2304,128]{1,0:T(8,128)S(1)}, f32[2304,128]{1,0:T(8,128)S(1)}, u32[]{:S(2)}, u32[]{:S(2)}) collective-permute-start(f32[2304,128]{1,0:T(8,128)S(1)} %maximum_select_fusion.1), channel_id=1, source_target_pairs={{0,128},{16,144},{32,160},{48,176},{64,192},{80,208},{96,224},{112... | collective-permute-start | bytes 3538952 | tf_op jit(solution)/shard_map/ppermute | solution.py:45
  324.6 3.0 copy-start.1
  470.5 1.6 collective-permute-start.16
  472.2 8.4 %collective-permute-start.17 = (f32[256,256]{1,0:T(8,128)S(1)}, f32[256,256]{1,0:T(8,128)S(1)}, u32[]{:S(2)}, u32[]{:S(2)}) collective-permute-start(f32[256,256]{1,0:T(8,128)S(1)} %add.130), channel_id=1, source_target_pairs={{0,32},{16,48},{32,0},{48,16},{64,96},{80,112},{96,64},{112,80},{1... | collective-permute-start | bytes 786440 | tf_op jit(solution)/shard_map/ppermute | solution.py:19
  480.7 9.3 %collective-permute-start.18 = (f32[256,256]{1,0:T(8,128)S(1)}, f32[256,256]{1,0:T(8,128)S(1)}, u32[]{:S(2)}, u32[]{:S(2)}) collective-permute-start(f32[256,256]{1,0:T(8,128)S(1)} %add.131), channel_id=1, source_target_pairs={{0,64},{16,80},{32,96},{48,112},{64,0},{80,16},{96,32},{112,48},{1... | collective-permute-start | bytes 786440 | tf_op jit(solution)/shard_map/ppermute | solution.py:19
  490.0 7.8 %collective-permute-start.19 = (f32[256,256]{1,0:T(8,128)S(1)}, f32[256,256]{1,0:T(8,128)S(1)}, u32[]{:S(2)}, u32[]{:S(2)}) collective-permute-start(f32[256,256]{1,0:T(8,128)S(1)} %add.132), channel_id=1, source_target_pairs={{0,128},{16,144},{32,160},{48,176},{64,192},{80,208},{96,224},{112... | collective-permute-start | bytes 786440 | tf_op jit(solution)/shard_map/ppermute | solution.py:19
  497.9 6.5 %collective-permute-start.20 = (f32[256,256]{1,0:T(8,128)S(1)}, f32[256,256]{1,0:T(8,128)S(1)}, u32[]{:S(2)}, u32[]{:S(2)}) collective-permute-start(f32[256,256]{1,0:T(8,128)S(1)} %add.133), channel_id=1, source_target_pairs={{0,1},{1,0},{2,3},{3,2},{4,5},{5,4},{6,7},{7,6},{8,9},{9,8},{10,11... | collective-permute-start | bytes 786440 | tf_op jit(solution)/shard_map/ppermute | solution.py:19
  504.4 8.0 %collective-permute-start.21 = (f32[256,256]{1,0:T(8,128)S(1)}, f32[256,256]{1,0:T(8,128)S(1)}, u32[]{:S(2)}, u32[]{:S(2)}) collective-permute-start(f32[256,256]{1,0:T(8,128)S(1)} %add.134), channel_id=1, source_target_pairs={{0,2},{1,3},{2,0},{3,1},{4,6},{5,7},{6,4},{7,5},{8,10},{9,11},{10,... | collective-permute-start | bytes 786440 | tf_op jit(solution)/shard_map/ppermute | solution.py:19
  512.4 16.9 %collective-permute-start.22 = (f32[256,256]{1,0:T(8,128)S(1)}, f32[256,256]{1,0:T(8,128)S(1)}, u32[]{:S(2)}, u32[]{:S(2)}) collective-permute-start(f32[256,256]{1,0:T(8,128)S(1)} %add.135), channel_id=1, source_target_pairs={{0,4},{1,5},{2,6},{3,7},{4,0},{5,1},{6,2},{7,3},{8,12},{9,13},{10,... | collective-permute-start | bytes 786440 | tf_op jit(solution)/shard_map/ppermute | solution.py:19
  529.3 12.8 %collective-permute-start.23 = (f32[256,256]{1,0:T(8,128)S(1)}, f32[256,256]{1,0:T(8,128)S(1)}, u32[]{:S(2)}, u32[]{:S(2)}) collective-permute-start(f32[256,256]{1,0:T(8,128)S(1)} %add.136), channel_id=1, source_target_pairs={{0,8},{1,9},{2,10},{3,11},{4,12},{5,13},{6,14},{7,15},{8,0},{9,1},... | collective-permute-start | bytes 786440 | tf_op jit(solution)/shard_map/ppermute | solution.py:19

commit v5 on v3

--- a/solution.py
+++ b/solution.py
@@ -49,9 +49,11 @@
 
 def body(species_field, initial):
     highest = lax.Precision.HIGHEST
-    regrouped = lax.all_to_all(species_field, "gx", split_axis=3, concat_axis=1, tiled=True)
-    species, rows_x, cols_y, slab_z = regrouped.shape
-    fibers = regrouped.reshape(species, rows_x, cols_y * slab_z)
+    by_row = jnp.moveaxis(species_field, 2, 0)
+    regrouped = lax.all_to_all(by_row, "gx", split_axis=0, concat_axis=0, tiled=True)
+    x_blocks, species, block_x, slab_z = regrouped.shape
+    rows_x = x_blocks * block_x
+    fibers = jnp.swapaxes(regrouped, 0, 1).reshape(species, rows_x, slab_z)
     scale_one = 1.0 / (S * NY * NZ)
     n_blocks = rows_x // BLOCK
     lower = []
@@ -83,9 +85,14 @@
         factor_low = jnp.linalg.cholesky(square)
         basis = jax.scipy.linalg.solve_triangular(factor_low, wide.T, lower=True).T
     core_tensor = jnp.einsum("xr,sxc->src", basis, fibers, precision=highest)
-    core_blocks = core_tensor.reshape(species, R, cols_y, slab_z)
-    blocks = lax.all_to_all(core_blocks, "gy", split_axis=1, concat_axis=2, tiled=True)
-    second_part = jnp.einsum("sryz,srwz->yw", blocks, blocks, precision=highest) / (S * R * NZ)
+    n_gy = lax.axis_size("gy")
+    n_gx = lax.axis_size("gx")
+    by_rank = jnp.swapaxes(core_tensor.reshape(species, n_gy, R // n_gy, slab_z), 0, 1)
+    stage_one = lax.all_to_all(by_rank, "gy", split_axis=0, concat_axis=0, tiled=True)
+    pairs = stage_one.reshape(n_gy, n_gx, species * (R // n_gy) // n_gx, slab_z)
+    stage_two = lax.all_to_all(jnp.swapaxes(pairs, 0, 1), "gx", split_axis=0, concat_axis=0, tiled=True)
+    columns = jnp.swapaxes(stage_two, 0, 1).reshape(n_gy * n_gx, -1)
+    second_part = jnp.einsum("yc,wc->yw", columns, columns, precision=highest) / (S * R * NZ)
     gram_two = butterfly_sum(second_part, "gx", lax.axis_size("gx"))
     gram_two = butterfly_sum(gram_two, "gy", lax.axis_size("gy"))
     return (basis * math.sqrt(rows_x), gram_two)

time: 548 us -> 483 us (0.88)
  local copies, waits for them, and re-layouts: 84.1 us -> 24.3 us
  blocking collectives: 22.9 us -> 38.6 us
  other arithmetic: 92.1 us -> 76.6 us
    unnamed x47 -> x44, local copies, waits for them, and re-layouts: 37.9 us -> 8.88 us
    all_to_all x4 -> x1, local copies, waits for them, and re-layouts: 21.1 us -> 0.31 us  [body(): lax.all_to_all(by_rank, 'gy', split_axis=0, concat_axis=0, tiled=True)]
    all_to_all x1 -> x2, blocking collectives: 22.9 us -> 38.6 us  [the longest x1 22.9 us: body(): lax.all_to_all(by_rank, 'gy', split_axis=0, concat_axis=0, tiled=True)]
    all_to_all x2 -> x0, other arithmetic: 15.6 us -> none  [the longest x1 13.7 us: body(): lax.all_to_all(species_field, 'gx', split_axis=3, concat_axis=1, tiled=True)]
    reshape x2 -> x1, local copies, waits for them, and re-layouts: 12.6 us -> 0.04 us  [body(): core_tensor.reshape(species, n_gy, R // n_gy, slab_z)]
where the time goes in v5:
time: 483 us; the launch traced here: 479 us
  waiting for transfers between devices  247 us (51%)
  other arithmetic  76.6 us (16%)
  starting transfers between devices  46 us (10%)
  matrix products  45.3 us (9%)
  blocking collectives  38.6 us (8%)
  local copies, waits for them, and re-layouts  24.3 us (5%)
    ppermute x8, waiting for transfers between devices, halving_doubling_sum(): other = lax.ppermute(value, axis, [(i, i ^ stride) for i in range(size)])  63.8 us
    ppermute x8, waiting for transfers between devices, butterfly_sum(): lax.ppermute(value, axis, [(i, i ^ stride) for i in range(size)])  61.5 us
    all_to_all x1, waiting for transfers between devices, body(): lax.all_to_all(by_row, 'gx', split_axis=0, concat_axis=0, tiled=True)  60.9 us
    ppermute x8, waiting for transfers between devices, halving_doubling_sum(): lax.ppermute(send, axis, [(i, i ^ stride) for i in range(size)])  60.7 us
    another operation x9, other arithmetic, body(): factor_low = jnp.linalg.cholesky(square)  37.2 us
    another operation x6, other arithmetic, body(): basis = jax.scipy.linalg.solve_triangular(factor_low, wide.T, lower=True).T  31.8 us
    all_to_all x1, blocking collectives, body(): lax.all_to_all(by_rank, 'gy', split_axis=0, concat_axis=0, tiled=True)  22.9 us
    dot_general x8, matrix products, body(): jnp.einsum('sxc,swc->xw', fibers[:, row * BLOCK:(row + 1) * BLOCK], fiber...  20.1 us
  transfers between devices with their start and end apart: 25, of which 25 were waited for; matrix products, arithmetic and copies ran while one was open for 0% of the time, Pallas kernels for 0%

profile of v5, /device:TPU:6, one launch (start us, length us, event | category | flops | bytes accessed | tf_op | source)
XLA Modules:
  0.0 479.5 jit_solution(2897865221888869533)
XLA Ops:
  0.6 6.7 %copy.54 = f32[4,64,16,256]{3,1,0,2:T(8,128)} copy(f32[4,64,16,256]{3,2,1,0:T(8,128)} %param.6) | data formatting | bytes 8388608 | tf_op args[0]
  7.3 6.6 %all-to-all-start = ((f32[16,4,64,256]{3,2,1,0:T(8,128)}), f32[16,4,64,256]{3,2,1,0:T(8,128)}, u32[]{:S(2)}, u32[]{:S(2)}) async-start(f32[16,4,64,256]{3,2,1,0:T(8,128)} %bitcast.135), calls=%async_computation | async-start | bytes 8388608 | tf_op jit(solution)/shard_map/all_to_all | solution.py:53
  14.0 60.9 %all-to-all-done = f32[16,4,64,256]{3,2,1,0:T(8,128)} async-done(((f32[16,4,64,256]{3,2,1,0:T(8,128)}), f32[16,4,64,256]{3,2,1,0:T(8,128)}, u32[]{:S(2)}, u32[]{:S(2)}) %all-to-all-start) | async-done | bytes 4194336 | tf_op jit(solution)/shard_map/all_to_all | solution.py:53
  74.8 2.5 copy.28
  77.3 1.2 fusion.50
  79.1 1.5 fusion.47
  80.6 2.3 fusion.41
  82.9 2.7 fusion.38
  85.6 3.3 fusion.32
  88.9 4.1 fusion.26
  93.0 4.4 fusion.19
  99.1 1.6 collective-permute-start
  100.7 26.8 %collective-permute-done = f32[2304,128]{1,0:T(8,128)} collective-permute-done((f32[2304,128]{1,0:T(8,128)S(1)}, f32[2304,128]{1,0:T(8,128)}, u32[]{:S(2)}, u32[]{:S(2)}) %collective-permute-start) | collective-permute-done | bytes 1179680 | tf_op jit(solution)/shard_map/ppermute | solution.py:42
  127.4 1.4 select_add_fusion
  129.1 16.2 %collective-permute-done.1 = f32[1152,128]{1,0:T(8,128)S(1)} collective-permute-done((f32[1152,128]{1,0:T(8,128)S(1)}, f32[1152,128]{1,0:T(8,128)S(1)}, u32[]{:S(2)}, u32[]{:S(2)}) %collective-permute-start.1) | collective-permute-done | bytes 589856 | tf_op jit(solution)/shard_map/ppermute | solution.py:42
  145.5 7.6 %collective-permute-done.2 = f32[576,128]{1,0:T(8,128)S(1)} collective-permute-done((f32[576,128]{1,0:T(8,128)S(1)}, f32[576,128]{1,0:T(8,128)S(1)}, u32[]{:S(2)}, u32[]{:S(2)}) %collective-permute-start.2) | collective-permute-done | bytes 294944 | tf_op jit(solution)/shard_map/ppermute | solution.py:42
  153.3 1.3 collective-permute-done.3
  154.7 7.2 %collective-permute-start.4 = (f32[144,128]{1,0:T(8,128)S(1)}, f32[144,128]{1,0:T(8,128)S(1)}, u32[]{:S(2)}, u32[]{:S(2)}) collective-permute-start(f32[144,128]{1,0:T(8,128)S(1)} %slice_select_fusion.3), channel_id=1, source_target_pairs={{0,8},{1,9},{2,10},{3,11},{4,12},{5,13},{6,14},{7,15},{8,0},{9,1},... | collective-permute-start | bytes 221192 | tf_op jit(solution)/shard_map/ppermute | solution.py:42
  161.8 2.7 collective-permute-done.4
  164.5 4.0 collective-permute-start.5
  168.6 1.9 collective-permute-done.5
  170.5 3.3 collective-permute-start.6
  173.8 2.1 collective-permute-done.6
  175.9 1.7 collective-permute-start.7
  177.6 2.1 collective-permute-done.7
  179.7 1.6 collective-permute-start.8
  181.3 2.1 collective-permute-done.8
  183.4 3.3 collective-permute-start.9
  186.7 2.1 collective-permute-done.9
  188.8 3.0 collective-permute-start.10
  191.9 3.8 collective-permute-done.10
  195.7 4.3 collective-permute-start.11
  200.0 4.1 collective-permute-done.11
  204.2 1.4 collective-permute-done.12
  205.9 8.8 %collective-permute-done.13 = f32[576,128]{1,0:T(8,128)S(1)} collective-permute-done((f32[576,128]{1,0:T(8,128)S(1)}, f32[576,128]{1,0:T(8,128)S(1)}, u32[]{:S(2)}, u32[]{:S(2)}) %collective-permute-start.13) | collective-permute-done | bytes 294944 | tf_op jit(solution)/shard_map/ppermute | solution.py:45
  215.4 15.5 %collective-permute-done.14 = f32[1152,128]{1,0:T(8,128)S(1)} collective-permute-done((f32[1152,128]{1,0:T(8,128)S(1)}, f32[1152,128]{1,0:T(8,128)S(1)}, u32[]{:S(2)}, u32[]{:S(2)}) %collective-permute-start.14) | collective-permute-done | bytes 589856 | tf_op jit(solution)/shard_map/ppermute | solution.py:45
  231.3 26.1 %collective-permute-done.15 = f32[2304,128]{1,0:T(8,128)S(1)} collective-permute-done((f32[2304,128]{1,0:T(8,128)S(1)}, f32[2304,128]{1,0:T(8,128)S(1)}, u32[]{:S(2)}, u32[]{:S(2)}) %collective-permute-start.15) | collective-permute-done | bytes 1179680 | tf_op jit(solution)/shard_map/ppermute | solution.py:45
  257.6 2.1 copy.29
  259.8 4.3 pad_maximum_fusion
  264.0 5.2 %gather_fusion = f32[64,128,128]{2,1,0:T(8,128)} fusion(f32[72,128,128]{2,1,0:T(8,128)} %pad_maximum_fusion, s32[1024]{0:T(1024)S(1)} %pad_clamp_fusion), kind=kCustom, calls=%fused_computation | custom fusion | bytes 8388864 | tf_op jit(solution)/shard_map/jit(_take)/gather | solution.py:79
  269.2 4.6 copy.30
  273.8 3.5 fusion.4
  277.3 1.0 fusion.82
  278.4 11.7 %cholesky.59 = f32[128,128]{1,0:T(8,128)S(1)} custom-call(f32[128,128]{1,0:T(8,128)S(1)} %fusion.77), custom_call_target="Cholesky" | custom-call | tf_op jit(solution)/shard_map/jit(cholesky)/cholesky | solution.py:85
  291.5 10.2 %custom-call.7 = f32[1,128,128]{1,2,0:T(8,128)S(1)} custom-call(f32[1,128,128]{2,1,0:T(8,128)S(1)} %fusion.69), custom_call_target="InvertDiagBlocksLowerTriangular" | custom-call | tf_op jit(solution)/shard_map/jit(_solve_triangular)/triangular_solve | solution.py:86
  302.3 5.7 %fusion.2 = f32[1024,128]{1,0:T(8,128)S(1)} fusion(f32[128,1024]{1,0:T(8,128)S(1)} %fusion.67, f32[128,8,8,128]{3,2,1,0:T(8,128)} %bitcast.131), kind=kOutput, calls=%fused_computation.4 | convolution fusion | flops 1610612736 | bytes 5242880 | tf_op jit(solution)/shard_map/dot_general | solution.py:83
  309.2 11.7 %cholesky.70 = f32[128,128]{1,0:T(8,128)S(1)} custom-call(f32[128,128]{1,0:T(8,128)S(1)} %fusion.75), custom_call_target="Cholesky" | custom-call | tf_op jit(solution)/shard_map/jit(cholesky)/cholesky | solution.py:85
  322.2 9.8 %custom-call.8 = f32[1,128,128]{1,2,0:T(8,128)S(1)} custom-call(f32[1,128,128]{2,1,0:T(8,128)S(1)} %fusion.70), custom_call_target="InvertDiagBlocksLowerTriangular" | custom-call | tf_op jit(solution)/shard_map/jit(_solve_triangular)/triangular_solve | solution.py:86
  332.7 5.9 %fusion = f32[1024,128]{1,0:T(8,128)S(1)} fusion(f32[128,1024]{1,0:T(8,128)S(1)} %fusion.65, f32[128,8,8,128]{3,2,1,0:T(8,128)} %bitcast.132), kind=kOutput, calls=%fused_computation.2 | convolution fusion | flops 1610612736 | bytes 5242880 | tf_op jit(solution)/shard_map/dot_general | solution.py:83
  339.7 11.7 %cholesky.81 = f32[128,128]{1,0:T(8,128)S(1)} custom-call(f32[128,128]{1,0:T(8,128)S(1)} %fusion.73), custom_call_target="Cholesky" | custom-call | tf_op jit(solution)/shard_map/jit(cholesky)/cholesky | solution.py:85
  352.8 9.8 %custom-call.9 = f32[1,128,128]{1,2,0:T(8,128)S(1)} custom-call(f32[1,128,128]{2,1,0:T(8,128)S(1)} %fusion.71), custom_call_target="InvertDiagBlocksLowerTriangular" | custom-call | tf_op jit(solution)/shard_map/jit(_solve_triangular)/triangular_solve | solution.py:86
  363.3 4.6 convolution_bitcast_fusion
  367.9 22.9 %all_to_all.15 = f32[16,4,8,256]{3,2,1,0:T(8,128)S(1)} all-to-all(f32[16,4,8,256]{3,2,1,0:T(8,128)S(1)} %bitcast.139), channel_id=1, replica_groups=mesh['gx'=16,'gy'=16] {'gy'}, dimensions={0} | all-to-all | bytes 1048576 | tf_op jit(solution)/shard_map/all_to_all | solution.py:91
  391.1 15.7 %all_to_all.16 = f32[16,16,2,256]{3,1,2,0:T(8,128)S(1)} all-to-all(f32[16,16,2,256]{3,1,2,0:T(8,128)S(1)} %bitcast.140), channel_id=1, replica_groups=mesh['gx'=16,'gy'=16] {'gx'}, dimensions={0} | all-to-all | bytes 1048576 | tf_op jit(solution)/shard_map/all_to_all | solution.py:93
  408.5 1.2 collective-permute-done.16
  409.8 8.6 %collective-permute-done.17 = f32[256,256]{1,0:T(8,128)S(1)} collective-permute-done((f32[256,256]{1,0:T(8,128)S(1)}, f32[256,256]{1,0:T(8,128)S(1)}, u32[]{:S(2)}, u32[]{:S(2)}) %collective-permute-start.17) | collective-permute-done | bytes 262176 | tf_op jit(solution)/shard_map/ppermute | solution.py:19
  418.5 1.9 collective-permute-start.18
  420.4 7.4 %collective-permute-done.18 = f32[256,256]{1,0:T(8,128)S(1)} collective-permute-done((f32[256,256]{1,0:T(8,128)S(1)}, f32[256,256]{1,0:T(8,128)S(1)}, u32[]{:S(2)}, u32[]{:S(2)}) %collective-permute-start.18) | collective-permute-done | bytes 262176 | tf_op jit(solution)/shard_map/ppermute | solution.py:19
  428.4 6.4 %collective-permute-done.19 = f32[256,256]{1,0:T(8,128)S(1)} collective-permute-done((f32[256,256]{1,0:T(8,128)S(1)}, f32[256,256]{1,0:T(8,128)S(1)}, u32[]{:S(2)}, u32[]{:S(2)}) %collective-permute-start.19) | collective-permute-done | bytes 262176 | tf_op jit(solution)/shard_map/ppermute | solution.py:19
  435.5 6.6 %collective-permute-done.20 = f32[256,256]{1,0:T(8,128)S(1)} collective-permute-done((f32[256,256]{1,0:T(8,128)S(1)}, f32[256,256]{1,0:T(8,128)S(1)}, u32[]{:S(2)}, u32[]{:S(2)}) %collective-permute-start.20) | collective-permute-done | bytes 262176 | tf_op jit(solution)/shard_map/ppermute | solution.py:19
  442.7 7.4 %collective-permute-done.21 = f32[256,256]{1,0:T(8,128)S(1)} collective-permute-done((f32[256,256]{1,0:T(8,128)S(1)}, f32[256,256]{1,0:T(8,128)S(1)}, u32[]{:S(2)}, u32[]{:S(2)}) %collective-permute-start.21) | collective-permute-done | bytes 262176 | tf_op jit(solution)/shard_map/ppermute | solution.py:19
  450.6 15.3 %collective-permute-done.22 = f32[256,256]{1,0:T(8,128)S(1)} collective-permute-done((f32[256,256]{1,0:T(8,128)S(1)}, f32[256,256]{1,0:T(8,128)S(1)}, u32[]{:S(2)}, u32[]{:S(2)}) %collective-permute-start.22) | collective-permute-done | bytes 262176 | tf_op jit(solution)/shard_map/ppermute | solution.py:19
  465.9 2.9 collective-permute-start.23
  469.8 8.7 %collective-permute-done.23 = f32[256,256]{1,0:T(8,128)S(1)} collective-permute-done((f32[256,256]{1,0:T(8,128)S(1)}, f32[256,256]{1,0:T(8,128)S(1)}, u32[]{:S(2)}, u32[]{:S(2)}) %collective-permute-start.23) | collective-permute-done | bytes 262176 | tf_op jit(solution)/shard_map/ppermute | solution.py:19
  (115 shorter events, 19.0 us)
Async XLA Ops:
  0.6 273.2 %copy-start = (f32[1024,128]{1,0:T(8,128)S(1)}, f32[1024,128]{1,0:T(8,128)}, u32[]{:S(2)}) copy-start(f32[1024,128]{1,0:T(8,128)} %param.7) | copy-start | bytes 1572868
  7.3 67.5 %all-to-all-start = ((f32[16,4,64,256]{3,2,1,0:T(8,128)}), f32[16,4,64,256]{3,2,1,0:T(8,128)}, u32[]{:S(2)}, u32[]{:S(2)}) async-start(f32[16,4,64,256]{3,2,1,0:T(8,128)} %bitcast.135), calls=%async_computation | async-start | bytes 8388608 | tf_op jit(solution)/shard_map/all_to_all | solution.py:53
  77.3 15.7 %copy-start.1 = (f32[4,16,64,256]{3,2,1,0:T(8,128)}, f32[4,16,64,256]{3,2,1,0:T(8,128)S(1)}, u32[]{:S(2)}) copy-start(f32[4,16,64,256]{3,2,1,0:T(8,128)S(1)} %copy.28) | copy-start | bytes 12582916
  98.0 1.0 copy-start.3
  99.1 28.4 %collective-permute-start = (f32[2304,128]{1,0:T(8,128)S(1)}, f32[2304,128]{1,0:T(8,128)}, u32[]{:S(2)}, u32[]{:S(2)}) collective-permute-start(f32[2304,128]{1,0:T(8,128)S(1)} %broadcast_select_fusion), channel_id=1, source_target_pairs={{0,128},{16,144},{32,160},{48,176},{64,192},{80,208},{96,224},{112... | collective-permute-start | bytes 3538952 | tf_op jit(solution)/shard_map/ppermute | solution.py:42
  128.9 16.4 %collective-permute-start.1 = (f32[1152,128]{1,0:T(8,128)S(1)}, f32[1152,128]{1,0:T(8,128)S(1)}, u32[]{:S(2)}, u32[]{:S(2)}) collective-permute-start(f32[1152,128]{1,0:T(8,128)S(1)} %slice_select_fusion), channel_id=1, source_target_pairs={{0,64},{16,80},{32,96},{48,112},{64,0},{80,16},{96,32},{112,48},{1... | collective-permute-start | bytes 1769480 | tf_op jit(solution)/shard_map/ppermute | solution.py:42
  145.4 7.7 %collective-permute-start.2 = (f32[576,128]{1,0:T(8,128)S(1)}, f32[576,128]{1,0:T(8,128)S(1)}, u32[]{:S(2)}, u32[]{:S(2)}) collective-permute-start(f32[576,128]{1,0:T(8,128)S(1)} %slice_select_fusion.1), channel_id=1, source_target_pairs={{0,32},{16,48},{32,0},{48,16},{64,96},{80,112},{96,64},{112,80},{1... | collective-permute-start | bytes 884744 | tf_op jit(solution)/shard_map/ppermute | solution.py:42
  153.2 1.5 collective-permute-start.3
  154.7 9.8 %collective-permute-start.4 = (f32[144,128]{1,0:T(8,128)S(1)}, f32[144,128]{1,0:T(8,128)S(1)}, u32[]{:S(2)}, u32[]{:S(2)}) collective-permute-start(f32[144,128]{1,0:T(8,128)S(1)} %slice_select_fusion.3), channel_id=1, source_target_pairs={{0,8},{1,9},{2,10},{3,11},{4,12},{5,13},{6,14},{7,15},{8,0},{9,1},... | collective-permute-start | bytes 221192 | tf_op jit(solution)/shard_map/ppermute | solution.py:42
  164.5 6.0 %collective-permute-start.5 = (f32[72,128]{1,0:T(8,128)S(1)}, f32[72,128]{1,0:T(8,128)S(1)}, u32[]{:S(2)}, u32[]{:S(2)}) collective-permute-start(f32[72,128]{1,0:T(8,128)S(1)} %slice_select_fusion.4), channel_id=1, source_target_pairs={{0,4},{1,5},{2,6},{3,7},{4,0},{5,1},{6,2},{7,3},{8,12},{9,13},{10,... | collective-permute-start | bytes 110600 | tf_op jit(solution)/shard_map/ppermute | solution.py:42
  170.5 5.4 %collective-permute-start.6 = (f32[36,128]{1,0:T(8,128)S(1)}, f32[36,128]{1,0:T(8,128)S(1)}, u32[]{:S(2)}, u32[]{:S(2)}) collective-permute-start(f32[36,128]{1,0:T(8,128)S(1)} %slice_select_fusion.5), channel_id=1, source_target_pairs={{0,2},{1,3},{2,0},{3,1},{4,6},{5,7},{6,4},{7,5},{8,10},{9,11},{10,... | collective-permute-start | bytes 55304 | tf_op jit(solution)/shard_map/ppermute | solution.py:42
  175.9 3.8 collective-permute-start.7
  179.7 3.7 collective-permute-start.8
  183.4 5.4 %collective-permute-start.9 = (f32[36,128]{1,0:T(8,128)S(1)}, f32[36,128]{1,0:T(8,128)S(1)}, u32[]{:S(2)}, u32[]{:S(2)}) collective-permute-start(f32[36,128]{1,0:T(8,128)S(1)} %maximum_select_fusion.7), channel_id=1, source_target_pairs={{0,2},{1,3},{2,0},{3,1},{4,6},{5,7},{6,4},{7,5},{8,10},{9,11},{10,... | collective-permute-start | bytes 55304 | tf_op jit(solution)/shard_map/ppermute | solution.py:45
  188.8 6.9 %collective-permute-start.10 = (f32[72,128]{1,0:T(8,128)S(1)}, f32[72,128]{1,0:T(8,128)S(1)}, u32[]{:S(2)}, u32[]{:S(2)}) collective-permute-start(f32[72,128]{1,0:T(8,128)S(1)} %maximum_select_fusion.6), channel_id=1, source_target_pairs={{0,4},{1,5},{2,6},{3,7},{4,0},{5,1},{6,2},{7,3},{8,12},{9,13},{10,... | collective-permute-start | bytes 110600 | tf_op jit(solution)/shard_map/ppermute | solution.py:45
  195.7 8.3 %collective-permute-start.11 = (f32[144,128]{1,0:T(8,128)S(1)}, f32[144,128]{1,0:T(8,128)S(1)}, u32[]{:S(2)}, u32[]{:S(2)}) collective-permute-start(f32[144,128]{1,0:T(8,128)S(1)} %maximum_select_fusion.5), channel_id=1, source_target_pairs={{0,8},{1,9},{2,10},{3,11},{4,12},{5,13},{6,14},{7,15},{8,0},{9,1},... | collective-permute-start | bytes 221192 | tf_op jit(solution)/shard_map/ppermute | solution.py:45
  204.0 1.5 collective-permute-start.12
  205.5 9.1 %collective-permute-start.13 = (f32[576,128]{1,0:T(8,128)S(1)}, f32[576,128]{1,0:T(8,128)S(1)}, u32[]{:S(2)}, u32[]{:S(2)}) collective-permute-start(f32[576,128]{1,0:T(8,128)S(1)} %maximum_select_fusion.3), channel_id=1, source_target_pairs={{0,32},{16,48},{32,0},{48,16},{64,96},{80,112},{96,64},{112,80},{1... | collective-permute-start | bytes 884744 | tf_op jit(solution)/shard_map/ppermute | solution.py:45
  214.7 16.5 %copy-start.4 = (s32[64]{0:T(128)S(1)}, s32[64]{0:T(128)}, u32[]{:S(2)}) copy-start(s32[64]{0:T(128)} %constant.219) | copy-start | bytes 772
  214.7 16.1 %collective-permute-start.14 = (f32[1152,128]{1,0:T(8,128)S(1)}, f32[1152,128]{1,0:T(8,128)S(1)}, u32[]{:S(2)}, u32[]{:S(2)}) collective-permute-start(f32[1152,128]{1,0:T(8,128)S(1)} %maximum_select_fusion.2), channel_id=1, source_target_pairs={{0,64},{16,80},{32,96},{48,112},{64,0},{80,16},{96,32},{112,48},{1... | collective-permute-start | bytes 1769480 | tf_op jit(solution)/shard_map/ppermute | solution.py:45
  231.0 26.4 %collective-permute-start.15 = (f32[2304,128]{1,0:T(8,128)S(1)}, f32[2304,128]{1,0:T(8,128)S(1)}, u32[]{:S(2)}, u32[]{:S(2)}) collective-permute-start(f32[2304,128]{1,0:T(8,128)S(1)} %maximum_select_fusion.1), channel_id=1, source_target_pairs={{0,128},{16,144},{32,160},{48,176},{64,192},{80,208},{96,224},{112... | collective-permute-start | bytes 3538952 | tf_op jit(solution)/shard_map/ppermute | solution.py:45
  273.8 3.5 copy-start.2
  407.9 1.8 collective-permute-start.16
  409.7 8.7 %collective-permute-start.17 = (f32[256,256]{1,0:T(8,128)S(1)}, f32[256,256]{1,0:T(8,128)S(1)}, u32[]{:S(2)}, u32[]{:S(2)}) collective-permute-start(f32[256,256]{1,0:T(8,128)S(1)} %add.124), channel_id=1, source_target_pairs={{0,32},{16,48},{32,0},{48,16},{64,96},{80,112},{96,64},{112,80},{1... | collective-permute-start | bytes 786440 | tf_op jit(solution)/shard_map/ppermute | solution.py:19
  418.5 9.3 %collective-permute-start.18 = (f32[256,256]{1,0:T(8,128)S(1)}, f32[256,256]{1,0:T(8,128)S(1)}, u32[]{:S(2)}, u32[]{:S(2)}) collective-permute-start(f32[256,256]{1,0:T(8,128)S(1)} %add.125), channel_id=1, source_target_pairs={{0,64},{16,80},{32,96},{48,112},{64,0},{80,16},{96,32},{112,48},{1... | collective-permute-start | bytes 786440 | tf_op jit(solution)/shard_map/ppermute | solution.py:19
  427.8 7.0 %collective-permute-start.19 = (f32[256,256]{1,0:T(8,128)S(1)}, f32[256,256]{1,0:T(8,128)S(1)}, u32[]{:S(2)}, u32[]{:S(2)}) collective-permute-start(f32[256,256]{1,0:T(8,128)S(1)} %add.126), channel_id=1, source_target_pairs={{0,128},{16,144},{32,160},{48,176},{64,192},{80,208},{96,224},{112... | collective-permute-start | bytes 786440 | tf_op jit(solution)/shard_map/ppermute | solution.py:19
  434.8 7.3 %collective-permute-start.20 = (f32[256,256]{1,0:T(8,128)S(1)}, f32[256,256]{1,0:T(8,128)S(1)}, u32[]{:S(2)}, u32[]{:S(2)}) collective-permute-start(f32[256,256]{1,0:T(8,128)S(1)} %add.127), channel_id=1, source_target_pairs={{0,1},{1,0},{2,3},{3,2},{4,5},{5,4},{6,7},{7,6},{8,9},{9,8},{10,11... | collective-permute-start | bytes 786440 | tf_op jit(solution)/shard_map/ppermute | solution.py:19
  442.1 8.0 %collective-permute-start.21 = (f32[256,256]{1,0:T(8,128)S(1)}, f32[256,256]{1,0:T(8,128)S(1)}, u32[]{:S(2)}, u32[]{:S(2)}) collective-permute-start(f32[256,256]{1,0:T(8,128)S(1)} %add.128), channel_id=1, source_target_pairs={{0,2},{1,3},{2,0},{3,1},{4,6},{5,7},{6,4},{7,5},{8,10},{9,11},{10,... | collective-permute-start | bytes 786440 | tf_op jit(solution)/shard_map/ppermute | solution.py:19
  450.1 15.7 %collective-permute-start.22 = (f32[256,256]{1,0:T(8,128)S(1)}, f32[256,256]{1,0:T(8,128)S(1)}, u32[]{:S(2)}, u32[]{:S(2)}) collective-permute-start(f32[256,256]{1,0:T(8,128)S(1)} %add.129), channel_id=1, source_target_pairs={{0,4},{1,5},{2,6},{3,7},{4,0},{5,1},{6,2},{7,3},{8,12},{9,13},{10,... | collective-permute-start | bytes 786440 | tf_op jit(solution)/shard_map/ppermute | solution.py:19
  465.9 12.7 %collective-permute-start.23 = (f32[256,256]{1,0:T(8,128)S(1)}, f32[256,256]{1,0:T(8,128)S(1)}, u32[]{:S(2)}, u32[]{:S(2)}) collective-permute-start(f32[256,256]{1,0:T(8,128)S(1)} %add.130), channel_id=1, source_target_pairs={{0,8},{1,9},{2,10},{3,11},{4,12},{5,13},{6,14},{7,15},{8,0},{9,1},... | collective-permute-start | bytes 786440 | tf_op jit(solution)/shard_map/ppermute | solution.py:19

commit v6 on v5

--- a/solution.py
+++ b/solution.py
@@ -31,20 +31,30 @@
     return steps
 
 
+def halving_step(value, axis, size, stride):
+    upper = (lax.axis_index(axis) // stride) % 2 == 1
+    half = value.shape[0] // 2
+    low, high = value[:half], value[half:]
+    keep = jnp.where(upper, high, low)
+    send = jnp.where(upper, low, high)
+    return keep + lax.ppermute(send, axis, [(i, i ^ stride) for i in range(size)])
+
+
+def doubling_step(value, axis, size, stride):
+    upper = (lax.axis_index(axis) // stride) % 2 == 1
+    other = lax.ppermute(value, axis, [(i, i ^ stride) for i in range(size)])
+    return jnp.where(upper, jnp.concatenate([other, value]), jnp.concatenate([value, other]))
+
+
 def halving_doubling_sum(value, sizes):
-    steps = halving_steps(sizes)
-    for axis, size, stride in steps:
-        upper = (lax.axis_index(axis) // stride) % 2 == 1
-        half = value.shape[0] // 2
-        low, high = value[:half], value[half:]
-        keep = jnp.where(upper, high, low)
-        send = jnp.where(upper, low, high)
-        value = keep + lax.ppermute(send, axis, [(i, i ^ stride) for i in range(size)])
-    for axis, size, stride in reversed(steps):
-        upper = (lax.axis_index(axis) // stride) % 2 == 1
-        other = lax.ppermute(value, axis, [(i, i ^ stride) for i in range(size)])
-        value = jnp.where(upper, jnp.concatenate([other, value]), jnp.concatenate([value, other]))
-    return value
+    half = value.shape[0] // 2
+    chains = [value[:half], value[half:]]
+    orders = [halving_steps(sizes), halving_steps(tuple(reversed(sizes)))]
+    for index in range(len(orders[0])):
+        chains = [halving_step(chain, *order[index]) for chain, order in zip(chains, orders)]
+    for index in reversed(range(len(orders[0]))):
+        chains = [doubling_step(chain, *order[index]) for chain, order in zip(chains, orders)]
+    return jnp.concatenate(chains)
 
 
 def body(species_field, initial):
@@ -93,8 +103,7 @@
     stage_two = lax.all_to_all(jnp.swapaxes(pairs, 0, 1), "gx", split_axis=0, concat_axis=0, tiled=True)
     columns = jnp.swapaxes(stage_two, 0, 1).reshape(n_gy * n_gx, -1)
     second_part = jnp.einsum("yc,wc->yw", columns, columns, precision=highest) / (S * R * NZ)
-    gram_two = butterfly_sum(second_part, "gx", lax.axis_size("gx"))
-    gram_two = butterfly_sum(gram_two, "gy", lax.axis_size("gy"))
+    gram_two = halving_doubling_sum(second_part.reshape(-1, BLOCK), sizes).reshape(second_part.shape)
     return (basis * math.sqrt(rows_x), gram_two)
 
 

time: 483 us -> 518 us (1.072)
  starting transfers between devices: 46 us -> 107 us
  waiting for transfers between devices: 247 us -> 210 us
  blocking collectives: 38.6 us -> 47.5 us
    ppermute x24 -> x64, starting transfers between devices: 39.3 us -> 99.6 us  [the longest x32 57.7 us: halving_step(): lax.ppermute(send, axis, [(i, i ^ stride) for i in range(size)])]
    ppermute x24 -> x64, waiting for transfers between devices: 186 us -> 150 us  [the longest x32 75.2 us: halving_step(): lax.ppermute(send, axis, [(i, i ^ stride) for i in range(size)])]
    all_to_all x1, blocking collectives: 22.9 us -> 33 us  [body(): lax.all_to_all(by_rank, 'gy', split_axis=0, concat_axis=0, tiled=True)]
  transfers between devices with their start and end apart: 25 -> 65, of which waited for: 25 -> 40; matrix products, arithmetic and copies ran while one was open for 0% -> 0% of each run, Pallas kernels for 0% -> 0%
where the time goes in v6:
time: 518 us; the launch traced here: 513 us
  waiting for transfers between devices  210 us (41%)
  starting transfers between devices  107 us (21%)
  other arithmetic  74.8 us (14%)
  blocking collectives  47.5 us (9%)
  matrix products  45.3 us (9%)
  local copies, waits for them, and re-layouts  26.5 us (5%)
    ppermute x32, waiting for transfers between devices, halving_step(): lax.ppermute(send, axis, [(i, i ^ stride) for i in range(size)])  75.2 us
    ppermute x32, waiting for transfers between devices, doubling_step(): other = lax.ppermute(value, axis, [(i, i ^ stride) for i in range(size)])  74.6 us
    all_to_all x1, waiting for transfers between devices, body(): lax.all_to_all(by_row, 'gx', split_axis=0, concat_axis=0, tiled=True)  60.4 us
    ppermute x32, starting transfers between devices, halving_step(): lax.ppermute(send, axis, [(i, i ^ stride) for i in range(size)])  57.7 us
    ppermute x32, starting transfers between devices, doubling_step(): other = lax.ppermute(value, axis, [(i, i ^ stride) for i in range(size)])  41.9 us
    another operation x9, other arithmetic, body(): factor_low = jnp.linalg.cholesky(square)  37.2 us
    all_to_all x1, blocking collectives, body(): lax.all_to_all(by_rank, 'gy', split_axis=0, concat_axis=0, tiled=True)  33 us
    another operation x6, other arithmetic, body(): basis = jax.scipy.linalg.solve_triangular(factor_low, wide.T, lower=True).T  31.5 us
  transfers between devices with their start and end apart: 65, of which 40 were waited for; matrix products, arithmetic and copies ran while one was open for 0% of the time, Pallas kernels for 0%

profile of v6, /device:TPU:6, one launch (start us, length us, event | category | flops | bytes accessed | tf_op | source)
XLA Modules:
  0.0 513.1 jit_solution(7456447030899223728)
XLA Ops:
  0.6 6.7 %copy.54 = f32[4,64,16,256]{3,1,0,2:T(8,128)} copy(f32[4,64,16,256]{3,2,1,0:T(8,128)} %param.6) | data formatting | bytes 8388608 | tf_op args[0]
  7.3 7.0 %all-to-all-start = ((f32[16,4,64,256]{3,2,1,0:T(8,128)}), f32[16,4,64,256]{3,2,1,0:T(8,128)}, u32[]{:S(2)}, u32[]{:S(2)}) async-start(f32[16,4,64,256]{3,2,1,0:T(8,128)} %bitcast.135), calls=%async_computation | async-start | bytes 8388608 | tf_op jit(solution)/shard_map/all_to_all | solution.py:63
  14.5 60.4 %all-to-all-done = f32[16,4,64,256]{3,2,1,0:T(8,128)} async-done(((f32[16,4,64,256]{3,2,1,0:T(8,128)}), f32[16,4,64,256]{3,2,1,0:T(8,128)}, u32[]{:S(2)}, u32[]{:S(2)}) %all-to-all-start) | async-done | bytes 4194336 | tf_op jit(solution)/shard_map/all_to_all | solution.py:63
  74.9 2.5 copy.28
  80.7 2.3 fusion.41
  82.9 2.7 fusion.38
  85.6 3.3 fusion.32
  88.9 3.9 fusion.26
  92.8 4.4 fusion.19
  99.6 6.7 %collective-permute-start.16 = (f32[1152,128]{1,0:T(8,128)S(1)}, f32[1152,128]{1,0:T(8,128)S(1)}, u32[]{:S(2)}, u32[]{:S(2)}) collective-permute-start(f32[1152,128]{1,0:T(8,128)S(1)} %broadcast_select_fusion), channel_id=1, source_target_pairs={{0,8},{1,9},{2,10},{3,11},{4,12},{5,13},{6,14},{7,15},{8,0},{9,1},... | collective-permute-start | bytes 1769480 | tf_op jit(solution)/shard_map/ppermute | solution.py:40
  106.3 7.6 %collective-permute-done = f32[1152,128]{1,0:T(8,128)S(1)} collective-permute-done((f32[1152,128]{1,0:T(8,128)S(1)}, f32[1152,128]{1,0:T(8,128)S(1)}, u32[]{:S(2)}, u32[]{:S(2)}) %collective-permute-start) | collective-permute-done | bytes 589856 | tf_op jit(solution)/shard_map/ppermute | solution.py:40
  114.3 18.5 %collective-permute-done.16 = f32[1152,128]{1,0:T(8,128)S(1)} collective-permute-done((f32[1152,128]{1,0:T(8,128)S(1)}, f32[1152,128]{1,0:T(8,128)S(1)}, u32[]{:S(2)}, u32[]{:S(2)}) %collective-permute-start.16) | collective-permute-done | bytes 589856 | tf_op jit(solution)/shard_map/ppermute | solution.py:40
  132.9 13.6 %collective-permute-start.17 = (f32[576,128]{1,0:T(8,128)S(1)}, f32[576,128]{1,0:T(8,128)S(1)}, u32[]{:S(2)}, u32[]{:S(2)}) collective-permute-start(f32[576,128]{1,0:T(8,128)S(1)} %slice_select_fusion), channel_id=1, source_target_pairs={{0,4},{1,5},{2,6},{3,7},{4,0},{5,1},{6,2},{7,3},{8,12},{9,13},{10,... | collective-permute-start | bytes 884744 | tf_op jit(solution)/shard_map/ppermute | solution.py:40
  146.7 12.8 %collective-permute-done.17 = f32[576,128]{1,0:T(8,128)S(1)} collective-permute-done((f32[576,128]{1,0:T(8,128)S(1)}, f32[576,128]{1,0:T(8,128)S(1)}, u32[]{:S(2)}, u32[]{:S(2)}) %collective-permute-start.17) | collective-permute-done | bytes 294944 | tf_op jit(solution)/shard_map/ppermute | solution.py:40
  159.6 3.3 collective-permute-start.18
  163.1 3.9 collective-permute-done.18
  171.6 5.1 collective-permute-done.4
  177.0 4.5 collective-permute-done.5
  181.5 3.2 collective-permute-start.6
  184.8 2.2 collective-permute-done.6
  188.5 2.2 collective-permute-done.7
  191.2 3.2 collective-permute-done.8
  194.4 3.0 collective-permute-start.9
  197.5 2.2 collective-permute-done.9
  200.2 4.3 collective-permute-done.10
  206.1 6.3 %collective-permute-done.11 = f32[72,128]{1,0:T(8,128)S(1)} collective-permute-done((f32[72,128]{1,0:T(8,128)S(1)}, f32[72,128]{1,0:T(8,128)S(1)}, u32[]{:S(2)}, u32[]{:S(2)}) %collective-permute-start.11) | collective-permute-done | bytes 36896 | tf_op jit(solution)/shard_map/ppermute | solution.py:45
  214.0 2.7 collective-permute-done.27
  217.2 2.7 collective-permute-done.13
  221.1 3.0 collective-permute-start.29
  224.2 3.7 collective-permute-done.29
  230.9 11.2 %collective-permute-done.30 = f32[576,128]{1,0:T(8,128)S(1)} collective-permute-done((f32[576,128]{1,0:T(8,128)S(1)}, f32[576,128]{1,0:T(8,128)S(1)}, u32[]{:S(2)}, u32[]{:S(2)}) %collective-permute-start.30) | collective-permute-done | bytes 294944 | tf_op jit(solution)/shard_map/ppermute | solution.py:45
  243.5 20.9 %collective-permute-done.15 = f32[1152,128]{1,0:T(8,128)S(1)} collective-permute-done((f32[1152,128]{1,0:T(8,128)S(1)}, f32[1152,128]{1,0:T(8,128)S(1)}, u32[]{:S(2)}, u32[]{:S(2)}) %collective-permute-start.15) | collective-permute-done | bytes 589856 | tf_op jit(solution)/shard_map/ppermute | solution.py:45
  264.8 2.4 copy.29
  267.2 4.3 pad_maximum_fusion
  271.6 5.3 %gather_fusion = f32[64,128,128]{2,1,0:T(8,128)} fusion(f32[72,128,128]{2,1,0:T(8,128)} %pad_maximum_fusion, s32[1024]{0:T(1024)S(1)} %pad_clamp_fusion), kind=kCustom, calls=%fused_computation | custom fusion | bytes 8388864 | tf_op jit(solution)/shard_map/jit(_take)/gather | solution.py:89
  276.8 4.6 copy.30
  283.4 3.5 fusion.4
  288.0 11.7 %cholesky.59 = f32[128,128]{1,0:T(8,128)S(1)} custom-call(f32[128,128]{1,0:T(8,128)S(1)} %fusion.77), custom_call_target="Cholesky" | custom-call | tf_op jit(solution)/shard_map/jit(cholesky)/cholesky | solution.py:95
  301.0 9.9 %custom-call.7 = f32[1,128,128]{1,2,0:T(8,128)S(1)} custom-call(f32[1,128,128]{2,1,0:T(8,128)S(1)} %fusion.69), custom_call_target="InvertDiagBlocksLowerTriangular" | custom-call | tf_op jit(solution)/shard_map/jit(_solve_triangular)/triangular_solve | solution.py:96
  311.6 5.7 %fusion.2 = f32[1024,128]{1,0:T(8,128)S(1)} fusion(f32[128,1024]{1,0:T(8,128)S(1)} %fusion.67, f32[128,8,8,128]{3,2,1,0:T(8,128)} %bitcast.131), kind=kOutput, calls=%fused_computation.4 | convolution fusion | flops 1610612736 | bytes 5242880 | tf_op jit(solution)/shard_map/dot_general | solution.py:93
  318.5 11.7 %cholesky.70 = f32[128,128]{1,0:T(8,128)S(1)} custom-call(f32[128,128]{1,0:T(8,128)S(1)} %fusion.75), custom_call_target="Cholesky" | custom-call | tf_op jit(solution)/shard_map/jit(cholesky)/cholesky | solution.py:95
  331.5 9.8 %custom-call.8 = f32[1,128,128]{1,2,0:T(8,128)S(1)} custom-call(f32[1,128,128]{2,1,0:T(8,128)S(1)} %fusion.70), custom_call_target="InvertDiagBlocksLowerTriangular" | custom-call | tf_op jit(solution)/shard_map/jit(_solve_triangular)/triangular_solve | solution.py:96
  342.0 6.1 %fusion = f32[1024,128]{1,0:T(8,128)S(1)} fusion(f32[128,1024]{1,0:T(8,128)S(1)} %fusion.65, f32[128,8,8,128]{3,2,1,0:T(8,128)} %bitcast.132), kind=kOutput, calls=%fused_computation.2 | convolution fusion | flops 1610612736 | bytes 5242880 | tf_op jit(solution)/shard_map/dot_general | solution.py:93
  349.3 11.7 %cholesky.81 = f32[128,128]{1,0:T(8,128)S(1)} custom-call(f32[128,128]{1,0:T(8,128)S(1)} %fusion.73), custom_call_target="Cholesky" | custom-call | tf_op jit(solution)/shard_map/jit(cholesky)/cholesky | solution.py:95
  362.3 9.8 %custom-call.9 = f32[1,128,128]{1,2,0:T(8,128)S(1)} custom-call(f32[1,128,128]{2,1,0:T(8,128)S(1)} %fusion.71), custom_call_target="InvertDiagBlocksLowerTriangular" | custom-call | tf_op jit(solution)/shard_map/jit(_solve_triangular)/triangular_solve | solution.py:96
  372.8 4.6 convolution_bitcast_fusion
  377.4 33.0 %all_to_all.15 = f32[16,4,8,256]{3,2,1,0:T(8,128)S(1)} all-to-all(f32[16,4,8,256]{3,2,1,0:T(8,128)S(1)} %bitcast.139), channel_id=1, replica_groups=mesh['gx'=16,'gy'=16] {'gy'}, dimensions={0} | all-to-all | bytes 1048576 | tf_op jit(solution)/shard_map/all_to_all | solution.py:101
  410.8 14.4 %all_to_all.16 = f32[16,16,2,256]{3,1,2,0:T(8,128)S(1)} all-to-all(f32[16,16,2,256]{3,1,2,0:T(8,128)S(1)} %bitcast.140), channel_id=1, replica_groups=mesh['gx'=16,'gy'=16] {'gx'}, dimensions={0} | all-to-all | bytes 1048576 | tf_op jit(solution)/shard_map/all_to_all | solution.py:103
  428.3 2.3 collective-permute-start.48
  432.5 4.0 collective-permute-done.48
  436.6 2.7 collective-permute-start.49
  443.4 3.4 collective-permute-done.50
  447.5 3.2 collective-permute-start.36
  450.8 2.1 collective-permute-start.52
  452.9 2.3 collective-permute-done.36
  455.1 2.2 collective-permute-start.37
  470.2 2.0 collective-permute-done.40
  477.3 2.2 collective-permute-start.42
  481.9 3.2 collective-permute-start.43
  486.7 2.8 collective-permute-done.43
  495.2 2.0 collective-permute-start.46
  498.5 2.2 collective-permute-start.62
  503.3 3.3 collective-permute-start.63
  506.6 5.5 %collective-permute-done.63 = f32[128,128]{1,0:T(8,128)S(1)} collective-permute-done((f32[128,128]{1,0:T(8,128)S(1)}, f32[128,128]{1,0:T(8,128)S(1)}, u32[]{:S(2)}, u32[]{:S(2)}) %collective-permute-start.63) | collective-permute-done | bytes 65568 | tf_op jit(solution)/shard_map/ppermute | solution.py:45
  (261 shorter events, 77.0 us)
Async XLA Ops:
  7.3 67.5 %all-to-all-start = ((f32[16,4,64,256]{3,2,1,0:T(8,128)}), f32[16,4,64,256]{3,2,1,0:T(8,128)}, u32[]{:S(2)}, u32[]{:S(2)}) async-start(f32[16,4,64,256]{3,2,1,0:T(8,128)} %bitcast.135), calls=%async_computation | async-start | bytes 8388608 | tf_op jit(solution)/shard_map/all_to_all | solution.py:63
  97.6 16.3 %collective-permute-start = (f32[1152,128]{1,0:T(8,128)S(1)}, f32[1152,128]{1,0:T(8,128)S(1)}, u32[]{:S(2)}, u32[]{:S(2)}) collective-permute-start(f32[1152,128]{1,0:T(8,128)S(1)} %broadcast_select_fusion.1), channel_id=1, source_target_pairs={{0,128},{16,144},{32,160},{48,176},{64,192},{80,208},{96,224},{112... | collective-permute-start | bytes 1769480 | tf_op jit(solution)/shard_map/ppermute | solution.py:40
  99.6 33.2 %collective-permute-start.16 = (f32[1152,128]{1,0:T(8,128)S(1)}, f32[1152,128]{1,0:T(8,128)S(1)}, u32[]{:S(2)}, u32[]{:S(2)}) collective-permute-start(f32[1152,128]{1,0:T(8,128)S(1)} %broadcast_select_fusion), channel_id=1, source_target_pairs={{0,8},{1,9},{2,10},{3,11},{4,12},{5,13},{6,14},{7,15},{8,0},{9,1},... | collective-permute-start | bytes 1769480 | tf_op jit(solution)/shard_map/ppermute | solution.py:40
  114.1 32.4 %collective-permute-start.1 = (f32[576,128]{1,0:T(8,128)S(1)}, f32[576,128]{1,0:T(8,128)S(1)}, u32[]{:S(2)}, u32[]{:S(2)}) collective-permute-start(f32[576,128]{1,0:T(8,128)S(1)} %slice_select_fusion.1), channel_id=1, source_target_pairs={{0,64},{16,80},{32,96},{48,112},{64,0},{80,16},{96,32},{112,48},{1... | collective-permute-start | bytes 884744 | tf_op jit(solution)/shard_map/ppermute | solution.py:40
  132.9 26.6 %collective-permute-start.17 = (f32[576,128]{1,0:T(8,128)S(1)}, f32[576,128]{1,0:T(8,128)S(1)}, u32[]{:S(2)}, u32[]{:S(2)}) collective-permute-start(f32[576,128]{1,0:T(8,128)S(1)} %slice_select_fusion), channel_id=1, source_target_pairs={{0,4},{1,5},{2,6},{3,7},{4,0},{5,1},{6,2},{7,3},{8,12},{9,13},{10,... | collective-permute-start | bytes 884744 | tf_op jit(solution)/shard_map/ppermute | solution.py:40
  146.6 16.3 %collective-permute-start.2 = (f32[288,128]{1,0:T(8,128)S(1)}, f32[288,128]{1,0:T(8,128)S(1)}, u32[]{:S(2)}, u32[]{:S(2)}) collective-permute-start(f32[288,128]{1,0:T(8,128)S(1)} %slice_select_fusion.3), channel_id=1, source_target_pairs={{0,32},{16,48},{32,0},{48,16},{64,96},{80,112},{96,64},{112,80},{1... | collective-permute-start | bytes 442376 | tf_op jit(solution)/shard_map/ppermute | solution.py:40
  159.6 7.4 %collective-permute-start.18 = (f32[288,128]{1,0:T(8,128)S(1)}, f32[288,128]{1,0:T(8,128)S(1)}, u32[]{:S(2)}, u32[]{:S(2)}) collective-permute-start(f32[288,128]{1,0:T(8,128)S(1)} %slice_select_fusion.2), channel_id=1, source_target_pairs={{0,2},{1,3},{2,0},{3,1},{4,6},{5,7},{6,4},{7,5},{8,10},{9,11},{10,... | collective-permute-start | bytes 442376 | tf_op jit(solution)/shard_map/ppermute | solution.py:40
  163.0 5.7 %collective-permute-start.3 = (f32[144,128]{1,0:T(8,128)S(1)}, f32[144,128]{1,0:T(8,128)S(1)}, u32[]{:S(2)}, u32[]{:S(2)}) collective-permute-start(f32[144,128]{1,0:T(8,128)S(1)} %slice_select_fusion.5), channel_id=1, source_target_pairs={{0,16},{16,0},{32,48},{48,32},{64,80},{80,64},{96,112},{112,96},{1... | collective-permute-start | bytes 221192 | tf_op jit(solution)/shard_map/ppermute | solution.py:40
  167.0 4.4 collective-permute-start.19
  168.7 8.0 %collective-permute-start.4 = (f32[72,128]{1,0:T(8,128)S(1)}, f32[72,128]{1,0:T(8,128)S(1)}, u32[]{:S(2)}, u32[]{:S(2)}) collective-permute-start(f32[72,128]{1,0:T(8,128)S(1)} %slice_select_fusion.11), channel_id=1, source_target_pairs={{0,8},{1,9},{2,10},{3,11},{4,12},{5,13},{6,14},{7,15},{8,0},{9,1},... | collective-permute-start | bytes 110600 | tf_op jit(solution)/shard_map/ppermute | solution.py:40
  171.5 5.3 %collective-permute-start.20 = (f32[72,128]{1,0:T(8,128)S(1)}, f32[72,128]{1,0:T(8,128)S(1)}, u32[]{:S(2)}, u32[]{:S(2)}) collective-permute-start(f32[72,128]{1,0:T(8,128)S(1)} %slice_select_fusion.10), channel_id=1, source_target_pairs={{0,128},{16,144},{32,160},{48,176},{64,192},{80,208},{96,224},{112... | collective-permute-start | bytes 110600 | tf_op jit(solution)/shard_map/ppermute | solution.py:40
  176.7 4.8 collective-permute-start.5
  176.9 7.9 %collective-permute-start.21 = (f32[36,128]{1,0:T(8,128)S(1)}, f32[36,128]{1,0:T(8,128)S(1)}, u32[]{:S(2)}, u32[]{:S(2)}) collective-permute-start(f32[36,128]{1,0:T(8,128)S(1)} %slice_select_fusion.14), channel_id=1, source_target_pairs={{0,64},{16,80},{32,96},{48,112},{64,0},{80,16},{96,32},{112,48},{1... | collective-permute-start | bytes 55304 | tf_op jit(solution)/shard_map/ppermute | solution.py:40
  181.5 5.5 %collective-permute-start.6 = (f32[18,128]{1,0:T(8,128)S(1)}, f32[18,128]{1,0:T(8,128)S(1)}, u32[]{:S(2)}, u32[]{:S(2)}) collective-permute-start(f32[18,128]{1,0:T(8,128)S(1)} %slice_select_fusion.19), channel_id=1, source_target_pairs={{0,2},{1,3},{2,0},{3,1},{4,6},{5,7},{6,4},{7,5},{8,10},{9,11},{10,... | collective-permute-start | bytes 27656 | tf_op jit(solution)/shard_map/ppermute | solution.py:40
  184.7 3.8 collective-permute-start.22
  187.0 3.7 collective-permute-start.7
  190.8 3.7 collective-permute-start.8
  191.2 6.2 %collective-permute-start.23 = (f32[9,128]{1,0:T(8,128)S(1)}, f32[9,128]{1,0:T(8,128)S(1)}, u32[]{:S(2)}, u32[]{:S(2)}) collective-permute-start(f32[9,128]{1,0:T(8,128)S(1)} %slice_select_fusion.22), channel_id=1, source_target_pairs={{0,16},{16,0},{32,48},{48,32},{64,80},{80,64},{96,112},{112,96},{1... | collective-permute-start | bytes 13832 | tf_op jit(solution)/shard_map/ppermute | solution.py:40
  194.4 5.3 %collective-permute-start.9 = (f32[18,128]{1,0:T(8,128)S(1)}, f32[18,128]{1,0:T(8,128)S(1)}, u32[]{:S(2)}, u32[]{:S(2)}) collective-permute-start(f32[18,128]{1,0:T(8,128)S(1)} %maximum_select_fusion.22), channel_id=1, source_target_pairs={{0,2},{1,3},{2,0},{3,1},{4,6},{5,7},{6,4},{7,5},{8,10},{9,11},{10,... | collective-permute-start | bytes 27656 | tf_op jit(solution)/shard_map/ppermute | solution.py:45
  197.4 2.4 collective-permute-start.24
  199.7 4.8 collective-permute-start.10
  199.9 6.2 %collective-permute-start.25 = (f32[18,128]{1,0:T(8,128)S(1)}, f32[18,128]{1,0:T(8,128)S(1)}, u32[]{:S(2)}, u32[]{:S(2)}) collective-permute-start(f32[18,128]{1,0:T(8,128)S(1)} %maximum_select_fusion.23), channel_id=1, source_target_pairs={{0,32},{16,48},{32,0},{48,16},{64,96},{80,112},{96,64},{112,80},{1... | collective-permute-start | bytes 27656 | tf_op jit(solution)/shard_map/ppermute | solution.py:45
  204.5 8.0 %collective-permute-start.11 = (f32[72,128]{1,0:T(8,128)S(1)}, f32[72,128]{1,0:T(8,128)S(1)}, u32[]{:S(2)}, u32[]{:S(2)}) collective-permute-start(f32[72,128]{1,0:T(8,128)S(1)} %maximum_select_fusion.14), channel_id=1, source_target_pairs={{0,8},{1,9},{2,10},{3,11},{4,12},{5,13},{6,14},{7,15},{8,0},{9,1},... | collective-permute-start | bytes 110600 | tf_op jit(solution)/shard_map/ppermute | solution.py:45
  206.0 6.5 %collective-permute-start.26 = (f32[36,128]{1,0:T(8,128)S(1)}, f32[36,128]{1,0:T(8,128)S(1)}, u32[]{:S(2)}, u32[]{:S(2)}) collective-permute-start(f32[36,128]{1,0:T(8,128)S(1)} %maximum_select_fusion.19), channel_id=1, source_target_pairs={{0,64},{16,80},{32,96},{48,112},{64,0},{80,16},{96,32},{112,48},{1... | collective-permute-start | bytes 55304 | tf_op jit(solution)/shard_map/ppermute | solution.py:45
  212.6 4.0 collective-permute-start.27
  213.9 6.0 %collective-permute-start.13 = (f32[288,128]{1,0:T(8,128)S(1)}, f32[288,128]{1,0:T(8,128)S(1)}, u32[]{:S(2)}, u32[]{:S(2)}) collective-permute-start(f32[288,128]{1,0:T(8,128)S(1)} %maximum_select_fusion.6), channel_id=1, source_target_pairs={{0,32},{16,48},{32,0},{48,16},{64,96},{80,112},{96,64},{112,80},{1... | collective-permute-start | bytes 442376 | tf_op jit(solution)/shard_map/ppermute | solution.py:45
  216.7 4.4 collective-permute-start.28
  219.9 9.8 %collective-permute-start.14 = (f32[576,128]{1,0:T(8,128)S(1)}, f32[576,128]{1,0:T(8,128)S(1)}, u32[]{:S(2)}, u32[]{:S(2)}) collective-permute-start(f32[576,128]{1,0:T(8,128)S(1)} %maximum_select_fusion.4), channel_id=1, source_target_pairs={{0,64},{16,80},{32,96},{48,112},{64,0},{80,16},{96,32},{112,48},{1... | collective-permute-start | bytes 884744 | tf_op jit(solution)/shard_map/ppermute | solution.py:45
  221.1 6.7 %collective-permute-start.29 = (f32[288,128]{1,0:T(8,128)S(1)}, f32[288,128]{1,0:T(8,128)S(1)}, u32[]{:S(2)}, u32[]{:S(2)}) collective-permute-start(f32[288,128]{1,0:T(8,128)S(1)} %maximum_select_fusion.7), channel_id=1, source_target_pairs={{0,2},{1,3},{2,0},{3,1},{4,6},{5,7},{6,4},{7,5},{8,10},{9,11},{10,... | collective-permute-start | bytes 442376 | tf_op jit(solution)/shard_map/ppermute | solution.py:45
  227.9 14.2 %collective-permute-start.30 = (f32[576,128]{1,0:T(8,128)S(1)}, f32[576,128]{1,0:T(8,128)S(1)}, u32[]{:S(2)}, u32[]{:S(2)}) collective-permute-start(f32[576,128]{1,0:T(8,128)S(1)} %maximum_select_fusion.5), channel_id=1, source_target_pairs={{0,4},{1,5},{2,6},{3,7},{4,0},{5,1},{6,2},{7,3},{8,12},{9,13},{10,... | collective-permute-start | bytes 884744 | tf_op jit(solution)/shard_map/ppermute | solution.py:45
  229.7 34.7 %collective-permute-start.15 = (f32[1152,128]{1,0:T(8,128)S(1)}, f32[1152,128]{1,0:T(8,128)S(1)}, u32[]{:S(2)}, u32[]{:S(2)}) collective-permute-start(f32[1152,128]{1,0:T(8,128)S(1)} %maximum_select_fusion.2), channel_id=1, source_target_pairs={{0,128},{16,144},{32,160},{48,176},{64,192},{80,208},{96,224},{112... | collective-permute-start | bytes 1769480 | tf_op jit(solution)/shard_map/ppermute | solution.py:45
  242.2 22.4 %collective-permute-start.31 = (f32[1152,128]{1,0:T(8,128)S(1)}, f32[1152,128]{1,0:T(8,128)S(1)}, u32[]{:S(2)}, u32[]{:S(2)}) collective-permute-start(f32[1152,128]{1,0:T(8,128)S(1)} %maximum_select_fusion.3), channel_id=1, source_target_pairs={{0,8},{1,9},{2,10},{3,11},{4,12},{5,13},{6,14},{7,15},{8,0},{9,1},... | collective-permute-start | bytes 1769480 | tf_op jit(solution)/shard_map/ppermute | solution.py:45
  426.4 4.6 collective-permute-start.32
  428.3 8.3 %collective-permute-start.48 = (f32[128,128]{1,0:T(8,128)S(1)}, f32[128,128]{1,0:T(8,128)S(1)}, u32[]{:S(2)}, u32[]{:S(2)}) collective-permute-start(f32[128,128]{1,0:T(8,128)S(1)} %select_n.958), channel_id=1, source_target_pairs={{0,8},{1,9},{2,10},{3,11},{4,12},{5,13},{6,14},{7,15},{8,0},{9,1},... | collective-permute-start | bytes 196616 | tf_op jit(solution)/shard_map/ppermute | solution.py:40
  431.0 8.3 %collective-permute-start.33 = (f32[64,128]{1,0:T(8,128)S(1)}, f32[64,128]{1,0:T(8,128)S(1)}, u32[]{:S(2)}, u32[]{:S(2)}) collective-permute-start(f32[64,128]{1,0:T(8,128)S(1)} %slice_select_fusion.13), channel_id=1, source_target_pairs={{0,64},{16,80},{32,96},{48,112},{64,0},{80,16},{96,32},{112,48},{1... | collective-permute-start | bytes 98312 | tf_op jit(solution)/shard_map/ppermute | solution.py:40
  436.6 4.9 collective-permute-start.49
  439.3 4.0 collective-permute-start.34
  441.5 5.3 %collective-permute-start.50 = (f32[32,128]{1,0:T(8,128)S(1)}, f32[32,128]{1,0:T(8,128)S(1)}, u32[]{:S(2)}, u32[]{:S(2)}) collective-permute-start(f32[32,128]{1,0:T(8,128)S(1)} %slice_select_fusion.16), channel_id=1, source_target_pairs={{0,2},{1,3},{2,0},{3,1},{4,6},{5,7},{6,4},{7,5},{8,10},{9,11},{10,... | collective-permute-start | bytes 49160 | tf_op jit(solution)/shard_map/ppermute | solution.py:40
  443.3 4.2 collective-permute-start.35
  446.9 3.9 collective-permute-start.51
  447.5 7.6 %collective-permute-start.36 = (f32[8,128]{1,0:T(8,128)S(1)}, f32[8,128]{1,0:T(8,128)S(1)}, u32[]{:S(2)}, u32[]{:S(2)}) collective-permute-start(f32[8,128]{1,0:T(8,128)S(1)} %slice_select_fusion.25), channel_id=1, source_target_pairs={{0,8},{1,9},{2,10},{3,11},{4,12},{5,13},{6,14},{7,15},{8,0},{9,1},... | collective-permute-start | bytes 12296 | tf_op jit(solution)/shard_map/ppermute | solution.py:40
  450.8 6.6 %collective-permute-start.52 = (f32[8,128]{1,0:T(8,128)S(1)}, f32[8,128]{1,0:T(8,128)S(1)}, u32[]{:S(2)}, u32[]{:S(2)}) collective-permute-start(f32[8,128]{1,0:T(8,128)S(1)} %slice_select_fusion.24), channel_id=1, source_target_pairs={{0,128},{16,144},{32,160},{48,176},{64,192},{80,208},{96,224},{112... | collective-permute-start | bytes 12296 | tf_op jit(solution)/shard_map/ppermute | solution.py:40
  455.1 4.6 collective-permute-start.37
  457.4 5.2 %collective-permute-start.53 = (f32[4,128]{1,0:T(4,128)S(1)}, f32[4,128]{1,0:T(4,128)S(1)}, u32[]{:S(2)}, u32[]{:S(2)}) collective-permute-start(f32[4,128]{1,0:T(4,128)S(1)} %slice_select_fusion.26), channel_id=1, source_target_pairs={{0,64},{16,80},{32,96},{48,112},{64,0},{80,16},{96,32},{112,48},{1... | collective-permute-start | bytes 6152 | tf_op jit(solution)/shard_map/ppermute | solution.py:40
  459.7 5.2 %collective-permute-start.38 = (f32[2,128]{1,0:T(2,128)S(1)}, f32[2,128]{1,0:T(2,128)S(1)}, u32[]{:S(2)}, u32[]{:S(2)}) collective-permute-start(f32[2,128]{1,0:T(2,128)S(1)} %broadcast_select_fusion.5), channel_id=1, source_target_pairs={{0,2},{1,3},{2,0},{3,1},{4,6},{5,7},{6,4},{7,5},{8,10},{9,11},{10,... | collective-permute-start | bytes 3080 | tf_op jit(solution)/shard_map/ppermute | solution.py:40
  462.6 3.9 collective-permute-start.54
  464.9 3.7 collective-permute-start.39
  466.5 3.6 collective-permute-start.55
  468.6 3.6 collective-permute-start.40
  470.1 3.9 collective-permute-start.56
  472.2 5.2 %collective-permute-start.41 = (f32[2,128]{1,0:T(2,128)S(1)}, f32[2,128]{1,0:T(2,128)S(1)}, u32[]{:S(2)}, u32[]{:S(2)}) collective-permute-start(f32[2,128]{1,0:T(2,128)S(1)} %maximum_select_fusion.30), channel_id=1, source_target_pairs={{0,2},{1,3},{2,0},{3,1},{4,6},{5,7},{6,4},{7,5},{8,10},{9,11},{10,... | collective-permute-start | bytes 3080 | tf_op jit(solution)/shard_map/ppermute | solution.py:45
  473.9 5.6 %collective-permute-start.57 = (f32[2,128]{1,0:T(2,128)S(1)}, f32[2,128]{1,0:T(2,128)S(1)}, u32[]{:S(2)}, u32[]{:S(2)}) collective-permute-start(f32[2,128]{1,0:T(2,128)S(1)} %maximum_select_fusion.31), channel_id=1, source_target_pairs={{0,32},{16,48},{32,0},{48,16},{64,96},{80,112},{96,64},{112,80},{1... | collective-permute-start | bytes 3080 | tf_op jit(solution)/shard_map/ppermute | solution.py:45
  477.3 4.6 collective-permute-start.42
  479.6 5.6 %collective-permute-start.58 = (f32[4,128]{1,0:T(4,128)S(1)}, f32[4,128]{1,0:T(4,128)S(1)}, u32[]{:S(2)}, u32[]{:S(2)}) collective-permute-start(f32[4,128]{1,0:T(4,128)S(1)} %maximum_select_fusion.29), channel_id=1, source_target_pairs={{0,64},{16,80},{32,96},{48,112},{64,0},{80,16},{96,32},{112,48},{1... | collective-permute-start | bytes 6152 | tf_op jit(solution)/shard_map/ppermute | solution.py:45
  481.9 7.6 %collective-permute-start.43 = (f32[8,128]{1,0:T(8,128)S(1)}, f32[8,128]{1,0:T(8,128)S(1)}, u32[]{:S(2)}, u32[]{:S(2)}) collective-permute-start(f32[8,128]{1,0:T(8,128)S(1)} %maximum_select_fusion.26), channel_id=1, source_target_pairs={{0,8},{1,9},{2,10},{3,11},{4,12},{5,13},{6,14},{7,15},{8,0},{9,1},... | collective-permute-start | bytes 12296 | tf_op jit(solution)/shard_map/ppermute | solution.py:45
  485.2 4.3 collective-permute-start.59
  489.5 1.8 collective-permute-start.44
  489.5 3.7 collective-permute-start.60
  491.3 3.9 collective-permute-start.45
  493.3 5.2 %collective-permute-start.61 = (f32[32,128]{1,0:T(8,128)S(1)}, f32[32,128]{1,0:T(8,128)S(1)}, u32[]{:S(2)}, u32[]{:S(2)}) collective-permute-start(f32[32,128]{1,0:T(8,128)S(1)} %maximum_select_fusion.21), channel_id=1, source_target_pairs={{0,2},{1,3},{2,0},{3,1},{4,6},{5,7},{6,4},{7,5},{8,10},{9,11},{10,... | collective-permute-start | bytes 49160 | tf_op jit(solution)/shard_map/ppermute | solution.py:45
  495.2 5.5 %collective-permute-start.46 = (f32[64,128]{1,0:T(8,128)S(1)}, f32[64,128]{1,0:T(8,128)S(1)}, u32[]{:S(2)}, u32[]{:S(2)}) collective-permute-start(f32[64,128]{1,0:T(8,128)S(1)} %maximum_select_fusion.16), channel_id=1, source_target_pairs={{0,64},{16,80},{32,96},{48,112},{64,0},{80,16},{96,32},{112,48},{1... | collective-permute-start | bytes 98312 | tf_op jit(solution)/shard_map/ppermute | solution.py:45
  498.5 4.8 collective-permute-start.62
  500.7 5.9 %collective-permute-start.47 = (f32[128,128]{1,0:T(8,128)S(1)}, f32[128,128]{1,0:T(8,128)S(1)}, u32[]{:S(2)}, u32[]{:S(2)}) collective-permute-start(f32[128,128]{1,0:T(8,128)S(1)} %maximum_select_fusion.12), channel_id=1, source_target_pairs={{0,128},{16,144},{32,160},{48,176},{64,192},{80,208},{96,224},{112... | collective-permute-start | bytes 196616 | tf_op jit(solution)/shard_map/ppermute | solution.py:45
  503.3 8.7 %collective-permute-start.63 = (f32[128,128]{1,0:T(8,128)S(1)}, f32[128,128]{1,0:T(8,128)S(1)}, u32[]{:S(2)}, u32[]{:S(2)}) collective-permute-start(f32[128,128]{1,0:T(8,128)S(1)} %maximum_select_fusion.13), channel_id=1, source_target_pairs={{0,8},{1,9},{2,10},{3,11},{4,12},{5,13},{6,14},{7,15},{8,0},{9,1},... | collective-permute-start | bytes 196616 | tf_op jit(solution)/shard_map/ppermute | solution.py:45
  (5 other events, 385.5 us)

commit v7 on v5

--- a/solution.py
+++ b/solution.py
@@ -83,7 +83,7 @@
         wide = jnp.dot(gram_one, basis, precision=highest, preferred_element_type=jnp.float32)
         square = jnp.dot(wide.T, wide, precision=highest, preferred_element_type=jnp.float32)
         factor_low = jnp.linalg.cholesky(square)
-        basis = jax.scipy.linalg.solve_triangular(factor_low, wide.T, lower=True).T
+        basis = lax.linalg.triangular_solve(factor_low, wide, left_side=False, lower=True, transpose_a=True)
     core_tensor = jnp.einsum("xr,sxc->src", basis, fibers, precision=highest)
     n_gy = lax.axis_size("gy")
     n_gx = lax.axis_size("gx")
@@ -93,8 +93,14 @@
     stage_two = lax.all_to_all(jnp.swapaxes(pairs, 0, 1), "gx", split_axis=0, concat_axis=0, tiled=True)
     columns = jnp.swapaxes(stage_two, 0, 1).reshape(n_gy * n_gx, -1)
     second_part = jnp.einsum("yc,wc->yw", columns, columns, precision=highest) / (S * R * NZ)
-    gram_two = butterfly_sum(second_part, "gx", lax.axis_size("gx"))
-    gram_two = butterfly_sum(gram_two, "gy", lax.axis_size("gy"))
+    half_y = second_part.shape[0] // 2
+    lower_two = jnp.stack([second_part[:half_y, :half_y], second_part[half_y:, :half_y], second_part[half_y:, half_y:]])
+    lower_two = butterfly_sum(lower_two, "gx", lax.axis_size("gx"))
+    lower_two = butterfly_sum(lower_two, "gy", lax.axis_size("gy"))
+    gram_two = jnp.concatenate([
+        jnp.concatenate([lower_two[0], lower_two[1].T], axis=1),
+        jnp.concatenate([lower_two[1], lower_two[2]], axis=1),
+    ], axis=0)
     return (basis * math.sqrt(rows_x), gram_two)
 
 

time: 483 us -> 474 us (0.981)
  waiting for transfers between devices: 247 us -> 238 us
    ppermute x8, waiting for transfers between devices: 61.5 us -> 52.2 us  [butterfly_sum(): lax.ppermute(value, axis, [(i, i ^ stride) for i in range(size)])]
    unnamed x44 -> x46, local copies, waits for them, and re-layouts: 8.88 us -> 9.78 us
    another operation x6 -> x7, other arithmetic: 31.8 us -> 31.8 us  [the longest x6 31.8 us: body(): lax.linalg.triangular_solve(factor_low, wide, left_side=False, lower=True...]
where the time goes in v7:
time: 474 us; the launch traced here: 470 us
  waiting for transfers between devices  238 us (50%)
  other arithmetic  75.8 us (16%)
  starting transfers between devices  46 us (10%)
  matrix products  45.3 us (10%)
  blocking collectives  38.5 us (8%)
  local copies, waits for them, and re-layouts  25.2 us (5%)
    ppermute x8, waiting for transfers between devices, halving_doubling_sum(): other = lax.ppermute(value, axis, [(i, i ^ stride) for i in range(size)])  63.8 us
    all_to_all x1, waiting for transfers between devices, body(): lax.all_to_all(by_row, 'gx', split_axis=0, concat_axis=0, tiled=True)  60.9 us
    ppermute x8, waiting for transfers between devices, halving_doubling_sum(): lax.ppermute(send, axis, [(i, i ^ stride) for i in range(size)])  60.7 us
    ppermute x8, waiting for transfers between devices, butterfly_sum(): lax.ppermute(value, axis, [(i, i ^ stride) for i in range(size)])  52.2 us
    another operation x9, other arithmetic, body(): factor_low = jnp.linalg.cholesky(square)  37.2 us
    another operation x6, other arithmetic, body(): lax.linalg.triangular_solve(factor_low, wide, left_side=False, lower=True...  31.8 us
    all_to_all x1, blocking collectives, body(): lax.all_to_all(by_rank, 'gy', split_axis=0, concat_axis=0, tiled=True)  23 us
    dot_general x8, matrix products, body(): jnp.einsum('sxc,swc->xw', fibers[:, row * BLOCK:(row + 1) * BLOCK], fiber...  20.1 us
  transfers between devices with their start and end apart: 25, of which 25 were waited for; matrix products, arithmetic and copies ran while one was open for 0% of the time, Pallas kernels for 0%

profile of v7, /device:TPU:6, one launch (start us, length us, event | category | flops | bytes accessed | tf_op | source)
XLA Modules:
  0.0 470.3 jit_solution(13175093747417347950)
XLA Ops:
  0.6 6.7 %copy.68 = f32[4,64,16,256]{3,1,0,2:T(8,128)} copy(f32[4,64,16,256]{3,2,1,0:T(8,128)} %param.6) | data formatting | bytes 8388608 | tf_op args[0]
  7.3 6.6 %all-to-all-start = ((f32[16,4,64,256]{3,2,1,0:T(8,128)}), f32[16,4,64,256]{3,2,1,0:T(8,128)}, u32[]{:S(2)}, u32[]{:S(2)}) async-start(f32[16,4,64,256]{3,2,1,0:T(8,128)} %bitcast.151), calls=%async_computation | async-start | bytes 8388608 | tf_op jit(solution)/shard_map/all_to_all | solution.py:53
  14.0 60.9 %all-to-all-done = f32[16,4,64,256]{3,2,1,0:T(8,128)} async-done(((f32[16,4,64,256]{3,2,1,0:T(8,128)}), f32[16,4,64,256]{3,2,1,0:T(8,128)}, u32[]{:S(2)}, u32[]{:S(2)}) %all-to-all-start) | async-done | bytes 4194336 | tf_op jit(solution)/shard_map/all_to_all | solution.py:53
  74.8 2.5 copy.37
  77.3 1.2 fusion.50
  79.1 1.5 fusion.47
  80.6 2.3 fusion.41
  82.9 2.7 fusion.38
  85.6 3.3 fusion.32
  88.9 4.1 fusion.26
  93.0 4.4 fusion.19
  99.0 1.6 collective-permute-start
  100.6 26.8 %collective-permute-done = f32[2304,128]{1,0:T(8,128)} collective-permute-done((f32[2304,128]{1,0:T(8,128)S(1)}, f32[2304,128]{1,0:T(8,128)}, u32[]{:S(2)}, u32[]{:S(2)}) %collective-permute-start) | collective-permute-done | bytes 1179680 | tf_op jit(solution)/shard_map/ppermute | solution.py:42
  127.4 1.4 select_add_fusion
  129.0 16.2 %collective-permute-done.1 = f32[1152,128]{1,0:T(8,128)S(1)} collective-permute-done((f32[1152,128]{1,0:T(8,128)S(1)}, f32[1152,128]{1,0:T(8,128)S(1)}, u32[]{:S(2)}, u32[]{:S(2)}) %collective-permute-start.1) | collective-permute-done | bytes 589856 | tf_op jit(solution)/shard_map/ppermute | solution.py:42
  145.5 7.6 %collective-permute-done.2 = f32[576,128]{1,0:T(8,128)S(1)} collective-permute-done((f32[576,128]{1,0:T(8,128)S(1)}, f32[576,128]{1,0:T(8,128)S(1)}, u32[]{:S(2)}, u32[]{:S(2)}) %collective-permute-start.2) | collective-permute-done | bytes 294944 | tf_op jit(solution)/shard_map/ppermute | solution.py:42
  153.3 1.3 collective-permute-done.3
  154.7 7.1 %collective-permute-start.4 = (f32[144,128]{1,0:T(8,128)S(1)}, f32[144,128]{1,0:T(8,128)S(1)}, u32[]{:S(2)}, u32[]{:S(2)}) collective-permute-start(f32[144,128]{1,0:T(8,128)S(1)} %slice_select_fusion.3), channel_id=1, source_target_pairs={{0,8},{1,9},{2,10},{3,11},{4,12},{5,13},{6,14},{7,15},{8,0},{9,1},... | collective-permute-start | bytes 221192 | tf_op jit(solution)/shard_map/ppermute | solution.py:42
  161.8 2.7 collective-permute-done.4
  164.5 4.0 collective-permute-start.5
  168.5 1.9 collective-permute-done.5
  170.5 3.3 collective-permute-start.6
  173.8 2.1 collective-permute-done.6
  175.9 1.7 collective-permute-start.7
  177.6 2.1 collective-permute-done.7
  179.7 1.6 collective-permute-start.8
  181.3 2.1 collective-permute-done.8
  183.4 3.3 collective-permute-start.9
  186.7 2.1 collective-permute-done.9
  188.8 3.0 collective-permute-start.10
  191.8 3.9 collective-permute-done.10
  195.6 4.3 collective-permute-start.11
  199.9 4.1 collective-permute-done.11
  204.1 1.4 collective-permute-done.12
  205.9 8.8 %collective-permute-done.13 = f32[576,128]{1,0:T(8,128)S(1)} collective-permute-done((f32[576,128]{1,0:T(8,128)S(1)}, f32[576,128]{1,0:T(8,128)S(1)}, u32[]{:S(2)}, u32[]{:S(2)}) %collective-permute-start.13) | collective-permute-done | bytes 294944 | tf_op jit(solution)/shard_map/ppermute | solution.py:45
  215.3 15.5 %collective-permute-done.14 = f32[1152,128]{1,0:T(8,128)S(1)} collective-permute-done((f32[1152,128]{1,0:T(8,128)S(1)}, f32[1152,128]{1,0:T(8,128)S(1)}, u32[]{:S(2)}, u32[]{:S(2)}) %collective-permute-start.14) | collective-permute-done | bytes 589856 | tf_op jit(solution)/shard_map/ppermute | solution.py:45
  231.2 26.1 %collective-permute-done.15 = f32[2304,128]{1,0:T(8,128)S(1)} collective-permute-done((f32[2304,128]{1,0:T(8,128)S(1)}, f32[2304,128]{1,0:T(8,128)S(1)}, u32[]{:S(2)}, u32[]{:S(2)}) %collective-permute-start.15) | collective-permute-done | bytes 1179680 | tf_op jit(solution)/shard_map/ppermute | solution.py:45
  257.6 2.1 copy.38
  259.7 4.3 pad_maximum_fusion
  263.9 5.2 %gather_fusion = f32[64,128,128]{2,1,0:T(8,128)} fusion(f32[72,128,128]{2,1,0:T(8,128)} %pad_maximum_fusion, s32[1024]{0:T(1024)S(1)} %pad_clamp_fusion), kind=kCustom, calls=%fused_computation | custom fusion | bytes 8388864 | tf_op jit(solution)/shard_map/jit(_take)/gather | solution.py:79
  269.2 4.6 copy.39
  273.7 3.5 fusion.4
  278.3 11.7 %cholesky.59 = f32[128,128]{1,0:T(8,128)S(1)} custom-call(f32[128,128]{1,0:T(8,128)S(1)} %fusion.72), custom_call_target="Cholesky" | custom-call | tf_op jit(solution)/shard_map/jit(cholesky)/cholesky | solution.py:85
  291.4 10.2 %custom-call.7 = f32[1,128,128]{1,2,0:T(8,128)S(1)} custom-call(f32[1,128,128]{2,1,0:T(8,128)S(1)} %fusion.63), custom_call_target="InvertDiagBlocksLowerTriangular" | custom-call | tf_op jit(solution)/shard_map/triangular_solve/custom-call.0 | solution.py:86
  302.2 5.7 %fusion.2 = f32[1024,128]{1,0:T(8,128)S(1)} fusion(f32[1024,128]{0,1:T(8,128)S(1)} %convolution_bitcast_fusion.1, f32[128,8,8,128]{3,2,1,0:T(8,128)} %bitcast.147), kind=kOutput, calls=%fused_computation.4 | convolution fusion | flops 1610612736 | bytes 5242880 | tf_op jit(solution)/shard_map/dot_general | solution.py:83
  308.0 1.0 fusion.79
  309.1 11.7 %cholesky.70 = f32[128,128]{1,0:T(8,128)S(1)} custom-call(f32[128,128]{1,0:T(8,128)S(1)} %fusion.70), custom_call_target="Cholesky" | custom-call | tf_op jit(solution)/shard_map/jit(cholesky)/cholesky | solution.py:85
  322.2 9.8 %custom-call.8 = f32[1,128,128]{1,2,0:T(8,128)S(1)} custom-call(f32[1,128,128]{2,1,0:T(8,128)S(1)} %fusion.64), custom_call_target="InvertDiagBlocksLowerTriangular" | custom-call | tf_op jit(solution)/shard_map/triangular_solve/custom-call.0 | solution.py:86
  332.6 5.9 %fusion = f32[1024,128]{1,0:T(8,128)S(1)} fusion(f32[1024,128]{0,1:T(8,128)S(1)} %convolution_bitcast_fusion, f32[128,8,8,128]{3,2,1,0:T(8,128)} %bitcast.148), kind=kOutput, calls=%fused_computation.2 | convolution fusion | flops 1610612736 | bytes 5242880 | tf_op jit(solution)/shard_map/dot_general | solution.py:83
  339.7 11.7 %cholesky.81 = f32[128,128]{1,0:T(8,128)S(1)} custom-call(f32[128,128]{1,0:T(8,128)S(1)} %fusion.68), custom_call_target="Cholesky" | custom-call | tf_op jit(solution)/shard_map/jit(cholesky)/cholesky | solution.py:85
  352.7 9.8 %custom-call.9 = f32[1,128,128]{1,2,0:T(8,128)S(1)} custom-call(f32[1,128,128]{2,1,0:T(8,128)S(1)} %fusion.65), custom_call_target="InvertDiagBlocksLowerTriangular" | custom-call | tf_op jit(solution)/shard_map/triangular_solve/custom-call.0 | solution.py:86
  363.2 4.6 convolution_bitcast_fusion.2
  367.8 23.0 %all_to_all.15 = f32[16,4,8,256]{3,2,1,0:T(8,128)S(1)} all-to-all(f32[16,4,8,256]{3,2,1,0:T(8,128)S(1)} %bitcast.155), channel_id=1, replica_groups=mesh['gx'=16,'gy'=16] {'gy'}, dimensions={0} | all-to-all | bytes 1048576 | tf_op jit(solution)/shard_map/all_to_all | solution.py:91
  391.1 15.6 %all_to_all.16 = f32[16,16,2,256]{3,1,2,0:T(8,128)S(1)} all-to-all(f32[16,16,2,256]{3,1,2,0:T(8,128)S(1)} %bitcast.156), channel_id=1, replica_groups=mesh['gx'=16,'gy'=16] {'gx'}, dimensions={0} | all-to-all | bytes 1048576 | tf_op jit(solution)/shard_map/all_to_all | solution.py:93
  408.5 1.1 collective-permute-done.16
  409.7 7.2 %collective-permute-done.17 = f32[3,128,128]{1,2,0:T(8,128)S(1)} collective-permute-done((f32[3,128,128]{1,2,0:T(8,128)S(1)}, f32[3,128,128]{1,2,0:T(8,128)S(1)}, u32[]{:S(2)}, u32[]{:S(2)}) %collective-permute-start.17) | collective-permute-done | bytes 196640 | tf_op jit(solution)/shard_map/ppermute | solution.py:19
  416.9 1.9 collective-permute-start.18
  418.8 6.0 %collective-permute-done.18 = f32[3,128,128]{1,2,0:T(8,128)S(1)} collective-permute-done((f32[3,128,128]{1,2,0:T(8,128)S(1)}, f32[3,128,128]{1,2,0:T(8,128)S(1)}, u32[]{:S(2)}, u32[]{:S(2)}) %collective-permute-start.18) | collective-permute-done | bytes 196640 | tf_op jit(solution)/shard_map/ppermute | solution.py:19
  425.4 5.2 %collective-permute-done.19 = f32[3,128,128]{1,2,0:T(8,128)S(1)} collective-permute-done((f32[3,128,128]{1,2,0:T(8,128)S(1)}, f32[3,128,128]{1,2,0:T(8,128)S(1)}, u32[]{:S(2)}, u32[]{:S(2)}) %collective-permute-start.19) | collective-permute-done | bytes 196640 | tf_op jit(solution)/shard_map/ppermute | solution.py:19
  431.3 6.2 %collective-permute-done.20 = f32[3,128,128]{1,2,0:T(8,128)S(1)} collective-permute-done((f32[3,128,128]{1,2,0:T(8,128)S(1)}, f32[3,128,128]{1,2,0:T(8,128)S(1)}, u32[]{:S(2)}, u32[]{:S(2)}) %collective-permute-start.20) | collective-permute-done | bytes 196640 | tf_op jit(solution)/shard_map/ppermute | solution.py:19
  437.8 6.9 %collective-permute-done.21 = f32[3,128,128]{1,2,0:T(8,128)S(1)} collective-permute-done((f32[3,128,128]{1,2,0:T(8,128)S(1)}, f32[3,128,128]{1,2,0:T(8,128)S(1)}, u32[]{:S(2)}, u32[]{:S(2)}) %collective-permute-start.21) | collective-permute-done | bytes 196640 | tf_op jit(solution)/shard_map/ppermute | solution.py:19
  445.3 12.4 %collective-permute-done.22 = f32[3,128,128]{1,2,0:T(8,128)S(1)} collective-permute-done((f32[3,128,128]{1,2,0:T(8,128)S(1)}, f32[3,128,128]{1,2,0:T(8,128)S(1)}, u32[]{:S(2)}, u32[]{:S(2)}) %collective-permute-start.22) | collective-permute-done | bytes 196640 | tf_op jit(solution)/shard_map/ppermute | solution.py:19
  457.7 3.0 collective-permute-start.23
  461.8 7.3 %collective-permute-done.23 = f32[3,128,128]{1,2,0:T(8,128)S(1)} collective-permute-done((f32[3,128,128]{1,2,0:T(8,128)S(1)}, f32[3,128,128]{1,2,0:T(8,128)S(1)}, u32[]{:S(2)}, u32[]{:S(2)}) %collective-permute-start.23) | collective-permute-done | bytes 196640 | tf_op jit(solution)/shard_map/ppermute | solution.py:19
  (120 shorter events, 19.1 us)
Async XLA Ops:
  0.6 273.1 %copy-start = (f32[1024,128]{1,0:T(8,128)S(1)}, f32[1024,128]{1,0:T(8,128)}, u32[]{:S(2)}) copy-start(f32[1024,128]{1,0:T(8,128)} %param.7) | copy-start | bytes 1572868
  7.3 67.5 %all-to-all-start = ((f32[16,4,64,256]{3,2,1,0:T(8,128)}), f32[16,4,64,256]{3,2,1,0:T(8,128)}, u32[]{:S(2)}, u32[]{:S(2)}) async-start(f32[16,4,64,256]{3,2,1,0:T(8,128)} %bitcast.151), calls=%async_computation | async-start | bytes 8388608 | tf_op jit(solution)/shard_map/all_to_all | solution.py:53
  77.3 15.7 %copy-start.1 = (f32[4,16,64,256]{3,2,1,0:T(8,128)}, f32[4,16,64,256]{3,2,1,0:T(8,128)S(1)}, u32[]{:S(2)}) copy-start(f32[4,16,64,256]{3,2,1,0:T(8,128)S(1)} %copy.37) | copy-start | bytes 12582916
  98.0 1.0 copy-start.3
  99.0 28.4 %collective-permute-start = (f32[2304,128]{1,0:T(8,128)S(1)}, f32[2304,128]{1,0:T(8,128)}, u32[]{:S(2)}, u32[]{:S(2)}) collective-permute-start(f32[2304,128]{1,0:T(8,128)S(1)} %broadcast_select_fusion), channel_id=1, source_target_pairs={{0,128},{16,144},{32,160},{48,176},{64,192},{80,208},{96,224},{112... | collective-permute-start | bytes 3538952 | tf_op jit(solution)/shard_map/ppermute | solution.py:42
  128.9 16.4 %collective-permute-start.1 = (f32[1152,128]{1,0:T(8,128)S(1)}, f32[1152,128]{1,0:T(8,128)S(1)}, u32[]{:S(2)}, u32[]{:S(2)}) collective-permute-start(f32[1152,128]{1,0:T(8,128)S(1)} %slice_select_fusion), channel_id=1, source_target_pairs={{0,64},{16,80},{32,96},{48,112},{64,0},{80,16},{96,32},{112,48},{1... | collective-permute-start | bytes 1769480 | tf_op jit(solution)/shard_map/ppermute | solution.py:42
  145.4 7.7 %collective-permute-start.2 = (f32[576,128]{1,0:T(8,128)S(1)}, f32[576,128]{1,0:T(8,128)S(1)}, u32[]{:S(2)}, u32[]{:S(2)}) collective-permute-start(f32[576,128]{1,0:T(8,128)S(1)} %slice_select_fusion.1), channel_id=1, source_target_pairs={{0,32},{16,48},{32,0},{48,16},{64,96},{80,112},{96,64},{112,80},{1... | collective-permute-start | bytes 884744 | tf_op jit(solution)/shard_map/ppermute | solution.py:42
  153.2 1.5 collective-permute-start.3
  154.7 9.8 %collective-permute-start.4 = (f32[144,128]{1,0:T(8,128)S(1)}, f32[144,128]{1,0:T(8,128)S(1)}, u32[]{:S(2)}, u32[]{:S(2)}) collective-permute-start(f32[144,128]{1,0:T(8,128)S(1)} %slice_select_fusion.3), channel_id=1, source_target_pairs={{0,8},{1,9},{2,10},{3,11},{4,12},{5,13},{6,14},{7,15},{8,0},{9,1},... | collective-permute-start | bytes 221192 | tf_op jit(solution)/shard_map/ppermute | solution.py:42
  164.5 6.0 %collective-permute-start.5 = (f32[72,128]{1,0:T(8,128)S(1)}, f32[72,128]{1,0:T(8,128)S(1)}, u32[]{:S(2)}, u32[]{:S(2)}) collective-permute-start(f32[72,128]{1,0:T(8,128)S(1)} %slice_select_fusion.4), channel_id=1, source_target_pairs={{0,4},{1,5},{2,6},{3,7},{4,0},{5,1},{6,2},{7,3},{8,12},{9,13},{10,... | collective-permute-start | bytes 110600 | tf_op jit(solution)/shard_map/ppermute | solution.py:42
  170.5 5.4 %collective-permute-start.6 = (f32[36,128]{1,0:T(8,128)S(1)}, f32[36,128]{1,0:T(8,128)S(1)}, u32[]{:S(2)}, u32[]{:S(2)}) collective-permute-start(f32[36,128]{1,0:T(8,128)S(1)} %slice_select_fusion.5), channel_id=1, source_target_pairs={{0,2},{1,3},{2,0},{3,1},{4,6},{5,7},{6,4},{7,5},{8,10},{9,11},{10,... | collective-permute-start | bytes 55304 | tf_op jit(solution)/shard_map/ppermute | solution.py:42
  175.9 3.8 collective-permute-start.7
  179.7 3.7 collective-permute-start.8
  183.4 5.4 %collective-permute-start.9 = (f32[36,128]{1,0:T(8,128)S(1)}, f32[36,128]{1,0:T(8,128)S(1)}, u32[]{:S(2)}, u32[]{:S(2)}) collective-permute-start(f32[36,128]{1,0:T(8,128)S(1)} %maximum_select_fusion.7), channel_id=1, source_target_pairs={{0,2},{1,3},{2,0},{3,1},{4,6},{5,7},{6,4},{7,5},{8,10},{9,11},{10,... | collective-permute-start | bytes 55304 | tf_op jit(solution)/shard_map/ppermute | solution.py:45
  188.8 6.9 %collective-permute-start.10 = (f32[72,128]{1,0:T(8,128)S(1)}, f32[72,128]{1,0:T(8,128)S(1)}, u32[]{:S(2)}, u32[]{:S(2)}) collective-permute-start(f32[72,128]{1,0:T(8,128)S(1)} %maximum_select_fusion.6), channel_id=1, source_target_pairs={{0,4},{1,5},{2,6},{3,7},{4,0},{5,1},{6,2},{7,3},{8,12},{9,13},{10,... | collective-permute-start | bytes 110600 | tf_op jit(solution)/shard_map/ppermute | solution.py:45
  195.6 8.3 %collective-permute-start.11 = (f32[144,128]{1,0:T(8,128)S(1)}, f32[144,128]{1,0:T(8,128)S(1)}, u32[]{:S(2)}, u32[]{:S(2)}) collective-permute-start(f32[144,128]{1,0:T(8,128)S(1)} %maximum_select_fusion.5), channel_id=1, source_target_pairs={{0,8},{1,9},{2,10},{3,11},{4,12},{5,13},{6,14},{7,15},{8,0},{9,1},... | collective-permute-start | bytes 221192 | tf_op jit(solution)/shard_map/ppermute | solution.py:45
  204.0 1.5 collective-permute-start.12
  205.5 9.1 %collective-permute-start.13 = (f32[576,128]{1,0:T(8,128)S(1)}, f32[576,128]{1,0:T(8,128)S(1)}, u32[]{:S(2)}, u32[]{:S(2)}) collective-permute-start(f32[576,128]{1,0:T(8,128)S(1)} %maximum_select_fusion.3), channel_id=1, source_target_pairs={{0,32},{16,48},{32,0},{48,16},{64,96},{80,112},{96,64},{112,80},{1... | collective-permute-start | bytes 884744 | tf_op jit(solution)/shard_map/ppermute | solution.py:45
  214.7 16.5 %copy-start.4 = (s32[64]{0:T(128)S(1)}, s32[64]{0:T(128)}, u32[]{:S(2)}) copy-start(s32[64]{0:T(128)} %constant.217) | copy-start | bytes 772
  214.7 16.1 %collective-permute-start.14 = (f32[1152,128]{1,0:T(8,128)S(1)}, f32[1152,128]{1,0:T(8,128)S(1)}, u32[]{:S(2)}, u32[]{:S(2)}) collective-permute-start(f32[1152,128]{1,0:T(8,128)S(1)} %maximum_select_fusion.2), channel_id=1, source_target_pairs={{0,64},{16,80},{32,96},{48,112},{64,0},{80,16},{96,32},{112,48},{1... | collective-permute-start | bytes 1769480 | tf_op jit(solution)/shard_map/ppermute | solution.py:45
  230.9 26.4 %collective-permute-start.15 = (f32[2304,128]{1,0:T(8,128)S(1)}, f32[2304,128]{1,0:T(8,128)S(1)}, u32[]{:S(2)}, u32[]{:S(2)}) collective-permute-start(f32[2304,128]{1,0:T(8,128)S(1)} %maximum_select_fusion.1), channel_id=1, source_target_pairs={{0,128},{16,144},{32,160},{48,176},{64,192},{80,208},{96,224},{112... | collective-permute-start | bytes 3538952 | tf_op jit(solution)/shard_map/ppermute | solution.py:45
  273.7 3.5 copy-start.2
  407.8 1.8 collective-permute-start.16
  409.6 7.3 %collective-permute-start.17 = (f32[3,128,128]{1,2,0:T(8,128)S(1)}, f32[3,128,128]{1,2,0:T(8,128)S(1)}, u32[]{:S(2)}, u32[]{:S(2)}) collective-permute-start(f32[3,128,128]{1,2,0:T(8,128)S(1)} %fusion.77), channel_id=1, source_target_pairs={{0,32},{16,48},{32,0},{48,16},{64,96},{80,112},{96,64},{112,80},{1... | collective-permute-start | bytes 589832 | tf_op jit(solution)/shard_map/ppermute | solution.py:19
  416.9 7.9 %collective-permute-start.18 = (f32[3,128,128]{1,2,0:T(8,128)S(1)}, f32[3,128,128]{1,2,0:T(8,128)S(1)}, u32[]{:S(2)}, u32[]{:S(2)}) collective-permute-start(f32[3,128,128]{1,2,0:T(8,128)S(1)} %fusion.97), channel_id=1, source_target_pairs={{0,64},{16,80},{32,96},{48,112},{64,0},{80,16},{96,32},{112,48},{1... | collective-permute-start | bytes 589832 | tf_op jit(solution)/shard_map/ppermute | solution.py:19
  424.8 5.8 %collective-permute-start.19 = (f32[3,128,128]{1,2,0:T(8,128)S(1)}, f32[3,128,128]{1,2,0:T(8,128)S(1)}, u32[]{:S(2)}, u32[]{:S(2)}) collective-permute-start(f32[3,128,128]{1,2,0:T(8,128)S(1)} %add.125), channel_id=1, source_target_pairs={{0,128},{16,144},{32,160},{48,176},{64,192},{80,208},{96,224},{112... | collective-permute-start | bytes 589832 | tf_op jit(solution)/shard_map/ppermute | solution.py:19
  430.6 6.8 %collective-permute-start.20 = (f32[3,128,128]{1,2,0:T(8,128)S(1)}, f32[3,128,128]{1,2,0:T(8,128)S(1)}, u32[]{:S(2)}, u32[]{:S(2)}) collective-permute-start(f32[3,128,128]{1,2,0:T(8,128)S(1)} %add.126), channel_id=1, source_target_pairs={{0,1},{1,0},{2,3},{3,2},{4,5},{5,4},{6,7},{7,6},{8,9},{9,8},{10,11... | collective-permute-start | bytes 589832 | tf_op jit(solution)/shard_map/ppermute | solution.py:19
  437.5 7.3 %collective-permute-start.21 = (f32[3,128,128]{1,2,0:T(8,128)S(1)}, f32[3,128,128]{1,2,0:T(8,128)S(1)}, u32[]{:S(2)}, u32[]{:S(2)}) collective-permute-start(f32[3,128,128]{1,2,0:T(8,128)S(1)} %add.127), channel_id=1, source_target_pairs={{0,2},{1,3},{2,0},{3,1},{4,6},{5,7},{6,4},{7,5},{8,10},{9,11},{10,... | collective-permute-start | bytes 589832 | tf_op jit(solution)/shard_map/ppermute | solution.py:19
  444.8 13.0 %collective-permute-start.22 = (f32[3,128,128]{1,2,0:T(8,128)S(1)}, f32[3,128,128]{1,2,0:T(8,128)S(1)}, u32[]{:S(2)}, u32[]{:S(2)}) collective-permute-start(f32[3,128,128]{1,2,0:T(8,128)S(1)} %add.128), channel_id=1, source_target_pairs={{0,4},{1,5},{2,6},{3,7},{4,0},{5,1},{6,2},{7,3},{8,12},{9,13},{10,... | collective-permute-start | bytes 589832 | tf_op jit(solution)/shard_map/ppermute | solution.py:19
  457.7 11.3 %collective-permute-start.23 = (f32[3,128,128]{1,2,0:T(8,128)S(1)}, f32[3,128,128]{1,2,0:T(8,128)S(1)}, u32[]{:S(2)}, u32[]{:S(2)}) collective-permute-start(f32[3,128,128]{1,2,0:T(8,128)S(1)} %add.129), channel_id=1, source_target_pairs={{0,8},{1,9},{2,10},{3,11},{4,12},{5,13},{6,14},{7,15},{8,0},{9,1},... | collective-permute-start | bytes 589832 | tf_op jit(solution)/shard_map/ppermute | solution.py:19

commit v8 on v7

--- a/solution.py
+++ b/solution.py
@@ -87,11 +87,9 @@
     core_tensor = jnp.einsum("xr,sxc->src", basis, fibers, precision=highest)
     n_gy = lax.axis_size("gy")
     n_gx = lax.axis_size("gx")
-    by_rank = jnp.swapaxes(core_tensor.reshape(species, n_gy, R // n_gy, slab_z), 0, 1)
-    stage_one = lax.all_to_all(by_rank, "gy", split_axis=0, concat_axis=0, tiled=True)
-    pairs = stage_one.reshape(n_gy, n_gx, species * (R // n_gy) // n_gx, slab_z)
-    stage_two = lax.all_to_all(jnp.swapaxes(pairs, 0, 1), "gx", split_axis=0, concat_axis=0, tiled=True)
-    columns = jnp.swapaxes(stage_two, 0, 1).reshape(n_gy * n_gx, -1)
+    pairs = core_tensor.reshape(n_gx * n_gy, -1, slab_z)
+    gathered = lax.all_to_all(pairs, ("gx", "gy"), split_axis=0, concat_axis=0, tiled=True)
+    columns = jnp.swapaxes(gathered.reshape(n_gx, n_gy, -1), 0, 1).reshape(n_gy * n_gx, -1)
     second_part = jnp.einsum("yc,wc->yw", columns, columns, precision=highest) / (S * R * NZ)
     half_y = second_part.shape[0] // 2
     lower_two = jnp.stack([second_part[:half_y, :half_y], second_part[half_y:, :half_y], second_part[half_y:, half_y:]])

time: 474 us -> 465 us (0.981)
  blocking collectives: 38.5 us -> 31.3 us
  waiting for transfers between devices: 238 us -> 232 us
    all_to_all x2 -> x1, blocking collectives: 38.5 us -> 31.3 us  [body(): lax.all_to_all(pairs, ('gx', 'gy'), split_axis=0, concat_axis=0, tiled=True)]
    ppermute x8, waiting for transfers between devices: 52.2 us -> 46.2 us  [butterfly_sum(): lax.ppermute(value, axis, [(i, i ^ stride) for i in range(size)])]
    unnamed x46 -> x45, local copies, waits for them, and re-layouts: 9.78 us -> 9.75 us
where the time goes in v8:
time: 465 us; the launch traced here: 462 us
  waiting for transfers between devices  232 us (50%)
  other arithmetic  75.8 us (16%)
  starting transfers between devices  50.6 us (11%)
  matrix products  45.3 us (10%)
  blocking collectives  31.3 us (7%)
  local copies, waits for them, and re-layouts  25.5 us (5%)
    ppermute x8, waiting for transfers between devices, halving_doubling_sum(): other = lax.ppermute(value, axis, [(i, i ^ stride) for i in range(size)])  63.8 us
    all_to_all x1, waiting for transfers between devices, body(): lax.all_to_all(by_row, 'gx', split_axis=0, concat_axis=0, tiled=True)  60.9 us
    ppermute x8, waiting for transfers between devices, halving_doubling_sum(): lax.ppermute(send, axis, [(i, i ^ stride) for i in range(size)])  60.7 us
    ppermute x8, waiting for transfers between devices, butterfly_sum(): lax.ppermute(value, axis, [(i, i ^ stride) for i in range(size)])  46.2 us
    another operation x9, other arithmetic, body(): factor_low = jnp.linalg.cholesky(square)  37.2 us
    another operation x6, other arithmetic, body(): lax.linalg.triangular_solve(factor_low, wide, left_side=False, lower=True...  31.8 us
    all_to_all x1, blocking collectives, body(): lax.all_to_all(pairs, ('gx', 'gy'), split_axis=0, concat_axis=0, tiled=True)  31.3 us
    dot_general x8, matrix products, body(): jnp.einsum('sxc,swc->xw', fibers[:, row * BLOCK:(row + 1) * BLOCK], fiber...  20.1 us
  transfers between devices with their start and end apart: 25, of which 25 were waited for; matrix products, arithmetic and copies ran while one was open for 0% of the time, Pallas kernels for 0%

profile of v8, /device:TPU:6, one launch (start us, length us, event | category | flops | bytes accessed | tf_op | source)
XLA Modules:
  0.0 461.9 jit_solution(5565891931104295877)
XLA Ops:
  0.6 6.7 %copy.62 = f32[4,64,16,256]{3,1,0,2:T(8,128)} copy(f32[4,64,16,256]{3,2,1,0:T(8,128)} %param.6) | data formatting | bytes 8388608 | tf_op args[0]
  7.3 6.6 %all-to-all-start = ((f32[16,4,64,256]{3,2,1,0:T(8,128)}), f32[16,4,64,256]{3,2,1,0:T(8,128)}, u32[]{:S(2)}, u32[]{:S(2)}) async-start(f32[16,4,64,256]{3,2,1,0:T(8,128)} %bitcast.141), calls=%async_computation | async-start | bytes 8388608 | tf_op jit(solution)/shard_map/all_to_all | solution.py:53
  14.0 60.9 %all-to-all-done = f32[16,4,64,256]{3,2,1,0:T(8,128)} async-done(((f32[16,4,64,256]{3,2,1,0:T(8,128)}), f32[16,4,64,256]{3,2,1,0:T(8,128)}, u32[]{:S(2)}, u32[]{:S(2)}) %all-to-all-start) | async-done | bytes 4194336 | tf_op jit(solution)/shard_map/all_to_all | solution.py:53
  74.8 2.5 copy.35
  77.3 1.2 fusion.50
  79.1 1.5 fusion.47
  80.6 2.3 fusion.41
  82.9 2.7 fusion.38
  85.6 3.3 fusion.32
  88.9 4.1 fusion.26
  93.0 4.4 fusion.19
  99.0 1.6 collective-permute-start
  100.6 26.8 %collective-permute-done = f32[2304,128]{1,0:T(8,128)} collective-permute-done((f32[2304,128]{1,0:T(8,128)S(1)}, f32[2304,128]{1,0:T(8,128)}, u32[]{:S(2)}, u32[]{:S(2)}) %collective-permute-start) | collective-permute-done | bytes 1179680 | tf_op jit(solution)/shard_map/ppermute | solution.py:42
  127.4 1.4 select_add_fusion
  129.0 16.2 %collective-permute-done.1 = f32[1152,128]{1,0:T(8,128)S(1)} collective-permute-done((f32[1152,128]{1,0:T(8,128)S(1)}, f32[1152,128]{1,0:T(8,128)S(1)}, u32[]{:S(2)}, u32[]{:S(2)}) %collective-permute-start.1) | collective-permute-done | bytes 589856 | tf_op jit(solution)/shard_map/ppermute | solution.py:42
  145.5 7.6 %collective-permute-done.2 = f32[576,128]{1,0:T(8,128)S(1)} collective-permute-done((f32[576,128]{1,0:T(8,128)S(1)}, f32[576,128]{1,0:T(8,128)S(1)}, u32[]{:S(2)}, u32[]{:S(2)}) %collective-permute-start.2) | collective-permute-done | bytes 294944 | tf_op jit(solution)/shard_map/ppermute | solution.py:42
  153.3 1.3 collective-permute-done.3
  154.7 7.1 %collective-permute-start.4 = (f32[144,128]{1,0:T(8,128)S(1)}, f32[144,128]{1,0:T(8,128)S(1)}, u32[]{:S(2)}, u32[]{:S(2)}) collective-permute-start(f32[144,128]{1,0:T(8,128)S(1)} %slice_select_fusion.3), channel_id=1, source_target_pairs={{0,8},{1,9},{2,10},{3,11},{4,12},{5,13},{6,14},{7,15},{8,0},{9,1},... | collective-permute-start | bytes 221192 | tf_op jit(solution)/shard_map/ppermute | solution.py:42
  161.8 2.7 collective-permute-done.4
  164.5 4.0 collective-permute-start.5
  168.5 1.9 collective-permute-done.5
  170.5 3.3 collective-permute-start.6
  173.8 2.1 collective-permute-done.6
  175.9 1.7 collective-permute-start.7
  177.6 2.1 collective-permute-done.7
  179.7 1.6 collective-permute-start.8
  181.3 2.1 collective-permute-done.8
  183.4 3.3 collective-permute-start.9
  186.7 2.1 collective-permute-done.9
  188.8 3.0 collective-permute-start.10
  191.8 3.9 collective-permute-done.10
  195.6 4.3 collective-permute-start.11
  199.9 4.1 collective-permute-done.11
  204.1 1.4 collective-permute-done.12
  205.9 8.8 %collective-permute-done.13 = f32[576,128]{1,0:T(8,128)S(1)} collective-permute-done((f32[576,128]{1,0:T(8,128)S(1)}, f32[576,128]{1,0:T(8,128)S(1)}, u32[]{:S(2)}, u32[]{:S(2)}) %collective-permute-start.13) | collective-permute-done | bytes 294944 | tf_op jit(solution)/shard_map/ppermute | solution.py:45
  215.3 15.5 %collective-permute-done.14 = f32[1152,128]{1,0:T(8,128)S(1)} collective-permute-done((f32[1152,128]{1,0:T(8,128)S(1)}, f32[1152,128]{1,0:T(8,128)S(1)}, u32[]{:S(2)}, u32[]{:S(2)}) %collective-permute-start.14) | collective-permute-done | bytes 589856 | tf_op jit(solution)/shard_map/ppermute | solution.py:45
  231.2 26.1 %collective-permute-done.15 = f32[2304,128]{1,0:T(8,128)S(1)} collective-permute-done((f32[2304,128]{1,0:T(8,128)S(1)}, f32[2304,128]{1,0:T(8,128)S(1)}, u32[]{:S(2)}, u32[]{:S(2)}) %collective-permute-start.15) | collective-permute-done | bytes 1179680 | tf_op jit(solution)/shard_map/ppermute | solution.py:45
  257.6 2.1 copy.36
  259.7 4.3 pad_maximum_fusion
  263.9 5.2 %gather_fusion = f32[64,128,128]{2,1,0:T(8,128)} fusion(f32[72,128,128]{2,1,0:T(8,128)} %pad_maximum_fusion, s32[1024]{0:T(1024)S(1)} %pad_clamp_fusion), kind=kCustom, calls=%fused_computation | custom fusion | bytes 8388864 | tf_op jit(solution)/shard_map/jit(_take)/gather | solution.py:79
  269.2 4.6 copy.37
  273.7 3.5 fusion.4
  278.3 11.7 %cholesky.59 = f32[128,128]{1,0:T(8,128)S(1)} custom-call(f32[128,128]{1,0:T(8,128)S(1)} %fusion.72), custom_call_target="Cholesky" | custom-call | tf_op jit(solution)/shard_map/jit(cholesky)/cholesky | solution.py:85
  291.4 10.2 %custom-call.7 = f32[1,128,128]{1,2,0:T(8,128)S(1)} custom-call(f32[1,128,128]{2,1,0:T(8,128)S(1)} %fusion.63), custom_call_target="InvertDiagBlocksLowerTriangular" | custom-call | tf_op jit(solution)/shard_map/triangular_solve/custom-call.0 | solution.py:86
  302.2 5.7 %fusion.2 = f32[1024,128]{1,0:T(8,128)S(1)} fusion(f32[1024,128]{0,1:T(8,128)S(1)} %convolution_bitcast_fusion.1, f32[128,8,8,128]{3,2,1,0:T(8,128)} %bitcast.137), kind=kOutput, calls=%fused_computation.4 | convolution fusion | flops 1610612736 | bytes 5242880 | tf_op jit(solution)/shard_map/dot_general | solution.py:83
  309.1 11.7 %cholesky.70 = f32[128,128]{1,0:T(8,128)S(1)} custom-call(f32[128,128]{1,0:T(8,128)S(1)} %fusion.70), custom_call_target="Cholesky" | custom-call | tf_op jit(solution)/shard_map/jit(cholesky)/cholesky | solution.py:85
  322.2 9.8 %custom-call.8 = f32[1,128,128]{1,2,0:T(8,128)S(1)} custom-call(f32[1,128,128]{2,1,0:T(8,128)S(1)} %fusion.64), custom_call_target="InvertDiagBlocksLowerTriangular" | custom-call | tf_op jit(solution)/shard_map/triangular_solve/custom-call.0 | solution.py:86
  332.6 5.9 %fusion = f32[1024,128]{1,0:T(8,128)S(1)} fusion(f32[1024,128]{0,1:T(8,128)S(1)} %convolution_bitcast_fusion, f32[128,8,8,128]{3,2,1,0:T(8,128)} %bitcast.138), kind=kOutput, calls=%fused_computation.2 | convolution fusion | flops 1610612736 | bytes 5242880 | tf_op jit(solution)/shard_map/dot_general | solution.py:83
  339.7 11.7 %cholesky.81 = f32[128,128]{1,0:T(8,128)S(1)} custom-call(f32[128,128]{1,0:T(8,128)S(1)} %fusion.68), custom_call_target="Cholesky" | custom-call | tf_op jit(solution)/shard_map/jit(cholesky)/cholesky | solution.py:85
  352.7 9.8 %custom-call.9 = f32[1,128,128]{1,2,0:T(8,128)S(1)} custom-call(f32[1,128,128]{2,1,0:T(8,128)S(1)} %fusion.65), custom_call_target="InvertDiagBlocksLowerTriangular" | custom-call | tf_op jit(solution)/shard_map/triangular_solve/custom-call.0 | solution.py:86
  363.2 4.6 convolution_bitcast_fusion.2
  368.1 31.3 %all_to_all.10 = f32[256,2,256]{2,1,0:T(2,128)S(1)} all-to-all(f32[256,2,256]{2,1,0:T(2,128)S(1)} %reshape.42), channel_id=1, replica_groups=mesh['gx'=16,'gy'=16] {'gx','gy'}, dimensions={0} | all-to-all | bytes 1048576 | tf_op jit(solution)/shard_map/all_to_all | solution.py:91
  400.9 1.4 collective-permute-done.16
  402.4 1.5 collective-permute-start.17
  403.9 5.6 %collective-permute-done.17 = f32[3,128,128]{1,2,0:T(8,128)S(1)} collective-permute-done((f32[3,128,128]{1,2,0:T(8,128)S(1)}, f32[3,128,128]{1,2,0:T(8,128)S(1)}, u32[]{:S(2)}, u32[]{:S(2)}) %collective-permute-start.17) | collective-permute-done | bytes 196640 | tf_op jit(solution)/shard_map/ppermute | solution.py:19
  409.4 2.4 collective-permute-start.18
  411.8 5.3 %collective-permute-done.18 = f32[3,128,128]{1,2,0:T(8,128)S(1)} collective-permute-done((f32[3,128,128]{1,2,0:T(8,128)S(1)}, f32[3,128,128]{1,2,0:T(8,128)S(1)}, u32[]{:S(2)}, u32[]{:S(2)}) %collective-permute-start.18) | collective-permute-done | bytes 196640 | tf_op jit(solution)/shard_map/ppermute | solution.py:19
  418.2 4.7 %collective-permute-done.19 = f32[3,128,128]{1,2,0:T(8,128)S(1)} collective-permute-done((f32[3,128,128]{1,2,0:T(8,128)S(1)}, f32[3,128,128]{1,2,0:T(8,128)S(1)}, u32[]{:S(2)}, u32[]{:S(2)}) %collective-permute-start.19) | collective-permute-done | bytes 196640 | tf_op jit(solution)/shard_map/ppermute | solution.py:19
  423.4 5.8 %collective-permute-done.20 = f32[3,128,128]{1,2,0:T(8,128)S(1)} collective-permute-done((f32[3,128,128]{1,2,0:T(8,128)S(1)}, f32[3,128,128]{1,2,0:T(8,128)S(1)}, u32[]{:S(2)}, u32[]{:S(2)}) %collective-permute-start.20) | collective-permute-done | bytes 196640 | tf_op jit(solution)/shard_map/ppermute | solution.py:19
  430.3 6.2 %collective-permute-done.21 = f32[3,128,128]{1,2,0:T(8,128)S(1)} collective-permute-done((f32[3,128,128]{1,2,0:T(8,128)S(1)}, f32[3,128,128]{1,2,0:T(8,128)S(1)}, u32[]{:S(2)}, u32[]{:S(2)}) %collective-permute-start.21) | collective-permute-done | bytes 196640 | tf_op jit(solution)/shard_map/ppermute | solution.py:19
  436.5 3.4 collective-permute-start.22
  439.9 10.0 %collective-permute-done.22 = f32[3,128,128]{1,2,0:T(8,128)S(1)} collective-permute-done((f32[3,128,128]{1,2,0:T(8,128)S(1)}, f32[3,128,128]{1,2,0:T(8,128)S(1)}, u32[]{:S(2)}, u32[]{:S(2)}) %collective-permute-start.22) | collective-permute-done | bytes 196640 | tf_op jit(solution)/shard_map/ppermute | solution.py:19
  449.9 2.4 collective-permute-start.23
  453.3 7.3 %collective-permute-done.23 = f32[3,128,128]{1,2,0:T(8,128)S(1)} collective-permute-done((f32[3,128,128]{1,2,0:T(8,128)S(1)}, f32[3,128,128]{1,2,0:T(8,128)S(1)}, u32[]{:S(2)}, u32[]{:S(2)}) %collective-permute-start.23) | collective-permute-done | bytes 196640 | tf_op jit(solution)/shard_map/ppermute | solution.py:19
  (118 shorter events, 20.1 us)
Async XLA Ops:
  0.6 273.1 %copy-start = (f32[1024,128]{1,0:T(8,128)S(1)}, f32[1024,128]{1,0:T(8,128)}, u32[]{:S(2)}) copy-start(f32[1024,128]{1,0:T(8,128)} %param.7) | copy-start | bytes 1572868
  7.3 67.5 %all-to-all-start = ((f32[16,4,64,256]{3,2,1,0:T(8,128)}), f32[16,4,64,256]{3,2,1,0:T(8,128)}, u32[]{:S(2)}, u32[]{:S(2)}) async-start(f32[16,4,64,256]{3,2,1,0:T(8,128)} %bitcast.141), calls=%async_computation | async-start | bytes 8388608 | tf_op jit(solution)/shard_map/all_to_all | solution.py:53
  77.3 15.7 %copy-start.1 = (f32[4,16,64,256]{3,2,1,0:T(8,128)}, f32[4,16,64,256]{3,2,1,0:T(8,128)S(1)}, u32[]{:S(2)}) copy-start(f32[4,16,64,256]{3,2,1,0:T(8,128)S(1)} %copy.35) | copy-start | bytes 12582916
  98.0 1.0 copy-start.3
  99.0 28.4 %collective-permute-start = (f32[2304,128]{1,0:T(8,128)S(1)}, f32[2304,128]{1,0:T(8,128)}, u32[]{:S(2)}, u32[]{:S(2)}) collective-permute-start(f32[2304,128]{1,0:T(8,128)S(1)} %broadcast_select_fusion), channel_id=1, source_target_pairs={{0,128},{16,144},{32,160},{48,176},{64,192},{80,208},{96,224},{112... | collective-permute-start | bytes 3538952 | tf_op jit(solution)/shard_map/ppermute | solution.py:42
  128.9 16.4 %collective-permute-start.1 = (f32[1152,128]{1,0:T(8,128)S(1)}, f32[1152,128]{1,0:T(8,128)S(1)}, u32[]{:S(2)}, u32[]{:S(2)}) collective-permute-start(f32[1152,128]{1,0:T(8,128)S(1)} %slice_select_fusion), channel_id=1, source_target_pairs={{0,64},{16,80},{32,96},{48,112},{64,0},{80,16},{96,32},{112,48},{1... | collective-permute-start | bytes 1769480 | tf_op jit(solution)/shard_map/ppermute | solution.py:42
  145.4 7.7 %collective-permute-start.2 = (f32[576,128]{1,0:T(8,128)S(1)}, f32[576,128]{1,0:T(8,128)S(1)}, u32[]{:S(2)}, u32[]{:S(2)}) collective-permute-start(f32[576,128]{1,0:T(8,128)S(1)} %slice_select_fusion.1), channel_id=1, source_target_pairs={{0,32},{16,48},{32,0},{48,16},{64,96},{80,112},{96,64},{112,80},{1... | collective-permute-start | bytes 884744 | tf_op jit(solution)/shard_map/ppermute | solution.py:42
  153.2 1.5 collective-permute-start.3
  154.7 9.8 %collective-permute-start.4 = (f32[144,128]{1,0:T(8,128)S(1)}, f32[144,128]{1,0:T(8,128)S(1)}, u32[]{:S(2)}, u32[]{:S(2)}) collective-permute-start(f32[144,128]{1,0:T(8,128)S(1)} %slice_select_fusion.3), channel_id=1, source_target_pairs={{0,8},{1,9},{2,10},{3,11},{4,12},{5,13},{6,14},{7,15},{8,0},{9,1},... | collective-permute-start | bytes 221192 | tf_op jit(solution)/shard_map/ppermute | solution.py:42
  164.5 6.0 %collective-permute-start.5 = (f32[72,128]{1,0:T(8,128)S(1)}, f32[72,128]{1,0:T(8,128)S(1)}, u32[]{:S(2)}, u32[]{:S(2)}) collective-permute-start(f32[72,128]{1,0:T(8,128)S(1)} %slice_select_fusion.4), channel_id=1, source_target_pairs={{0,4},{1,5},{2,6},{3,7},{4,0},{5,1},{6,2},{7,3},{8,12},{9,13},{10,... | collective-permute-start | bytes 110600 | tf_op jit(solution)/shard_map/ppermute | solution.py:42
  170.5 5.4 %collective-permute-start.6 = (f32[36,128]{1,0:T(8,128)S(1)}, f32[36,128]{1,0:T(8,128)S(1)}, u32[]{:S(2)}, u32[]{:S(2)}) collective-permute-start(f32[36,128]{1,0:T(8,128)S(1)} %slice_select_fusion.5), channel_id=1, source_target_pairs={{0,2},{1,3},{2,0},{3,1},{4,6},{5,7},{6,4},{7,5},{8,10},{9,11},{10,... | collective-permute-start | bytes 55304 | tf_op jit(solution)/shard_map/ppermute | solution.py:42
  175.9 3.8 collective-permute-start.7
  179.7 3.7 collective-permute-start.8
  183.4 5.4 %collective-permute-start.9 = (f32[36,128]{1,0:T(8,128)S(1)}, f32[36,128]{1,0:T(8,128)S(1)}, u32[]{:S(2)}, u32[]{:S(2)}) collective-permute-start(f32[36,128]{1,0:T(8,128)S(1)} %maximum_select_fusion.7), channel_id=1, source_target_pairs={{0,2},{1,3},{2,0},{3,1},{4,6},{5,7},{6,4},{7,5},{8,10},{9,11},{10,... | collective-permute-start | bytes 55304 | tf_op jit(solution)/shard_map/ppermute | solution.py:45
  188.8 6.9 %collective-permute-start.10 = (f32[72,128]{1,0:T(8,128)S(1)}, f32[72,128]{1,0:T(8,128)S(1)}, u32[]{:S(2)}, u32[]{:S(2)}) collective-permute-start(f32[72,128]{1,0:T(8,128)S(1)} %maximum_select_fusion.6), channel_id=1, source_target_pairs={{0,4},{1,5},{2,6},{3,7},{4,0},{5,1},{6,2},{7,3},{8,12},{9,13},{10,... | collective-permute-start | bytes 110600 | tf_op jit(solution)/shard_map/ppermute | solution.py:45
  195.6 8.3 %collective-permute-start.11 = (f32[144,128]{1,0:T(8,128)S(1)}, f32[144,128]{1,0:T(8,128)S(1)}, u32[]{:S(2)}, u32[]{:S(2)}) collective-permute-start(f32[144,128]{1,0:T(8,128)S(1)} %maximum_select_fusion.5), channel_id=1, source_target_pairs={{0,8},{1,9},{2,10},{3,11},{4,12},{5,13},{6,14},{7,15},{8,0},{9,1},... | collective-permute-start | bytes 221192 | tf_op jit(solution)/shard_map/ppermute | solution.py:45
  204.0 1.5 collective-permute-start.12
  205.5 9.1 %collective-permute-start.13 = (f32[576,128]{1,0:T(8,128)S(1)}, f32[576,128]{1,0:T(8,128)S(1)}, u32[]{:S(2)}, u32[]{:S(2)}) collective-permute-start(f32[576,128]{1,0:T(8,128)S(1)} %maximum_select_fusion.3), channel_id=1, source_target_pairs={{0,32},{16,48},{32,0},{48,16},{64,96},{80,112},{96,64},{112,80},{1... | collective-permute-start | bytes 884744 | tf_op jit(solution)/shard_map/ppermute | solution.py:45
  214.7 16.5 %copy-start.4 = (s32[64]{0:T(128)S(1)}, s32[64]{0:T(128)}, u32[]{:S(2)}) copy-start(s32[64]{0:T(128)} %constant.217) | copy-start | bytes 772
  214.7 16.1 %collective-permute-start.14 = (f32[1152,128]{1,0:T(8,128)S(1)}, f32[1152,128]{1,0:T(8,128)S(1)}, u32[]{:S(2)}, u32[]{:S(2)}) collective-permute-start(f32[1152,128]{1,0:T(8,128)S(1)} %maximum_select_fusion.2), channel_id=1, source_target_pairs={{0,64},{16,80},{32,96},{48,112},{64,0},{80,16},{96,32},{112,48},{1... | collective-permute-start | bytes 1769480 | tf_op jit(solution)/shard_map/ppermute | solution.py:45
  230.9 26.4 %collective-permute-start.15 = (f32[2304,128]{1,0:T(8,128)S(1)}, f32[2304,128]{1,0:T(8,128)S(1)}, u32[]{:S(2)}, u32[]{:S(2)}) collective-permute-start(f32[2304,128]{1,0:T(8,128)S(1)} %maximum_select_fusion.1), channel_id=1, source_target_pairs={{0,128},{16,144},{32,160},{48,176},{64,192},{80,208},{96,224},{112... | collective-permute-start | bytes 3538952 | tf_op jit(solution)/shard_map/ppermute | solution.py:45
  273.7 3.5 copy-start.2
  400.8 1.5 collective-permute-start.16
  402.4 7.0 %collective-permute-start.17 = (f32[3,128,128]{1,2,0:T(8,128)S(1)}, f32[3,128,128]{1,2,0:T(8,128)S(1)}, u32[]{:S(2)}, u32[]{:S(2)}) collective-permute-start(f32[3,128,128]{1,2,0:T(8,128)S(1)} %fusion.77), channel_id=1, source_target_pairs={{0,32},{16,48},{32,0},{48,16},{64,96},{80,112},{96,64},{112,80},{1... | collective-permute-start | bytes 589832 | tf_op jit(solution)/shard_map/ppermute | solution.py:19
  409.4 7.7 %collective-permute-start.18 = (f32[3,128,128]{1,2,0:T(8,128)S(1)}, f32[3,128,128]{1,2,0:T(8,128)S(1)}, u32[]{:S(2)}, u32[]{:S(2)}) collective-permute-start(f32[3,128,128]{1,2,0:T(8,128)S(1)} %fusion.97), channel_id=1, source_target_pairs={{0,64},{16,80},{32,96},{48,112},{64,0},{80,16},{96,32},{112,48},{1... | collective-permute-start | bytes 589832 | tf_op jit(solution)/shard_map/ppermute | solution.py:19
  417.2 5.8 %collective-permute-start.19 = (f32[3,128,128]{1,2,0:T(8,128)S(1)}, f32[3,128,128]{1,2,0:T(8,128)S(1)}, u32[]{:S(2)}, u32[]{:S(2)}) collective-permute-start(f32[3,128,128]{1,2,0:T(8,128)S(1)} %add.125), channel_id=1, source_target_pairs={{0,128},{16,144},{32,160},{48,176},{64,192},{80,208},{96,224},{112... | collective-permute-start | bytes 589832 | tf_op jit(solution)/shard_map/ppermute | solution.py:19
  422.9 6.2 %collective-permute-start.20 = (f32[3,128,128]{1,2,0:T(8,128)S(1)}, f32[3,128,128]{1,2,0:T(8,128)S(1)}, u32[]{:S(2)}, u32[]{:S(2)}) collective-permute-start(f32[3,128,128]{1,2,0:T(8,128)S(1)} %add.126), channel_id=1, source_target_pairs={{0,1},{1,0},{2,3},{3,2},{4,5},{5,4},{6,7},{7,6},{8,9},{9,8},{10,11... | collective-permute-start | bytes 589832 | tf_op jit(solution)/shard_map/ppermute | solution.py:19
  429.2 7.3 %collective-permute-start.21 = (f32[3,128,128]{1,2,0:T(8,128)S(1)}, f32[3,128,128]{1,2,0:T(8,128)S(1)}, u32[]{:S(2)}, u32[]{:S(2)}) collective-permute-start(f32[3,128,128]{1,2,0:T(8,128)S(1)} %add.127), channel_id=1, source_target_pairs={{0,2},{1,3},{2,0},{3,1},{4,6},{5,7},{6,4},{7,5},{8,10},{9,11},{10,... | collective-permute-start | bytes 589832 | tf_op jit(solution)/shard_map/ppermute | solution.py:19
  436.5 13.4 %collective-permute-start.22 = (f32[3,128,128]{1,2,0:T(8,128)S(1)}, f32[3,128,128]{1,2,0:T(8,128)S(1)}, u32[]{:S(2)}, u32[]{:S(2)}) collective-permute-start(f32[3,128,128]{1,2,0:T(8,128)S(1)} %add.128), channel_id=1, source_target_pairs={{0,4},{1,5},{2,6},{3,7},{4,0},{5,1},{6,2},{7,3},{8,12},{9,13},{10,... | collective-permute-start | bytes 589832 | tf_op jit(solution)/shard_map/ppermute | solution.py:19
  449.9 10.7 %collective-permute-start.23 = (f32[3,128,128]{1,2,0:T(8,128)S(1)}, f32[3,128,128]{1,2,0:T(8,128)S(1)}, u32[]{:S(2)}, u32[]{:S(2)}) collective-permute-start(f32[3,128,128]{1,2,0:T(8,128)S(1)} %add.129), channel_id=1, source_target_pairs={{0,8},{1,9},{2,10},{3,11},{4,12},{5,13},{6,14},{7,15},{8,0},{9,1},... | collective-permute-start | bytes 589832 | tf_op jit(solution)/shard_map/ppermute | solution.py:19

commit v9 on v8

--- a/solution.py
+++ b/solution.py
@@ -31,7 +31,7 @@
     return steps
 
 
-def halving_doubling_sum(value, sizes):
+def halving_doubling_sum(value, sizes, middle=None):
     steps = halving_steps(sizes)
     for axis, size, stride in steps:
         upper = (lax.axis_index(axis) // stride) % 2 == 1
@@ -40,6 +40,8 @@
         keep = jnp.where(upper, high, low)
         send = jnp.where(upper, low, high)
         value = keep + lax.ppermute(send, axis, [(i, i ^ stride) for i in range(size)])
+    if middle is not None:
+        value = middle(value)
     for axis, size, stride in reversed(steps):
         upper = (lax.axis_index(axis) // stride) % 2 == 1
         other = lax.ppermute(value, axis, [(i, i ^ stride) for i in range(size)])
@@ -67,7 +69,7 @@
         lower.extend(strip[:, col * BLOCK:(col + 1) * BLOCK] for col in range(row + 1))
     packed = jnp.concatenate(lower, axis=0)
     sizes = (("gx", lax.axis_size("gx")), ("gy", lax.axis_size("gy")))
-    packed = halving_doubling_sum(packed, sizes)
+    packed = halving_doubling_sum(packed, sizes[:1], middle=lambda chunk: butterfly_sum(chunk, *sizes[1]))
     blocks = packed.reshape(-1, BLOCK, BLOCK)
     both = jnp.concatenate([blocks, jnp.swapaxes(blocks, 1, 2)], axis=0)
     index = {}

time: 465 us -> 448 us (0.963)
  starting transfers between devices: 50.6 us -> 37.2 us
    ppermute x8 -> x12, waiting for transfers between devices: 46.2 us -> 64.3 us  [butterfly_sum(): lax.ppermute(value, axis, [(i, i ^ stride) for i in range(size)])]
    ppermute x8 -> x4, starting transfers between devices: 18 us -> 1.88 us  [halving_doubling_sum(): lax.ppermute(send, axis, [(i, i ^ stride) for i in range(size)])]
    ppermute x8 -> x12, starting transfers between devices: 12.4 us -> 27.3 us  [butterfly_sum(): lax.ppermute(value, axis, [(i, i ^ stride) for i in range(size)])]
    ppermute x8 -> x4, starting transfers between devices: 13.6 us -> 1.41 us  [halving_doubling_sum(): other = lax.ppermute(value, axis, [(i, i ^ stride) for i in range(size)])]
    ppermute x8 -> x4, waiting for transfers between devices: 63.8 us -> 51.7 us  [halving_doubling_sum(): other = lax.ppermute(value, axis, [(i, i ^ stride) for i in range(size)])]
    ppermute x8 -> x4, waiting for transfers between devices: 60.7 us -> 51.9 us  [halving_doubling_sum(): lax.ppermute(send, axis, [(i, i ^ stride) for i in range(size)])]
  transfers between devices with their start and end apart: 25 -> 21, of which waited for: 25 -> 21; matrix products, arithmetic and copies ran while one was open for 0% -> 0% of each run, Pallas kernels for 0% -> 0%
where the time goes in v9:
time: 448 us; the launch traced here: 445 us
  waiting for transfers between devices  229 us (51%)
  other arithmetic  75.8 us (17%)
  matrix products  45.3 us (10%)
  starting transfers between devices  37.2 us (8%)
  blocking collectives  30.7 us (7%)
  local copies, waits for them, and re-layouts  25.5 us (6%)
    ppermute x12, waiting for transfers between devices, butterfly_sum(): lax.ppermute(value, axis, [(i, i ^ stride) for i in range(size)])  64.3 us
    all_to_all x1, waiting for transfers between devices, body(): lax.all_to_all(by_row, 'gx', split_axis=0, concat_axis=0, tiled=True)  60.9 us
    ppermute x4, waiting for transfers between devices, halving_doubling_sum(): lax.ppermute(send, axis, [(i, i ^ stride) for i in range(size)])  51.9 us
    ppermute x4, waiting for transfers between devices, halving_doubling_sum(): other = lax.ppermute(value, axis, [(i, i ^ stride) for i in range(size)])  51.7 us
    another operation x9, other arithmetic, body(): factor_low = jnp.linalg.cholesky(square)  37.2 us
    another operation x6, other arithmetic, body(): lax.linalg.triangular_solve(factor_low, wide, left_side=False, lower=True...  31.8 us
    all_to_all x1, blocking collectives, body(): lax.all_to_all(pairs, ('gx', 'gy'), split_axis=0, concat_axis=0, tiled=True)  30.7 us
    ppermute x12, starting transfers between devices, butterfly_sum(): lax.ppermute(value, axis, [(i, i ^ stride) for i in range(size)])  27.3 us
  transfers between devices with their start and end apart: 21, of which 21 were waited for; matrix products, arithmetic and copies ran while one was open for 0% of the time, Pallas kernels for 0%

profile of v9, /device:TPU:6, one launch (start us, length us, event | category | flops | bytes accessed | tf_op | source)
XLA Modules:
  0.0 445.0 jit_solution(3694103206896436040)
XLA Ops:
  0.6 6.6 %copy.62 = f32[4,64,16,256]{3,1,0,2:T(8,128)} copy(f32[4,64,16,256]{3,2,1,0:T(8,128)} %param.6) | data formatting | bytes 8388608 | tf_op args[0]
  7.3 6.6 %all-to-all-start = ((f32[16,4,64,256]{3,2,1,0:T(8,128)}), f32[16,4,64,256]{3,2,1,0:T(8,128)}, u32[]{:S(2)}, u32[]{:S(2)}) async-start(f32[16,4,64,256]{3,2,1,0:T(8,128)} %bitcast.141), calls=%async_computation | async-start | bytes 8388608 | tf_op jit(solution)/shard_map/all_to_all | solution.py:55
  14.0 60.9 %all-to-all-done = f32[16,4,64,256]{3,2,1,0:T(8,128)} async-done(((f32[16,4,64,256]{3,2,1,0:T(8,128)}), f32[16,4,64,256]{3,2,1,0:T(8,128)}, u32[]{:S(2)}, u32[]{:S(2)}) %all-to-all-start) | async-done | bytes 4194336 | tf_op jit(solution)/shard_map/all_to_all | solution.py:55
  74.8 2.5 copy.35
  77.3 1.2 fusion.50
  79.1 1.5 fusion.47
  80.6 2.3 fusion.41
  82.9 2.7 fusion.38
  85.6 3.3 fusion.32
  88.9 4.1 fusion.26
  93.0 4.4 fusion.19
  98.2 0.9 copy-done.3
  99.0 1.6 collective-permute-start
  100.6 26.8 %collective-permute-done = f32[2304,128]{1,0:T(8,128)} collective-permute-done((f32[2304,128]{1,0:T(8,128)S(1)}, f32[2304,128]{1,0:T(8,128)}, u32[]{:S(2)}, u32[]{:S(2)}) %collective-permute-start) | collective-permute-done | bytes 1179680 | tf_op jit(solution)/shard_map/ppermute | solution.py:42
  127.4 1.4 select_add_fusion
  129.1 16.2 %collective-permute-done.1 = f32[1152,128]{1,0:T(8,128)S(1)} collective-permute-done((f32[1152,128]{1,0:T(8,128)S(1)}, f32[1152,128]{1,0:T(8,128)S(1)}, u32[]{:S(2)}, u32[]{:S(2)}) %collective-permute-start.1) | collective-permute-done | bytes 589856 | tf_op jit(solution)/shard_map/ppermute | solution.py:42
  145.5 7.6 %collective-permute-done.2 = f32[576,128]{1,0:T(8,128)S(1)} collective-permute-done((f32[576,128]{1,0:T(8,128)S(1)}, f32[576,128]{1,0:T(8,128)S(1)}, u32[]{:S(2)}, u32[]{:S(2)}) %collective-permute-start.2) | collective-permute-done | bytes 294944 | tf_op jit(solution)/shard_map/ppermute | solution.py:42
  153.3 1.4 collective-permute-done.3
  154.7 2.4 collective-permute-start.4
  157.1 4.2 collective-permute-done.4
  161.3 3.4 collective-permute-start.5
  164.7 3.5 collective-permute-done.5
  168.2 3.3 collective-permute-start.6
  171.5 5.3 %collective-permute-done.6 = f32[288,128]{1,0:T(8,128)S(1)} collective-permute-done((f32[288,128]{1,0:T(8,128)S(1)}, f32[288,128]{1,0:T(8,128)S(1)}, u32[]{:S(2)}, u32[]{:S(2)}) %collective-permute-start.6) | collective-permute-done | bytes 147488 | tf_op jit(solution)/shard_map/ppermute | solution.py:19
  176.9 5.7 %collective-permute-start.7 = (f32[288,128]{1,0:T(8,128)S(1)}, f32[288,128]{1,0:T(8,128)S(1)}, u32[]{:S(2)}, u32[]{:S(2)}) collective-permute-start(f32[288,128]{1,0:T(8,128)S(1)} %add.97), channel_id=1, source_target_pairs={{0,8},{1,9},{2,10},{3,11},{4,12},{5,13},{6,14},{7,15},{8,0},{9,1},... | collective-permute-start | bytes 442376 | tf_op jit(solution)/shard_map/ppermute | solution.py:19
  182.6 5.1 %collective-permute-done.7 = f32[288,128]{1,0:T(8,128)S(1)} collective-permute-done((f32[288,128]{1,0:T(8,128)S(1)}, f32[288,128]{1,0:T(8,128)S(1)}, u32[]{:S(2)}, u32[]{:S(2)}) %collective-permute-start.7) | collective-permute-done | bytes 147488 | tf_op jit(solution)/shard_map/ppermute | solution.py:19
  187.9 1.4 collective-permute-done.8
  189.6 8.8 %collective-permute-done.9 = f32[576,128]{1,0:T(8,128)S(1)} collective-permute-done((f32[576,128]{1,0:T(8,128)S(1)}, f32[576,128]{1,0:T(8,128)S(1)}, u32[]{:S(2)}, u32[]{:S(2)}) %collective-permute-start.9) | collective-permute-done | bytes 294944 | tf_op jit(solution)/shard_map/ppermute | solution.py:47
  199.1 15.5 %collective-permute-done.10 = f32[1152,128]{1,0:T(8,128)S(1)} collective-permute-done((f32[1152,128]{1,0:T(8,128)S(1)}, f32[1152,128]{1,0:T(8,128)S(1)}, u32[]{:S(2)}, u32[]{:S(2)}) %collective-permute-start.10) | collective-permute-done | bytes 589856 | tf_op jit(solution)/shard_map/ppermute | solution.py:47
  215.0 26.1 %collective-permute-done.11 = f32[2304,128]{1,0:T(8,128)S(1)} collective-permute-done((f32[2304,128]{1,0:T(8,128)S(1)}, f32[2304,128]{1,0:T(8,128)S(1)}, u32[]{:S(2)}, u32[]{:S(2)}) %collective-permute-start.11) | collective-permute-done | bytes 1179680 | tf_op jit(solution)/shard_map/ppermute | solution.py:47
  241.3 2.1 copy.36
  243.5 4.3 pad_maximum_fusion
  247.7 5.2 %gather_fusion = f32[64,128,128]{2,1,0:T(8,128)} fusion(f32[72,128,128]{2,1,0:T(8,128)} %pad_maximum_fusion, s32[1024]{0:T(1024)S(1)} %pad_clamp_fusion), kind=kCustom, calls=%fused_computation | custom fusion | bytes 8388864 | tf_op jit(solution)/shard_map/jit(_take)/gather | solution.py:81
  252.9 4.6 %copy.37 = f32[8,128,8,128]{3,2,1,0:T(8,128)S(1)} copy(f32[8,128,8,128]{3,1,2,0:T(8,128)} %bitcast.142) | data formatting | bytes 8388608 | tf_op jit(solution)/shard_map/jit(_take)/select_n | solution.py:81
  257.5 3.5 fusion.4
  261.0 1.0 fusion.78
  262.1 11.7 %cholesky.59 = f32[128,128]{1,0:T(8,128)S(1)} custom-call(f32[128,128]{1,0:T(8,128)S(1)} %fusion.72), custom_call_target="Cholesky" | custom-call | tf_op jit(solution)/shard_map/jit(cholesky)/cholesky | solution.py:87
  275.2 10.2 %custom-call.7 = f32[1,128,128]{1,2,0:T(8,128)S(1)} custom-call(f32[1,128,128]{2,1,0:T(8,128)S(1)} %fusion.63), custom_call_target="InvertDiagBlocksLowerTriangular" | custom-call | tf_op jit(solution)/shard_map/triangular_solve/custom-call.0 | solution.py:88
  286.0 5.7 %fusion.2 = f32[1024,128]{1,0:T(8,128)S(1)} fusion(f32[1024,128]{0,1:T(8,128)S(1)} %convolution_bitcast_fusion.1, f32[128,8,8,128]{3,2,1,0:T(8,128)} %bitcast.137), kind=kOutput, calls=%fused_computation.4 | convolution fusion | flops 1610612736 | bytes 5242880 | tf_op jit(solution)/shard_map/dot_general | solution.py:85
  291.7 1.0 fusion.79
  292.9 11.7 %cholesky.70 = f32[128,128]{1,0:T(8,128)S(1)} custom-call(f32[128,128]{1,0:T(8,128)S(1)} %fusion.70), custom_call_target="Cholesky" | custom-call | tf_op jit(solution)/shard_map/jit(cholesky)/cholesky | solution.py:87
  305.9 9.8 %custom-call.8 = f32[1,128,128]{1,2,0:T(8,128)S(1)} custom-call(f32[1,128,128]{2,1,0:T(8,128)S(1)} %fusion.64), custom_call_target="InvertDiagBlocksLowerTriangular" | custom-call | tf_op jit(solution)/shard_map/triangular_solve/custom-call.0 | solution.py:88
  316.4 5.9 %fusion = f32[1024,128]{1,0:T(8,128)S(1)} fusion(f32[1024,128]{0,1:T(8,128)S(1)} %convolution_bitcast_fusion, f32[128,8,8,128]{3,2,1,0:T(8,128)} %bitcast.138), kind=kOutput, calls=%fused_computation.2 | convolution fusion | flops 1610612736 | bytes 5242880 | tf_op jit(solution)/shard_map/dot_general | solution.py:85
  322.3 1.0 fusion.80
  323.4 11.7 %cholesky.81 = f32[128,128]{1,0:T(8,128)S(1)} custom-call(f32[128,128]{1,0:T(8,128)S(1)} %fusion.68), custom_call_target="Cholesky" | custom-call | tf_op jit(solution)/shard_map/jit(cholesky)/cholesky | solution.py:87
  336.5 9.8 %custom-call.9 = f32[1,128,128]{1,2,0:T(8,128)S(1)} custom-call(f32[1,128,128]{2,1,0:T(8,128)S(1)} %fusion.65), custom_call_target="InvertDiagBlocksLowerTriangular" | custom-call | tf_op jit(solution)/shard_map/triangular_solve/custom-call.0 | solution.py:88
  346.9 4.6 %convolution_bitcast_fusion.2 = f32[4,128,256]{2,1,0:T(8,128)S(1)} fusion(f32[4,1024,256]{2,1,0:T(8,128)} %bitcast.135, f32[128,1024]{1,0:T(8,128)S(1)} %get-tuple-element.26), kind=kOutput, calls=%fused_computation.25 | convolution fusion | flops 1610612736 | bytes 5242880 | tf_op jit(solution)/shard_map/xr,sxc->src/dot_general | solution.py:89
  351.8 30.7 %all_to_all.10 = f32[256,2,256]{2,1,0:T(2,128)S(1)} all-to-all(f32[256,2,256]{2,1,0:T(2,128)S(1)} %reshape.42), channel_id=1, replica_groups=mesh['gx'=16,'gy'=16] {'gx','gy'}, dimensions={0} | all-to-all | bytes 1048576 | tf_op jit(solution)/shard_map/all_to_all | solution.py:93
  384.1 1.4 collective-permute-done.12
  385.5 1.5 collective-permute-start.13
  387.0 5.6 %collective-permute-done.13 = f32[3,128,128]{1,2,0:T(8,128)S(1)} collective-permute-done((f32[3,128,128]{1,2,0:T(8,128)S(1)}, f32[3,128,128]{1,2,0:T(8,128)S(1)}, u32[]{:S(2)}, u32[]{:S(2)}) %collective-permute-start.13) | collective-permute-done | bytes 196640 | tf_op jit(solution)/shard_map/ppermute | solution.py:19
  392.6 2.4 collective-permute-start.14
  395.0 5.3 %collective-permute-done.14 = f32[3,128,128]{1,2,0:T(8,128)S(1)} collective-permute-done((f32[3,128,128]{1,2,0:T(8,128)S(1)}, f32[3,128,128]{1,2,0:T(8,128)S(1)}, u32[]{:S(2)}, u32[]{:S(2)}) %collective-permute-start.14) | collective-permute-done | bytes 196640 | tf_op jit(solution)/shard_map/ppermute | solution.py:19
  400.3 1.1 collective-permute-start.15
  401.4 4.7 %collective-permute-done.15 = f32[3,128,128]{1,2,0:T(8,128)S(1)} collective-permute-done((f32[3,128,128]{1,2,0:T(8,128)S(1)}, f32[3,128,128]{1,2,0:T(8,128)S(1)}, u32[]{:S(2)}, u32[]{:S(2)}) %collective-permute-start.15) | collective-permute-done | bytes 196640 | tf_op jit(solution)/shard_map/ppermute | solution.py:19
  406.5 5.8 %collective-permute-done.16 = f32[3,128,128]{1,2,0:T(8,128)S(1)} collective-permute-done((f32[3,128,128]{1,2,0:T(8,128)S(1)}, f32[3,128,128]{1,2,0:T(8,128)S(1)}, u32[]{:S(2)}, u32[]{:S(2)}) %collective-permute-start.16) | collective-permute-done | bytes 196640 | tf_op jit(solution)/shard_map/ppermute | solution.py:19
  412.3 1.1 collective-permute-start.17
  413.4 6.2 %collective-permute-done.17 = f32[3,128,128]{1,2,0:T(8,128)S(1)} collective-permute-done((f32[3,128,128]{1,2,0:T(8,128)S(1)}, f32[3,128,128]{1,2,0:T(8,128)S(1)}, u32[]{:S(2)}, u32[]{:S(2)}) %collective-permute-start.17) | collective-permute-done | bytes 196640 | tf_op jit(solution)/shard_map/ppermute | solution.py:19
  419.6 3.4 collective-permute-start.18
  423.0 10.0 %collective-permute-done.18 = f32[3,128,128]{1,2,0:T(8,128)S(1)} collective-permute-done((f32[3,128,128]{1,2,0:T(8,128)S(1)}, f32[3,128,128]{1,2,0:T(8,128)S(1)}, u32[]{:S(2)}, u32[]{:S(2)}) %collective-permute-start.18) | collective-permute-done | bytes 196640 | tf_op jit(solution)/shard_map/ppermute | solution.py:19
  433.0 2.4 collective-permute-start.19
  435.4 1.0 copy.44
  436.4 7.3 %collective-permute-done.19 = f32[3,128,128]{1,2,0:T(8,128)S(1)} collective-permute-done((f32[3,128,128]{1,2,0:T(8,128)S(1)}, f32[3,128,128]{1,2,0:T(8,128)S(1)}, u32[]{:S(2)}, u32[]{:S(2)}) %collective-permute-start.19) | collective-permute-done | bytes 196640 | tf_op jit(solution)/shard_map/ppermute | solution.py:19
  443.9 0.8 copy.45
  (102 shorter events, 12.2 us)
Async XLA Ops:
  0.6 256.9 %copy-start = (f32[1024,128]{1,0:T(8,128)S(1)}, f32[1024,128]{1,0:T(8,128)}, u32[]{:S(2)}) copy-start(f32[1024,128]{1,0:T(8,128)} %param.7) | copy-start | bytes 1572868
  7.3 67.5 %all-to-all-start = ((f32[16,4,64,256]{3,2,1,0:T(8,128)}), f32[16,4,64,256]{3,2,1,0:T(8,128)}, u32[]{:S(2)}, u32[]{:S(2)}) async-start(f32[16,4,64,256]{3,2,1,0:T(8,128)} %bitcast.141), calls=%async_computation | async-start | bytes 8388608 | tf_op jit(solution)/shard_map/all_to_all | solution.py:55
  77.3 15.7 %copy-start.1 = (f32[4,16,64,256]{3,2,1,0:T(8,128)}, f32[4,16,64,256]{3,2,1,0:T(8,128)S(1)}, u32[]{:S(2)}) copy-start(f32[4,16,64,256]{3,2,1,0:T(8,128)S(1)} %copy.35) | copy-start | bytes 12582916
  98.0 1.0 copy-start.3
  99.0 28.4 %collective-permute-start = (f32[2304,128]{1,0:T(8,128)S(1)}, f32[2304,128]{1,0:T(8,128)}, u32[]{:S(2)}, u32[]{:S(2)}) collective-permute-start(f32[2304,128]{1,0:T(8,128)S(1)} %broadcast_select_fusion), channel_id=1, source_target_pairs={{0,128},{16,144},{32,160},{48,176},{64,192},{80,208},{96,224},{112... | collective-permute-start | bytes 3538952 | tf_op jit(solution)/shard_map/ppermute | solution.py:42
  128.9 16.4 %collective-permute-start.1 = (f32[1152,128]{1,0:T(8,128)S(1)}, f32[1152,128]{1,0:T(8,128)S(1)}, u32[]{:S(2)}, u32[]{:S(2)}) collective-permute-start(f32[1152,128]{1,0:T(8,128)S(1)} %slice_select_fusion), channel_id=1, source_target_pairs={{0,64},{16,80},{32,96},{48,112},{64,0},{80,16},{96,32},{112,48},{1... | collective-permute-start | bytes 1769480 | tf_op jit(solution)/shard_map/ppermute | solution.py:42
  145.4 7.7 %collective-permute-start.2 = (f32[576,128]{1,0:T(8,128)S(1)}, f32[576,128]{1,0:T(8,128)S(1)}, u32[]{:S(2)}, u32[]{:S(2)}) collective-permute-start(f32[576,128]{1,0:T(8,128)S(1)} %slice_select_fusion.1), channel_id=1, source_target_pairs={{0,32},{16,48},{32,0},{48,16},{64,96},{80,112},{96,64},{112,80},{1... | collective-permute-start | bytes 884744 | tf_op jit(solution)/shard_map/ppermute | solution.py:42
  153.2 1.5 collective-permute-start.3
  154.7 6.6 %collective-permute-start.4 = (f32[288,128]{1,0:T(8,128)S(1)}, f32[288,128]{1,0:T(8,128)S(1)}, u32[]{:S(2)}, u32[]{:S(2)}) collective-permute-start(f32[288,128]{1,0:T(8,128)S(1)} %select_add_fusion.3), channel_id=1, source_target_pairs={{0,1},{1,0},{2,3},{3,2},{4,5},{5,4},{6,7},{7,6},{8,9},{9,8},{10,11... | collective-permute-start | bytes 442376 | tf_op jit(solution)/shard_map/ppermute | solution.py:19
  161.3 6.9 %collective-permute-start.5 = (f32[288,128]{1,0:T(8,128)S(1)}, f32[288,128]{1,0:T(8,128)S(1)}, u32[]{:S(2)}, u32[]{:S(2)}) collective-permute-start(f32[288,128]{1,0:T(8,128)S(1)} %add.95), channel_id=1, source_target_pairs={{0,2},{1,3},{2,0},{3,1},{4,6},{5,7},{6,4},{7,5},{8,10},{9,11},{10,... | collective-permute-start | bytes 442376 | tf_op jit(solution)/shard_map/ppermute | solution.py:19
  168.2 8.7 %collective-permute-start.6 = (f32[288,128]{1,0:T(8,128)S(1)}, f32[288,128]{1,0:T(8,128)S(1)}, u32[]{:S(2)}, u32[]{:S(2)}) collective-permute-start(f32[288,128]{1,0:T(8,128)S(1)} %add.96), channel_id=1, source_target_pairs={{0,4},{1,5},{2,6},{3,7},{4,0},{5,1},{6,2},{7,3},{8,12},{9,13},{10,... | collective-permute-start | bytes 442376 | tf_op jit(solution)/shard_map/ppermute | solution.py:19
  176.9 10.9 %collective-permute-start.7 = (f32[288,128]{1,0:T(8,128)S(1)}, f32[288,128]{1,0:T(8,128)S(1)}, u32[]{:S(2)}, u32[]{:S(2)}) collective-permute-start(f32[288,128]{1,0:T(8,128)S(1)} %add.97), channel_id=1, source_target_pairs={{0,8},{1,9},{2,10},{3,11},{4,12},{5,13},{6,14},{7,15},{8,0},{9,1},... | collective-permute-start | bytes 442376 | tf_op jit(solution)/shard_map/ppermute | solution.py:19
  187.8 1.5 collective-permute-start.8
  189.2 9.1 %collective-permute-start.9 = (f32[576,128]{1,0:T(8,128)S(1)}, f32[576,128]{1,0:T(8,128)S(1)}, u32[]{:S(2)}, u32[]{:S(2)}) collective-permute-start(f32[576,128]{1,0:T(8,128)S(1)} %maximum_select_fusion.3), channel_id=1, source_target_pairs={{0,32},{16,48},{32,0},{48,16},{64,96},{80,112},{96,64},{112,80},{1... | collective-permute-start | bytes 884744 | tf_op jit(solution)/shard_map/ppermute | solution.py:47
  198.4 16.5 %copy-start.4 = (s32[64]{0:T(128)S(1)}, s32[64]{0:T(128)}, u32[]{:S(2)}) copy-start(s32[64]{0:T(128)} %constant.155) | copy-start | bytes 772
  198.4 16.1 %collective-permute-start.10 = (f32[1152,128]{1,0:T(8,128)S(1)}, f32[1152,128]{1,0:T(8,128)S(1)}, u32[]{:S(2)}, u32[]{:S(2)}) collective-permute-start(f32[1152,128]{1,0:T(8,128)S(1)} %maximum_select_fusion.2), channel_id=1, source_target_pairs={{0,64},{16,80},{32,96},{48,112},{64,0},{80,16},{96,32},{112,48},{1... | collective-permute-start | bytes 1769480 | tf_op jit(solution)/shard_map/ppermute | solution.py:47
  214.7 26.4 %collective-permute-start.11 = (f32[2304,128]{1,0:T(8,128)S(1)}, f32[2304,128]{1,0:T(8,128)S(1)}, u32[]{:S(2)}, u32[]{:S(2)}) collective-permute-start(f32[2304,128]{1,0:T(8,128)S(1)} %maximum_select_fusion.1), channel_id=1, source_target_pairs={{0,128},{16,144},{32,160},{48,176},{64,192},{80,208},{96,224},{112... | collective-permute-start | bytes 3538952 | tf_op jit(solution)/shard_map/ppermute | solution.py:47
  257.5 3.5 copy-start.2
  384.0 1.5 collective-permute-start.12
  385.5 7.0 %collective-permute-start.13 = (f32[3,128,128]{1,2,0:T(8,128)S(1)}, f32[3,128,128]{1,2,0:T(8,128)S(1)}, u32[]{:S(2)}, u32[]{:S(2)}) collective-permute-start(f32[3,128,128]{1,2,0:T(8,128)S(1)} %fusion.77), channel_id=1, source_target_pairs={{0,32},{16,48},{32,0},{48,16},{64,96},{80,112},{96,64},{112,80},{1... | collective-permute-start | bytes 589832 | tf_op jit(solution)/shard_map/ppermute | solution.py:19
  392.6 7.7 %collective-permute-start.14 = (f32[3,128,128]{1,2,0:T(8,128)S(1)}, f32[3,128,128]{1,2,0:T(8,128)S(1)}, u32[]{:S(2)}, u32[]{:S(2)}) collective-permute-start(f32[3,128,128]{1,2,0:T(8,128)S(1)} %fusion.97), channel_id=1, source_target_pairs={{0,64},{16,80},{32,96},{48,112},{64,0},{80,16},{96,32},{112,48},{1... | collective-permute-start | bytes 589832 | tf_op jit(solution)/shard_map/ppermute | solution.py:19
  400.3 5.8 %collective-permute-start.15 = (f32[3,128,128]{1,2,0:T(8,128)S(1)}, f32[3,128,128]{1,2,0:T(8,128)S(1)}, u32[]{:S(2)}, u32[]{:S(2)}) collective-permute-start(f32[3,128,128]{1,2,0:T(8,128)S(1)} %add.101), channel_id=1, source_target_pairs={{0,128},{16,144},{32,160},{48,176},{64,192},{80,208},{96,224},{112... | collective-permute-start | bytes 589832 | tf_op jit(solution)/shard_map/ppermute | solution.py:19
  406.1 6.2 %collective-permute-start.16 = (f32[3,128,128]{1,2,0:T(8,128)S(1)}, f32[3,128,128]{1,2,0:T(8,128)S(1)}, u32[]{:S(2)}, u32[]{:S(2)}) collective-permute-start(f32[3,128,128]{1,2,0:T(8,128)S(1)} %add.102), channel_id=1, source_target_pairs={{0,1},{1,0},{2,3},{3,2},{4,5},{5,4},{6,7},{7,6},{8,9},{9,8},{10,11... | collective-permute-start | bytes 589832 | tf_op jit(solution)/shard_map/ppermute | solution.py:19
  412.3 7.3 %collective-permute-start.17 = (f32[3,128,128]{1,2,0:T(8,128)S(1)}, f32[3,128,128]{1,2,0:T(8,128)S(1)}, u32[]{:S(2)}, u32[]{:S(2)}) collective-permute-start(f32[3,128,128]{1,2,0:T(8,128)S(1)} %add.103), channel_id=1, source_target_pairs={{0,2},{1,3},{2,0},{3,1},{4,6},{5,7},{6,4},{7,5},{8,10},{9,11},{10,... | collective-permute-start | bytes 589832 | tf_op jit(solution)/shard_map/ppermute | solution.py:19
  419.6 13.4 %collective-permute-start.18 = (f32[3,128,128]{1,2,0:T(8,128)S(1)}, f32[3,128,128]{1,2,0:T(8,128)S(1)}, u32[]{:S(2)}, u32[]{:S(2)}) collective-permute-start(f32[3,128,128]{1,2,0:T(8,128)S(1)} %add.104), channel_id=1, source_target_pairs={{0,4},{1,5},{2,6},{3,7},{4,0},{5,1},{6,2},{7,3},{8,12},{9,13},{10,... | collective-permute-start | bytes 589832 | tf_op jit(solution)/shard_map/ppermute | solution.py:19
  433.0 10.7 %collective-permute-start.19 = (f32[3,128,128]{1,2,0:T(8,128)S(1)}, f32[3,128,128]{1,2,0:T(8,128)S(1)}, u32[]{:S(2)}, u32[]{:S(2)}) collective-permute-start(f32[3,128,128]{1,2,0:T(8,128)S(1)} %add.105), channel_id=1, source_target_pairs={{0,8},{1,9},{2,10},{3,11},{4,12},{5,13},{6,14},{7,15},{8,0},{9,1},... | collective-permute-start | bytes 589832 | tf_op jit(solution)/shard_map/ppermute | solution.py:19

commit v10 on v9

--- a/solution.py
+++ b/solution.py
@@ -13,9 +13,9 @@
 BLOCK = 128
 
 
-def butterfly_sum(value, axis, size):
+def butterfly_sum(value, axis, size, limit=None):
     stride = 1
-    while stride < size:
+    while stride < (limit or size):
         value = value + lax.ppermute(value, axis, [(i, i ^ stride) for i in range(size)])
         stride *= 2
     return value
@@ -31,8 +31,8 @@
     return steps
 
 
-def halving_doubling_sum(value, sizes, middle=None):
-    steps = halving_steps(sizes)
+def halving_doubling_sum(value, sizes, middle=None, extra=()):
+    steps = halving_steps(sizes) + list(extra)
     for axis, size, stride in steps:
         upper = (lax.axis_index(axis) // stride) % 2 == 1
         half = value.shape[0] // 2
@@ -69,7 +69,11 @@
         lower.extend(strip[:, col * BLOCK:(col + 1) * BLOCK] for col in range(row + 1))
     packed = jnp.concatenate(lower, axis=0)
     sizes = (("gx", lax.axis_size("gx")), ("gy", lax.axis_size("gy")))
-    packed = halving_doubling_sum(packed, sizes[:1], middle=lambda chunk: butterfly_sum(chunk, *sizes[1]))
+    axis_y, size_y = sizes[1]
+    packed = halving_doubling_sum(
+        packed, sizes[:1], middle=lambda chunk: butterfly_sum(chunk, axis_y, size_y, size_y // 2),
+        extra=((axis_y, size_y, size_y // 2),),
+    )
     blocks = packed.reshape(-1, BLOCK, BLOCK)
     both = jnp.concatenate([blocks, jnp.swapaxes(blocks, 1, 2)], axis=0)
     index = {}

time: 448 us -> 453 us (1.011)
  starting transfers between devices: 37.2 us -> 47.1 us
  waiting for transfers between devices: 229 us -> 222 us
    ppermute x12 -> x11, waiting for transfers between devices: 64.3 us -> 54 us  [butterfly_sum(): lax.ppermute(value, axis, [(i, i ^ stride) for i in range(size)])]
    ppermute x4 -> x5, starting transfers between devices: 1.41 us -> 10.2 us  [halving_doubling_sum(): other = lax.ppermute(value, axis, [(i, i ^ stride) for i in range(size)])]
    ppermute x4 -> x5, starting transfers between devices: 1.88 us -> 9.03 us  [halving_doubling_sum(): lax.ppermute(send, axis, [(i, i ^ stride) for i in range(size)])]
    ppermute x12 -> x11, starting transfers between devices: 27.3 us -> 21.3 us  [butterfly_sum(): lax.ppermute(value, axis, [(i, i ^ stride) for i in range(size)])]
    ppermute x4 -> x5, waiting for transfers between devices: 51.9 us -> 54.6 us  [halving_doubling_sum(): lax.ppermute(send, axis, [(i, i ^ stride) for i in range(size)])]
    ppermute x4 -> x5, waiting for transfers between devices: 51.7 us -> 52.9 us  [halving_doubling_sum(): other = lax.ppermute(value, axis, [(i, i ^ stride) for i in range(size)])]
  transfers between devices with their start and end apart: 21 -> 22, of which waited for: 21 -> 22; matrix products, arithmetic and copies ran while one was open for 0% -> 0% of each run, Pallas kernels for 0% -> 0%
where the time goes in v10:
time: 453 us; the launch traced here: 449 us
  waiting for transfers between devices  222 us (49%)
  other arithmetic  75.8 us (17%)
  starting transfers between devices  47.1 us (10%)
  matrix products  45.3 us (10%)
  blocking collectives  31.7 us (7%)
  local copies, waits for them, and re-layouts  25.4 us (6%)
    all_to_all x1, waiting for transfers between devices, body(): lax.all_to_all(by_row, 'gx', split_axis=0, concat_axis=0, tiled=True)  60.9 us
    ppermute x5, waiting for transfers between devices, halving_doubling_sum(): lax.ppermute(send, axis, [(i, i ^ stride) for i in range(size)])  54.6 us
    ppermute x11, waiting for transfers between devices, butterfly_sum(): lax.ppermute(value, axis, [(i, i ^ stride) for i in range(size)])  54 us
    ppermute x5, waiting for transfers between devices, halving_doubling_sum(): other = lax.ppermute(value, axis, [(i, i ^ stride) for i in range(size)])  52.9 us
    another operation x9, other arithmetic, body(): factor_low = jnp.linalg.cholesky(square)  37.2 us
    another operation x6, other arithmetic, body(): lax.linalg.triangular_solve(factor_low, wide, left_side=False, lower=True...  31.8 us
    all_to_all x1, blocking collectives, body(): lax.all_to_all(pairs, ('gx', 'gy'), split_axis=0, concat_axis=0, tiled=True)  31.7 us
    ppermute x11, starting transfers between devices, butterfly_sum(): lax.ppermute(value, axis, [(i, i ^ stride) for i in range(size)])  21.3 us
  transfers between devices with their start and end apart: 22, of which 22 were waited for; matrix products, arithmetic and copies ran while one was open for 0% of the time, Pallas kernels for 0%

profile of v10, /device:TPU:6, one launch (start us, length us, event | category | flops | bytes accessed | tf_op | source)
XLA Modules:
  0.0 449.4 jit_solution(5986421983996777983)
XLA Ops:
  0.6 6.7 %copy.62 = f32[4,64,16,256]{3,1,0,2:T(8,128)} copy(f32[4,64,16,256]{3,2,1,0:T(8,128)} %param.6) | data formatting | bytes 8388608 | tf_op args[0]
  7.3 6.6 %all-to-all-start = ((f32[16,4,64,256]{3,2,1,0:T(8,128)}), f32[16,4,64,256]{3,2,1,0:T(8,128)}, u32[]{:S(2)}, u32[]{:S(2)}) async-start(f32[16,4,64,256]{3,2,1,0:T(8,128)} %bitcast.141), calls=%async_computation | async-start | bytes 8388608 | tf_op jit(solution)/shard_map/all_to_all | solution.py:55
  14.0 60.9 %all-to-all-done = f32[16,4,64,256]{3,2,1,0:T(8,128)} async-done(((f32[16,4,64,256]{3,2,1,0:T(8,128)}), f32[16,4,64,256]{3,2,1,0:T(8,128)}, u32[]{:S(2)}, u32[]{:S(2)}) %all-to-all-start) | async-done | bytes 4194336 | tf_op jit(solution)/shard_map/all_to_all | solution.py:55
  74.8 2.5 copy.35
  77.3 1.2 fusion.50
  79.1 1.5 fusion.47
  80.6 2.3 fusion.41
  82.9 2.7 fusion.38
  85.6 3.3 fusion.32
  88.9 4.1 fusion.26
  93.0 4.4 fusion.19
  99.1 1.6 collective-permute-start
  100.7 26.8 %collective-permute-done = f32[2304,128]{1,0:T(8,128)} collective-permute-done((f32[2304,128]{1,0:T(8,128)S(1)}, f32[2304,128]{1,0:T(8,128)}, u32[]{:S(2)}, u32[]{:S(2)}) %collective-permute-start) | collective-permute-done | bytes 1179680 | tf_op jit(solution)/shard_map/ppermute | solution.py:42
  127.4 1.4 select_add_fusion
  129.1 16.2 %collective-permute-done.1 = f32[1152,128]{1,0:T(8,128)S(1)} collective-permute-done((f32[1152,128]{1,0:T(8,128)S(1)}, f32[1152,128]{1,0:T(8,128)S(1)}, u32[]{:S(2)}, u32[]{:S(2)}) %collective-permute-start.1) | collective-permute-done | bytes 589856 | tf_op jit(solution)/shard_map/ppermute | solution.py:42
  145.5 7.6 %collective-permute-done.2 = f32[576,128]{1,0:T(8,128)S(1)} collective-permute-done((f32[576,128]{1,0:T(8,128)S(1)}, f32[576,128]{1,0:T(8,128)S(1)}, u32[]{:S(2)}, u32[]{:S(2)}) %collective-permute-start.2) | collective-permute-done | bytes 294944 | tf_op jit(solution)/shard_map/ppermute | solution.py:42
  153.3 1.3 collective-permute-done.3
  154.7 7.2 %collective-permute-start.4 = (f32[144,128]{1,0:T(8,128)S(1)}, f32[144,128]{1,0:T(8,128)S(1)}, u32[]{:S(2)}, u32[]{:S(2)}) collective-permute-start(f32[144,128]{1,0:T(8,128)S(1)} %slice_select_fusion.3), channel_id=1, source_target_pairs={{0,8},{1,9},{2,10},{3,11},{4,12},{5,13},{6,14},{7,15},{8,0},{9,1},... | collective-permute-start | bytes 221192 | tf_op jit(solution)/shard_map/ppermute | solution.py:42
  161.8 2.7 collective-permute-done.4
  164.5 1.7 collective-permute-start.5
  166.2 2.8 collective-permute-done.5
  169.0 3.3 collective-permute-start.6
  172.2 2.7 collective-permute-done.6
  174.9 4.0 collective-permute-start.7
  179.0 2.3 collective-permute-done.7
  181.3 7.5 %collective-permute-start.8 = (f32[144,128]{1,0:T(8,128)S(1)}, f32[144,128]{1,0:T(8,128)S(1)}, u32[]{:S(2)}, u32[]{:S(2)}) collective-permute-start(f32[144,128]{1,0:T(8,128)S(1)} %add.104), channel_id=1, source_target_pairs={{0,8},{1,9},{2,10},{3,11},{4,12},{5,13},{6,14},{7,15},{8,0},{9,1},... | collective-permute-start | bytes 221192 | tf_op jit(solution)/shard_map/ppermute | solution.py:47
  188.8 2.3 collective-permute-done.8
  191.3 1.4 collective-permute-done.9
  193.0 8.8 %collective-permute-done.10 = f32[576,128]{1,0:T(8,128)S(1)} collective-permute-done((f32[576,128]{1,0:T(8,128)S(1)}, f32[576,128]{1,0:T(8,128)S(1)}, u32[]{:S(2)}, u32[]{:S(2)}) %collective-permute-start.10) | collective-permute-done | bytes 294944 | tf_op jit(solution)/shard_map/ppermute | solution.py:47
  202.5 15.5 %collective-permute-done.11 = f32[1152,128]{1,0:T(8,128)S(1)} collective-permute-done((f32[1152,128]{1,0:T(8,128)S(1)}, f32[1152,128]{1,0:T(8,128)S(1)}, u32[]{:S(2)}, u32[]{:S(2)}) %collective-permute-start.11) | collective-permute-done | bytes 589856 | tf_op jit(solution)/shard_map/ppermute | solution.py:47
  218.1 1.6 collective-permute-start.12
  219.7 25.0 %collective-permute-done.12 = f32[2304,128]{1,0:T(8,128)S(1)} collective-permute-done((f32[2304,128]{1,0:T(8,128)S(1)}, f32[2304,128]{1,0:T(8,128)S(1)}, u32[]{:S(2)}, u32[]{:S(2)}) %collective-permute-start.12) | collective-permute-done | bytes 1179680 | tf_op jit(solution)/shard_map/ppermute | solution.py:47
  244.9 2.0 copy.36
  246.9 4.3 pad_maximum_fusion
  251.2 5.2 %gather_fusion = f32[64,128,128]{2,1,0:T(8,128)} fusion(f32[72,128,128]{2,1,0:T(8,128)} %pad_maximum_fusion, s32[1024]{0:T(1024)S(1)} %pad_clamp_fusion), kind=kCustom, calls=%fused_computation | custom fusion | bytes 8388864 | tf_op jit(solution)/shard_map/jit(_take)/gather | solution.py:85
  256.4 4.6 %copy.37 = f32[8,128,8,128]{3,2,1,0:T(8,128)S(1)} copy(f32[8,128,8,128]{3,1,2,0:T(8,128)} %bitcast.142) | data formatting | bytes 8388608 | tf_op jit(solution)/shard_map/jit(_take)/select_n | solution.py:85
  261.0 3.5 fusion.4
  264.5 1.0 fusion.78
  265.6 11.7 %cholesky.59 = f32[128,128]{1,0:T(8,128)S(1)} custom-call(f32[128,128]{1,0:T(8,128)S(1)} %fusion.72), custom_call_target="Cholesky" | custom-call | tf_op jit(solution)/shard_map/jit(cholesky)/cholesky | solution.py:91
  278.6 10.2 %custom-call.7 = f32[1,128,128]{1,2,0:T(8,128)S(1)} custom-call(f32[1,128,128]{2,1,0:T(8,128)S(1)} %fusion.63), custom_call_target="InvertDiagBlocksLowerTriangular" | custom-call | tf_op jit(solution)/shard_map/triangular_solve/custom-call.0 | solution.py:92
  289.5 5.7 %fusion.2 = f32[1024,128]{1,0:T(8,128)S(1)} fusion(f32[1024,128]{0,1:T(8,128)S(1)} %convolution_bitcast_fusion.1, f32[128,8,8,128]{3,2,1,0:T(8,128)} %bitcast.137), kind=kOutput, calls=%fused_computation.4 | convolution fusion | flops 1610612736 | bytes 5242880 | tf_op jit(solution)/shard_map/dot_general | solution.py:89
  295.2 1.0 fusion.79
  296.3 11.7 %cholesky.70 = f32[128,128]{1,0:T(8,128)S(1)} custom-call(f32[128,128]{1,0:T(8,128)S(1)} %fusion.70), custom_call_target="Cholesky" | custom-call | tf_op jit(solution)/shard_map/jit(cholesky)/cholesky | solution.py:91
  309.4 9.8 %custom-call.8 = f32[1,128,128]{1,2,0:T(8,128)S(1)} custom-call(f32[1,128,128]{2,1,0:T(8,128)S(1)} %fusion.64), custom_call_target="InvertDiagBlocksLowerTriangular" | custom-call | tf_op jit(solution)/shard_map/triangular_solve/custom-call.0 | solution.py:92
  319.9 5.9 %fusion = f32[1024,128]{1,0:T(8,128)S(1)} fusion(f32[1024,128]{0,1:T(8,128)S(1)} %convolution_bitcast_fusion, f32[128,8,8,128]{3,2,1,0:T(8,128)} %bitcast.138), kind=kOutput, calls=%fused_computation.2 | convolution fusion | flops 1610612736 | bytes 5242880 | tf_op jit(solution)/shard_map/dot_general | solution.py:89
  325.8 1.0 fusion.80
  326.9 11.7 %cholesky.81 = f32[128,128]{1,0:T(8,128)S(1)} custom-call(f32[128,128]{1,0:T(8,128)S(1)} %fusion.68), custom_call_target="Cholesky" | custom-call | tf_op jit(solution)/shard_map/jit(cholesky)/cholesky | solution.py:91
  340.0 9.8 %custom-call.9 = f32[1,128,128]{1,2,0:T(8,128)S(1)} custom-call(f32[1,128,128]{2,1,0:T(8,128)S(1)} %fusion.65), custom_call_target="InvertDiagBlocksLowerTriangular" | custom-call | tf_op jit(solution)/shard_map/triangular_solve/custom-call.0 | solution.py:92
  350.4 4.6 %convolution_bitcast_fusion.2 = f32[4,128,256]{2,1,0:T(8,128)S(1)} fusion(f32[4,1024,256]{2,1,0:T(8,128)} %bitcast.135, f32[128,1024]{1,0:T(8,128)S(1)} %get-tuple-element.26), kind=kOutput, calls=%fused_computation.25 | convolution fusion | flops 1610612736 | bytes 5242880 | tf_op jit(solution)/shard_map/xr,sxc->src/dot_general | solution.py:93
  355.3 31.7 %all_to_all.10 = f32[256,2,256]{2,1,0:T(2,128)S(1)} all-to-all(f32[256,2,256]{2,1,0:T(2,128)S(1)} %reshape.42), channel_id=1, replica_groups=mesh['gx'=16,'gy'=16] {'gx','gy'}, dimensions={0} | all-to-all | bytes 1048576 | tf_op jit(solution)/shard_map/all_to_all | solution.py:97
  388.5 1.4 collective-permute-done.13
  390.0 1.5 collective-permute-start.14
  391.4 5.6 %collective-permute-done.14 = f32[3,128,128]{1,2,0:T(8,128)S(1)} collective-permute-done((f32[3,128,128]{1,2,0:T(8,128)S(1)}, f32[3,128,128]{1,2,0:T(8,128)S(1)}, u32[]{:S(2)}, u32[]{:S(2)}) %collective-permute-start.14) | collective-permute-done | bytes 196640 | tf_op jit(solution)/shard_map/ppermute | solution.py:19
  397.0 2.4 collective-permute-start.15
  399.4 5.3 %collective-permute-done.15 = f32[3,128,128]{1,2,0:T(8,128)S(1)} collective-permute-done((f32[3,128,128]{1,2,0:T(8,128)S(1)}, f32[3,128,128]{1,2,0:T(8,128)S(1)}, u32[]{:S(2)}, u32[]{:S(2)}) %collective-permute-start.15) | collective-permute-done | bytes 196640 | tf_op jit(solution)/shard_map/ppermute | solution.py:19
  404.7 1.1 collective-permute-start.16
  405.8 4.7 %collective-permute-done.16 = f32[3,128,128]{1,2,0:T(8,128)S(1)} collective-permute-done((f32[3,128,128]{1,2,0:T(8,128)S(1)}, f32[3,128,128]{1,2,0:T(8,128)S(1)}, u32[]{:S(2)}, u32[]{:S(2)}) %collective-permute-start.16) | collective-permute-done | bytes 196640 | tf_op jit(solution)/shard_map/ppermute | solution.py:19
  411.0 5.8 %collective-permute-done.17 = f32[3,128,128]{1,2,0:T(8,128)S(1)} collective-permute-done((f32[3,128,128]{1,2,0:T(8,128)S(1)}, f32[3,128,128]{1,2,0:T(8,128)S(1)}, u32[]{:S(2)}, u32[]{:S(2)}) %collective-permute-start.17) | collective-permute-done | bytes 196640 | tf_op jit(solution)/shard_map/ppermute | solution.py:19
  416.8 1.1 collective-permute-start.18
  417.9 6.2 %collective-permute-done.18 = f32[3,128,128]{1,2,0:T(8,128)S(1)} collective-permute-done((f32[3,128,128]{1,2,0:T(8,128)S(1)}, f32[3,128,128]{1,2,0:T(8,128)S(1)}, u32[]{:S(2)}, u32[]{:S(2)}) %collective-permute-start.18) | collective-permute-done | bytes 196640 | tf_op jit(solution)/shard_map/ppermute | solution.py:19
  424.1 3.4 collective-permute-start.19
  427.5 10.0 %collective-permute-done.19 = f32[3,128,128]{1,2,0:T(8,128)S(1)} collective-permute-done((f32[3,128,128]{1,2,0:T(8,128)S(1)}, f32[3,128,128]{1,2,0:T(8,128)S(1)}, u32[]{:S(2)}, u32[]{:S(2)}) %collective-permute-start.19) | collective-permute-done | bytes 196640 | tf_op jit(solution)/shard_map/ppermute | solution.py:19
  437.5 2.4 collective-permute-start.20
  440.9 7.3 %collective-permute-done.20 = f32[3,128,128]{1,2,0:T(8,128)S(1)} collective-permute-done((f32[3,128,128]{1,2,0:T(8,128)S(1)}, f32[3,128,128]{1,2,0:T(8,128)S(1)}, u32[]{:S(2)}, u32[]{:S(2)}) %collective-permute-start.20) | collective-permute-done | bytes 196640 | tf_op jit(solution)/shard_map/ppermute | solution.py:19
  (106 shorter events, 14.7 us)
Async XLA Ops:
  0.6 260.3 %copy-start = (f32[1024,128]{1,0:T(8,128)S(1)}, f32[1024,128]{1,0:T(8,128)}, u32[]{:S(2)}) copy-start(f32[1024,128]{1,0:T(8,128)} %param.7) | copy-start | bytes 1572868
  7.3 67.5 %all-to-all-start = ((f32[16,4,64,256]{3,2,1,0:T(8,128)}), f32[16,4,64,256]{3,2,1,0:T(8,128)}, u32[]{:S(2)}, u32[]{:S(2)}) async-start(f32[16,4,64,256]{3,2,1,0:T(8,128)} %bitcast.141), calls=%async_computation | async-start | bytes 8388608 | tf_op jit(solution)/shard_map/all_to_all | solution.py:55
  77.3 15.7 %copy-start.1 = (f32[4,16,64,256]{3,2,1,0:T(8,128)}, f32[4,16,64,256]{3,2,1,0:T(8,128)S(1)}, u32[]{:S(2)}) copy-start(f32[4,16,64,256]{3,2,1,0:T(8,128)S(1)} %copy.35) | copy-start | bytes 12582916
  98.0 1.0 copy-start.3
  99.1 28.4 %collective-permute-start = (f32[2304,128]{1,0:T(8,128)S(1)}, f32[2304,128]{1,0:T(8,128)}, u32[]{:S(2)}, u32[]{:S(2)}) collective-permute-start(f32[2304,128]{1,0:T(8,128)S(1)} %broadcast_select_fusion), channel_id=1, source_target_pairs={{0,128},{16,144},{32,160},{48,176},{64,192},{80,208},{96,224},{112... | collective-permute-start | bytes 3538952 | tf_op jit(solution)/shard_map/ppermute | solution.py:42
  128.9 16.4 %collective-permute-start.1 = (f32[1152,128]{1,0:T(8,128)S(1)}, f32[1152,128]{1,0:T(8,128)S(1)}, u32[]{:S(2)}, u32[]{:S(2)}) collective-permute-start(f32[1152,128]{1,0:T(8,128)S(1)} %slice_select_fusion), channel_id=1, source_target_pairs={{0,64},{16,80},{32,96},{48,112},{64,0},{80,16},{96,32},{112,48},{1... | collective-permute-start | bytes 1769480 | tf_op jit(solution)/shard_map/ppermute | solution.py:42
  145.4 7.7 %collective-permute-start.2 = (f32[576,128]{1,0:T(8,128)S(1)}, f32[576,128]{1,0:T(8,128)S(1)}, u32[]{:S(2)}, u32[]{:S(2)}) collective-permute-start(f32[576,128]{1,0:T(8,128)S(1)} %slice_select_fusion.1), channel_id=1, source_target_pairs={{0,32},{16,48},{32,0},{48,16},{64,96},{80,112},{96,64},{112,80},{1... | collective-permute-start | bytes 884744 | tf_op jit(solution)/shard_map/ppermute | solution.py:42
  153.2 1.5 collective-permute-start.3
  154.7 9.8 %collective-permute-start.4 = (f32[144,128]{1,0:T(8,128)S(1)}, f32[144,128]{1,0:T(8,128)S(1)}, u32[]{:S(2)}, u32[]{:S(2)}) collective-permute-start(f32[144,128]{1,0:T(8,128)S(1)} %slice_select_fusion.3), channel_id=1, source_target_pairs={{0,8},{1,9},{2,10},{3,11},{4,12},{5,13},{6,14},{7,15},{8,0},{9,1},... | collective-permute-start | bytes 221192 | tf_op jit(solution)/shard_map/ppermute | solution.py:42
  164.5 4.4 collective-permute-start.5
  169.0 5.9 %collective-permute-start.6 = (f32[144,128]{1,0:T(8,128)S(1)}, f32[144,128]{1,0:T(8,128)S(1)}, u32[]{:S(2)}, u32[]{:S(2)}) collective-permute-start(f32[144,128]{1,0:T(8,128)S(1)} %add.102), channel_id=1, source_target_pairs={{0,2},{1,3},{2,0},{3,1},{4,6},{5,7},{6,4},{7,5},{8,10},{9,11},{10,... | collective-permute-start | bytes 221192 | tf_op jit(solution)/shard_map/ppermute | solution.py:19
  174.9 6.4 %collective-permute-start.7 = (f32[144,128]{1,0:T(8,128)S(1)}, f32[144,128]{1,0:T(8,128)S(1)}, u32[]{:S(2)}, u32[]{:S(2)}) collective-permute-start(f32[144,128]{1,0:T(8,128)S(1)} %add.103), channel_id=1, source_target_pairs={{0,4},{1,5},{2,6},{3,7},{4,0},{5,1},{6,2},{7,3},{8,12},{9,13},{10,... | collective-permute-start | bytes 221192 | tf_op jit(solution)/shard_map/ppermute | solution.py:19
  181.3 9.8 %collective-permute-start.8 = (f32[144,128]{1,0:T(8,128)S(1)}, f32[144,128]{1,0:T(8,128)S(1)}, u32[]{:S(2)}, u32[]{:S(2)}) collective-permute-start(f32[144,128]{1,0:T(8,128)S(1)} %add.104), channel_id=1, source_target_pairs={{0,8},{1,9},{2,10},{3,11},{4,12},{5,13},{6,14},{7,15},{8,0},{9,1},... | collective-permute-start | bytes 221192 | tf_op jit(solution)/shard_map/ppermute | solution.py:47
  191.2 1.5 collective-permute-start.9
  192.7 9.1 %collective-permute-start.10 = (f32[576,128]{1,0:T(8,128)S(1)}, f32[576,128]{1,0:T(8,128)S(1)}, u32[]{:S(2)}, u32[]{:S(2)}) collective-permute-start(f32[576,128]{1,0:T(8,128)S(1)} %maximum_select_fusion.3), channel_id=1, source_target_pairs={{0,32},{16,48},{32,0},{48,16},{64,96},{80,112},{96,64},{112,80},{1... | collective-permute-start | bytes 884744 | tf_op jit(solution)/shard_map/ppermute | solution.py:47
  201.9 17.8 %copy-start.4 = (s32[64]{0:T(128)S(1)}, s32[64]{0:T(128)}, u32[]{:S(2)}) copy-start(s32[64]{0:T(128)} %constant.172) | copy-start | bytes 772
  201.9 16.1 %collective-permute-start.11 = (f32[1152,128]{1,0:T(8,128)S(1)}, f32[1152,128]{1,0:T(8,128)S(1)}, u32[]{:S(2)}, u32[]{:S(2)}) collective-permute-start(f32[1152,128]{1,0:T(8,128)S(1)} %maximum_select_fusion.2), channel_id=1, source_target_pairs={{0,64},{16,80},{32,96},{48,112},{64,0},{80,16},{96,32},{112,48},{1... | collective-permute-start | bytes 1769480 | tf_op jit(solution)/shard_map/ppermute | solution.py:47
  218.1 26.6 %collective-permute-start.12 = (f32[2304,128]{1,0:T(8,128)S(1)}, f32[2304,128]{1,0:T(8,128)S(1)}, u32[]{:S(2)}, u32[]{:S(2)}) collective-permute-start(f32[2304,128]{1,0:T(8,128)S(1)} %maximum_select_fusion.1), channel_id=1, source_target_pairs={{0,128},{16,144},{32,160},{48,176},{64,192},{80,208},{96,224},{112... | collective-permute-start | bytes 3538952 | tf_op jit(solution)/shard_map/ppermute | solution.py:47
  261.0 3.5 copy-start.2
  388.4 1.5 collective-permute-start.13
  390.0 7.0 %collective-permute-start.14 = (f32[3,128,128]{1,2,0:T(8,128)S(1)}, f32[3,128,128]{1,2,0:T(8,128)S(1)}, u32[]{:S(2)}, u32[]{:S(2)}) collective-permute-start(f32[3,128,128]{1,2,0:T(8,128)S(1)} %fusion.77), channel_id=1, source_target_pairs={{0,32},{16,48},{32,0},{48,16},{64,96},{80,112},{96,64},{112,80},{1... | collective-permute-start | bytes 589832 | tf_op jit(solution)/shard_map/ppermute | solution.py:19
  397.0 7.7 %collective-permute-start.15 = (f32[3,128,128]{1,2,0:T(8,128)S(1)}, f32[3,128,128]{1,2,0:T(8,128)S(1)}, u32[]{:S(2)}, u32[]{:S(2)}) collective-permute-start(f32[3,128,128]{1,2,0:T(8,128)S(1)} %fusion.97), channel_id=1, source_target_pairs={{0,64},{16,80},{32,96},{48,112},{64,0},{80,16},{96,32},{112,48},{1... | collective-permute-start | bytes 589832 | tf_op jit(solution)/shard_map/ppermute | solution.py:19
  404.7 5.8 %collective-permute-start.16 = (f32[3,128,128]{1,2,0:T(8,128)S(1)}, f32[3,128,128]{1,2,0:T(8,128)S(1)}, u32[]{:S(2)}, u32[]{:S(2)}) collective-permute-start(f32[3,128,128]{1,2,0:T(8,128)S(1)} %add.107), channel_id=1, source_target_pairs={{0,128},{16,144},{32,160},{48,176},{64,192},{80,208},{96,224},{112... | collective-permute-start | bytes 589832 | tf_op jit(solution)/shard_map/ppermute | solution.py:19
  410.5 6.2 %collective-permute-start.17 = (f32[3,128,128]{1,2,0:T(8,128)S(1)}, f32[3,128,128]{1,2,0:T(8,128)S(1)}, u32[]{:S(2)}, u32[]{:S(2)}) collective-permute-start(f32[3,128,128]{1,2,0:T(8,128)S(1)} %add.108), channel_id=1, source_target_pairs={{0,1},{1,0},{2,3},{3,2},{4,5},{5,4},{6,7},{7,6},{8,9},{9,8},{10,11... | collective-permute-start | bytes 589832 | tf_op jit(solution)/shard_map/ppermute | solution.py:19
  416.8 7.3 %collective-permute-start.18 = (f32[3,128,128]{1,2,0:T(8,128)S(1)}, f32[3,128,128]{1,2,0:T(8,128)S(1)}, u32[]{:S(2)}, u32[]{:S(2)}) collective-permute-start(f32[3,128,128]{1,2,0:T(8,128)S(1)} %add.109), channel_id=1, source_target_pairs={{0,2},{1,3},{2,0},{3,1},{4,6},{5,7},{6,4},{7,5},{8,10},{9,11},{10,... | collective-permute-start | bytes 589832 | tf_op jit(solution)/shard_map/ppermute | solution.py:19
  424.1 13.4 %collective-permute-start.19 = (f32[3,128,128]{1,2,0:T(8,128)S(1)}, f32[3,128,128]{1,2,0:T(8,128)S(1)}, u32[]{:S(2)}, u32[]{:S(2)}) collective-permute-start(f32[3,128,128]{1,2,0:T(8,128)S(1)} %add.110), channel_id=1, source_target_pairs={{0,4},{1,5},{2,6},{3,7},{4,0},{5,1},{6,2},{7,3},{8,12},{9,13},{10,... | collective-permute-start | bytes 589832 | tf_op jit(solution)/shard_map/ppermute | solution.py:19
  437.5 10.7 %collective-permute-start.20 = (f32[3,128,128]{1,2,0:T(8,128)S(1)}, f32[3,128,128]{1,2,0:T(8,128)S(1)}, u32[]{:S(2)}, u32[]{:S(2)}) collective-permute-start(f32[3,128,128]{1,2,0:T(8,128)S(1)} %add.111), channel_id=1, source_target_pairs={{0,8},{1,9},{2,10},{3,11},{4,12},{5,13},{6,14},{7,15},{8,0},{9,1},... | collective-permute-start | bytes 589832 | tf_op jit(solution)/shard_map/ppermute | solution.py:19
